TPU v7x, 128 devices: a whole 4x4x4 slice. The times are simulated.
128 devices in a mesh: req: 16 (over x, y), vocab: 8 (over z, core).
Axes of the slice: x: 4, y: 4, z: 4, core: 2. Of those that a mesh axis runs over, the one named last changes fastest.
Arguments:
- hidden: bfloat16 [64, 128, 2048], P('req'), may hold values from -1000 to 1000
- gain: float32 [2048], replicated, may hold values from 0.5 to 1.5
- embedding: bfloat16 [76800, 2048], P('vocab', 'req'), may hold values from -16 to 16
- targets: int32 [64, 128], P('req'), may hold values from 0 to 76799
- span_start: int32 [64], P('req'), may hold values from 0 to 127, as said below
- span_len: int32 [64], P('req'), may hold values from 1 to 128
- deal_order: int32 [64], replicated, may hold values from 0 to 63, as said below
Outputs:
- logprob: float32 [64, 128], P('req')
- entropy: float32 [64, 128], P('req')
Inputs may be any that keep to these rules, and one draw needn't show every extreme that they name: deal_order is a permutation of the requests; the span lengths of the 4 requests dealt to one group add up to at most 224, exactly 224 for some group. span_start + span_len <= 128 for every request.
All inputs are finite; a program needn't handle non-finite values.
Results may differ from a plain program's by a relative error of at most 0.0029.
Values may be sent and summed in bfloat16 or wider, within the bound.
No kernel may reach another device: no remote copies, remote signals or barrier semaphores. Data moves between devices by JAX's collectives and lax.ppermute only.
A program may use at most 128 MiB of HBM per device.

v0:
```python
import jax
import jax.numpy as jnp
from jax import lax
from jax.sharding import PartitionSpec as P

CAP = 224


eps = 1e-06


def compact_plan(row_base, lengths, capacity):
    offsets = jnp.cumsum(lengths) - lengths
    counter = jnp.arange(capacity, dtype=jnp.int32)
    member = jnp.sum((counter[:, None] >= offsets[None, :]).astype(jnp.int32), axis=1) - 1
    member_hot = (member[:, None] == jnp.arange(lengths.shape[0], dtype=jnp.int32)[None, :]).astype(
        jnp.int32
    )
    row_index = jnp.sum(member_hot * (row_base - offsets)[None, :], axis=1) + counter
    in_span = counter < jnp.sum(lengths)
    return (row_index, in_span)


def normalize(rows, gain):
    wide_rows = rows.astype(jnp.float32)
    scale = lax.rsqrt(jnp.mean(wide_rows * wide_rows, axis=1, keepdims=True) + eps)
    return (wide_rows * scale * gain).astype(jnp.bfloat16)


def shards(hidden, gain, embedding, targets, span_start, span_len, deal_order):
    per_dev = hidden.shape[0]
    slot_len = hidden.shape[1]
    width = hidden.shape[2]
    total = deal_order.shape[0]
    voc_local = embedding.shape[0]
    here = lax.axis_index("req")
    positions = jnp.arange(total, dtype=jnp.int32)
    source_of = jnp.sum(
        jnp.where(deal_order[None, :] == positions[:, None], positions[None, :], 0), axis=1
    )
    all_starts, all_lengths = (
        lax.all_gather(span_start, "req", axis=0, tiled=True),
        lax.all_gather(span_len, "req", axis=0, tiled=True),
    )
    my_slots = here * per_dev + jnp.arange(per_dev, dtype=jnp.int32)
    members = jnp.sum(
        jnp.where(my_slots[:, None] == positions[None, :], source_of[None, :], 0), axis=1
    )
    member_hot = members[:, None] == positions[None, :]
    lengths = jnp.sum(jnp.where(member_hot, all_lengths[None, :], 0), axis=1)
    starts = jnp.sum(jnp.where(member_hot, all_starts[None, :], 0), axis=1)
    row_base = jnp.arange(per_dev, dtype=jnp.int32) * slot_len + starts
    row_index, in_span = compact_plan(row_base, lengths, CAP)
    safe_index = jnp.where(in_span, row_index, 0)
    spread_rows, spread_marks = (
        lax.all_to_all(hidden, "req", split_axis=1, concat_axis=0, tiled=True),
        lax.all_to_all(targets, "req", split_axis=1, concat_axis=0, tiled=True),
    )
    dealt_rows = jnp.take(spread_rows, source_of, axis=0)
    dealt_marks = jnp.take(spread_marks, source_of, axis=0)
    home_rows, home_marks = (
        lax.all_to_all(dealt_rows, "req", split_axis=0, concat_axis=1, tiled=True),
        lax.all_to_all(dealt_marks, "req", split_axis=0, concat_axis=1, tiled=True),
    )
    rows = jnp.take(home_rows.reshape(per_dev * slot_len, width), safe_index, axis=0)
    target_ids = jnp.where(
        in_span, jnp.take(home_marks.reshape(per_dev * slot_len), safe_index), -1
    )
    normed = normalize(rows, gain)
    logits = lax.dot_general(
        normed,
        lax.all_gather(embedding, "req", axis=1, tiled=True),
        (((1,), (1,)), ((), ())),
        preferred_element_type=jnp.float32,
    )
    local_top = jnp.max(logits, axis=1)
    shifted = logits - local_top[:, None]
    weights = jnp.exp(shifted)
    local_mass = jnp.sum(weights, axis=1)
    local_spread = jnp.sum(weights * shifted, axis=1)
    local_ids = target_ids - lax.axis_index("vocab") * voc_local
    local_target = jnp.sum(
        jnp.where(
            jnp.arange(voc_local, dtype=jnp.int32)[None, :] == local_ids[:, None], logits, 0.0
        ),
        axis=1,
    )
    row_top = lax.pmax(local_top, "vocab")
    factor = jnp.exp(local_top - row_top)
    row_mass, row_spread, row_target = lax.psum(
        (
            factor * local_mass,
            factor * (local_spread + (local_top - row_top) * local_mass),
            local_target,
        ),
        "vocab",
    )
    log_mass = jnp.log(row_mass)
    compact_logprob = jnp.where(in_span, row_target - row_top - log_mass, 0.0)
    compact_entropy = jnp.where(in_span, log_mass - row_spread / row_mass, 0.0)
    spot = jnp.where(in_span, row_index, per_dev * slot_len)
    dealt_logprob = (
        jnp.zeros((per_dev * slot_len,), jnp.float32)
        .at[spot]
        .set(compact_logprob, mode="drop")
        .reshape(per_dev, slot_len)
    )
    dealt_entropy = (
        jnp.zeros((per_dev * slot_len,), jnp.float32)
        .at[spot]
        .set(compact_entropy, mode="drop")
        .reshape(per_dev, slot_len)
    )
    wide_logprob, wide_entropy = (
        lax.all_to_all(dealt_logprob, "req", split_axis=1, concat_axis=0, tiled=True),
        lax.all_to_all(dealt_entropy, "req", split_axis=1, concat_axis=0, tiled=True),
    )
    home_logprob = jnp.take(wide_logprob, deal_order, axis=0)
    home_entropy = jnp.take(wide_entropy, deal_order, axis=0)
    out_logprob, out_entropy = (
        lax.all_to_all(home_logprob, "req", split_axis=0, concat_axis=1, tiled=True),
        lax.all_to_all(home_entropy, "req", split_axis=0, concat_axis=1, tiled=True),
    )
    return (out_logprob, out_entropy)


def solution(mesh):
    in_specs = (
        P("req", None, None),
        P(),
        P("vocab", "req"),
        P("req", None),
        P("req"),
        P("req"),
        P(),
    )
    out_specs = (P("req", None), P("req", None))
    return jax.shard_map(shards, mesh=mesh, in_specs=in_specs, out_specs=out_specs, check_vma=False)
```

profile of v0, /device:TPU:1, one launch (start us, length us, event | category | flops | bytes accessed | tf_op | source)
XLA Modules:
  0.0 397.6 jit_solution(16751751695467223779)
XLA Ops:
  7.2 0.7 all-gather.2.cloned.1.call-update
  8.0 0.6 copy.39
  8.6 7.6 %all-to-all-start = ((s32[4,16,8]{2,0,1:T(4,128)}), s32[4,16,8]{2,0,1:T(4,128)S(1)}, u32[]{:S(2)}, u32[]{:S(2)}) async-start(s32[4,16,8]{2,0,1:T(4,128)} %copy.39), calls=%async_computation | async-start | bytes 65536 | tf_op jit(solution)/shard_map/all_to_all | solution.py:57
  16.2 2.9 copy.41
  19.1 3.5 all-to-all-done
  22.7 3.8 all-to-all-start.2
  26.7 0.6 gather_fusion
  27.3 0.7 broadcast_select_fusion.5
  28.0 37.4 %all-to-all-done.2 = bf16[4,128,2048]{2,0,1:T(4,128)(2,1)S(1)} async-done(((bf16[4,128,2048]{2,0,1:T(4,128)(2,1)}), bf16[4,128,2048]{2,0,1:T(4,128)(2,1)S(1)}, u32[]{:S(2)}, u32[]{:S(2)}) %all-to-all-start.2) | async-done | bytes 2097184 | tf_op jit(solution)/shard_map/all_to_all | solution.py:56
  65.4 5.4 %all-to-all-start.1 = ((s32[16,4,8]{2,1,0:T(4,128)}), s32[16,4,8]{2,1,0:T(4,128)S(1)}, u32[]{:S(2)}, u32[]{:S(2)}) async-start(s32[16,4,8]{2,1,0:T(4,128)} %broadcast_select_fusion.5), calls=%async_computation.1 | async-start | bytes 65536 | tf_op jit(solution)/shard_map/all_to_all | solution.py:63
  70.8 1.2 copy.50
  71.9 1.4 copy.43
  73.4 2.3 gather_fusion.2
  75.6 1.6 broadcast_select_fusion
  77.2 0.2 all-to-all-done.1
  77.4 6.6 %all-to-all-start.3 = ((bf16[64,8,2048]{2,1,0:T(8,128)(2,1)}), bf16[64,8,2048]{2,1,0:T(8,128)(2,1)S(1)}, u32[]{:S(2)}, u32[]{:S(2)}) async-start(bf16[64,8,2048]{2,1,0:T(8,128)(2,1)} %broadcast_select_fusion), calls=%async_computation.3 | async-start | bytes 4194304 | tf_op jit(solution)/shard_map/all_to_all | solution.py:62
  84.0 0.6 dynamic-slice
  85.7 33.3 %all-reduce.2 = (s32[64]{0:T(128)S(1)}, s32[64]{0:T(128)S(1)}) all-reduce(s32[64]{0:T(128)S(1)} %dynamic-update-slice, s32[64]{0:T(128)S(1)} %dynamic-update-slice.1), channel_id=1, replica_groups=mesh['req'=16,'vocab'=8] {'req'}, use_global_device_ids=true, to_apply=%add | all-reduce | flops 128 | bytes 1024
  119.3 0.7 select_reduce_fusion.4
  120.4 0.7 compare_select_fusion.1
  121.2 1.9 gather_fusion.1
  123.1 0.7 select_subtract_fusion
  123.8 1.3 copy-done
  125.1 1.7 copy.44
  126.8 1.3 gather_fusion.3
  128.1 0.4 fusion.1
  128.5 162.8 %all-gather.2.cloned.1.call-done = bf16[9600,2048]{1,0:T(8,128)(2,1)} async-done(((bf16[9600,128]{1,0:T(8,128)(2,1)}), bf16[9600,2048]{1,0:T(8,128)(2,1)}) %all-gather.2.cloned.1.call-update) | async-done | bytes 39321616 | tf_op jit(solution)/shard_map/all_gather | solution.py:72
  291.3 21.5 %fusion.14 = (f32[224]{0:T(256)S(1)}, f32[224,9600]{1,0:T(8,128)}) fusion(bf16[9600,2048]{1,0:T(8,128)(2,1)} %all-gather.2.cloned.1.call-done, f32[2048]{0:T(1024)S(1)} %copy-done.3, f32[224]{0:T(256)S(1)} %add_rsqrt_fusion, bf16[224,2048]{1,0:T(8,128)(2,1)S(1)} %gather_fusion.3, pred[224]{0:T(512)(128)(4,1)S(1)} %get-tuple-element.15), kind=kOutput, calls=%fused_computation.73 | convolution fusion | flops 8812482560 | bytes 48850912 | tf_op jit(solution)/shard_map/dot_general | solution.py:70
  312.8 14.1 %pmax.7 = f32[224]{0:T(256)S(1)} all-reduce(f32[224]{0:T(256)S(1)} %get-tuple-element.26), channel_id=1, replica_groups=mesh['req'=16,'vocab'=8] {'vocab'}, use_global_device_ids=true, to_apply=%region_12.13 | all-reduce | flops 224 | bytes 1792 | tf_op jit(solution)/shard_map/pmax | solution.py:88
  326.9 5.3 %fusion = (f32[224]{0:T(256)S(1)}, f32[224]{0:T(256)S(1)}, f32[224]{0:T(256)S(1)}) fusion(f32[224,9600]{1,0:T(8,128)} %get-tuple-element.27, f32[224]{0:T(256)S(1)} %get-tuple-element.26, s32[224]{0:T(256)S(1)} %get-tuple-element.14), kind=kLoop, calls=%fused_computation.10 | loop fusion | flops 15052128 | bytes 8606080 | tf_op jit(solution)/shard_map/reduce_sum | solution.py:80
  332.2 13.3 %all-reduce.3 = (f32[224]{0:T(256)S(1)}, f32[224]{0:T(256)S(1)}, f32[224]{0:T(256)S(1)}) all-reduce(f32[224]{0:T(256)S(1)} %get-tuple-element.5, f32[224]{0:T(256)S(1)} %get-tuple-element.19, f32[224]{0:T(256)S(1)} %get-tuple-element.18), channel_id=1, replica_groups=mesh['req'=16,'vocab'=8] {'vocab'}, use_global_device_ids=true, to_apply=%region_10.11 | all-reduce | flops 672 | bytes 5376 | tf_op jit(solution)/shard_map/psum | solution.py:90
  345.5 0.7 subtract_select_fusion
  346.2 1.3 scatter_custom_fusion.1
  347.6 0.6 copy.47
  348.2 4.7 %all-to-all-start.6 = ((f32[4,16,8]{2,0,1:T(4,128)}), f32[4,16,8]{2,0,1:T(4,128)S(1)}, u32[]{:S(2)}, u32[]{:S(2)}) async-start(f32[4,16,8]{2,0,1:T(4,128)} %copy.47), calls=%async_computation.6 | async-start | bytes 65536 | tf_op jit(solution)/shard_map/all_to_all | solution.py:116
  352.9 1.3 scatter_custom_fusion
  354.3 0.6 copy.45
  354.9 4.5 %all-to-all-done.6 = f32[4,16,8]{2,0,1:T(4,128)S(1)} async-done(((f32[4,16,8]{2,0,1:T(4,128)}), f32[4,16,8]{2,0,1:T(4,128)S(1)}, u32[]{:S(2)}, u32[]{:S(2)}) %all-to-all-start.6) | async-done | bytes 2080 | tf_op jit(solution)/shard_map/all_to_all | solution.py:116
  359.4 3.5 all-to-all-start.4
  362.8 0.6 gather_fusion.5
  363.4 5.8 %all-to-all-done.4 = f32[4,16,8]{2,0,1:T(4,128)S(1)} async-done(((f32[4,16,8]{2,0,1:T(4,128)}), f32[4,16,8]{2,0,1:T(4,128)S(1)}, u32[]{:S(2)}, u32[]{:S(2)}) %all-to-all-start.4) | async-done | bytes 2080 | tf_op jit(solution)/shard_map/all_to_all | solution.py:115
  369.2 0.6 gather_fusion.4
  369.8 0.7 broadcast_select_fusion.3
  370.5 9.6 %all_to_all.141 = f32[16,4,8]{2,1,0:T(4,128)S(1)} all-to-all(f32[16,4,8]{2,1,0:T(4,128)S(1)} %bitcast.49), channel_id=1, replica_groups=mesh['req'=16,'vocab'=8] {'req'}, dimensions={0} | all-to-all | bytes 4096 | tf_op jit(solution)/shard_map/all_to_all | solution.py:121
  380.1 3.5 all-to-all-start.7
  383.6 0.7 all_to_all.124
  384.3 5.7 %all-to-all-done.7 = f32[16,4,8]{2,1,0:T(4,128)S(1)} async-done(((f32[16,4,8]{2,1,0:T(4,128)}), f32[16,4,8]{2,1,0:T(4,128)S(1)}, u32[]{:S(2)}, u32[]{:S(2)}) %all-to-all-start.7) | async-done | bytes 2080 | tf_op jit(solution)/shard_map/all_to_all | solution.py:122
  390.0 0.7 all_to_all.132
  (47 shorter events, 1.7 us)
Async XLA Ops:
  7.2 0.8 copy-start.2
  7.2 9.0 %copy-start.1 = (bf16[4,128,2048]{2,1,0:T(8,128)(2,1)S(1)}, bf16[4,128,2048]{2,1,0:T(8,128)(2,1)}, u32[]{:S(2)}) copy-start(bf16[4,128,2048]{2,1,0:T(8,128)(2,1)} %param.9) | copy-start | bytes 6291460
  7.2 284.1 %all-gather.2.cloned.1.call-start = ((), (), s32[]{:S(2)}) async-start(), calls=%async_computation.8 | async-start | bytes 41779200 | tf_op jit(solution)/shard_map/all_gather | solution.py:72
  8.6 14.1 %all-to-all-start = ((s32[4,16,8]{2,0,1:T(4,128)}), s32[4,16,8]{2,0,1:T(4,128)S(1)}, u32[]{:S(2)}, u32[]{:S(2)}) async-start(s32[4,16,8]{2,0,1:T(4,128)} %copy.39), calls=%async_computation | async-start | bytes 65536 | tf_op jit(solution)/shard_map/all_to_all | solution.py:57
  19.1 7.3 %copy-start.6 = (s32[64]{0:T(128)S(1)}, s32[64]{0:T(128)}, u32[]{:S(2)}) copy-start(s32[64]{0:T(128)} %param.15) | copy-start | bytes 772
  22.7 42.7 %all-to-all-start.2 = ((bf16[4,128,2048]{2,0,1:T(4,128)(2,1)}), bf16[4,128,2048]{2,0,1:T(4,128)(2,1)S(1)}, u32[]{:S(2)}, u32[]{:S(2)}) async-start(bf16[4,128,2048]{2,0,1:T(4,128)(2,1)} %copy.41), calls=%async_computation.2 | async-start | bytes 4194304 | tf_op jit(solution)/shard_map/all_to_all | solution.py:56
  65.4 12.1 %all-to-all-start.1 = ((s32[16,4,8]{2,1,0:T(4,128)}), s32[16,4,8]{2,1,0:T(4,128)S(1)}, u32[]{:S(2)}, u32[]{:S(2)}) async-start(s32[16,4,8]{2,1,0:T(4,128)} %broadcast_select_fusion.5), calls=%async_computation.1 | async-start | bytes 65536 | tf_op jit(solution)/shard_map/all_to_all | solution.py:63
  77.2 6.8 %copy-start.7 = (u32[128]{0:T(128)S(1)}, u32[128]{0:T(128)}, u32[]{:S(2)}) copy-start(u32[128]{0:T(128)} %constant.108) | copy-start | bytes 1540
  77.2 8.1 %copy-start.4 = (s32[4]{0:T(128)S(1)}, s32[4]{0:T(128)}, u32[]{:S(2)}) copy-start(s32[4]{0:T(128)} %param.14) | copy-start | bytes 52
  77.2 8.3 %copy-start.5 = (s32[4]{0:T(128)S(1)}, s32[4]{0:T(128)}, u32[]{:S(2)}) copy-start(s32[4]{0:T(128)} %param.13) | copy-start | bytes 52
  77.4 46.3 %all-to-all-start.3 = ((bf16[64,8,2048]{2,1,0:T(8,128)(2,1)}), bf16[64,8,2048]{2,1,0:T(8,128)(2,1)S(1)}, u32[]{:S(2)}, u32[]{:S(2)}) async-start(bf16[64,8,2048]{2,1,0:T(8,128)(2,1)} %broadcast_select_fusion), calls=%async_computation.3 | async-start | bytes 4194304 | tf_op jit(solution)/shard_map/all_to_all | solution.py:62
  123.8 1.3 copy-start
  126.8 164.5 %copy-start.3 = (f32[2048]{0:T(1024)S(1)}, f32[2048]{0:T(1024)}, u32[]{:S(2)}) copy-start(f32[2048]{0:T(1024)} %param.10) | copy-start | bytes 24580
  348.2 11.2 %all-to-all-start.6 = ((f32[4,16,8]{2,0,1:T(4,128)}), f32[4,16,8]{2,0,1:T(4,128)S(1)}, u32[]{:S(2)}, u32[]{:S(2)}) async-start(f32[4,16,8]{2,0,1:T(4,128)} %copy.47), calls=%async_computation.6 | async-start | bytes 65536 | tf_op jit(solution)/shard_map/all_to_all | solution.py:116
  359.4 9.9 %all-to-all-start.4 = ((f32[4,16,8]{2,0,1:T(4,128)}), f32[4,16,8]{2,0,1:T(4,128)S(1)}, u32[]{:S(2)}, u32[]{:S(2)}) async-start(f32[4,16,8]{2,0,1:T(4,128)} %copy.45), calls=%async_computation.4 | async-start | bytes 65536 | tf_op jit(solution)/shard_map/all_to_all | solution.py:115
  380.1 9.9 %all-to-all-start.7 = ((f32[16,4,8]{2,1,0:T(4,128)}), f32[16,4,8]{2,1,0:T(4,128)S(1)}, u32[]{:S(2)}, u32[]{:S(2)}) async-start(f32[16,4,8]{2,1,0:T(4,128)} %bitcast.24), calls=%async_computation.7 | async-start | bytes 65536 | tf_op jit(solution)/shard_map/all_to_all | solution.py:122
Sparse Core Ops, SparseCore 0:
  10.1 281.1 all-gather.1
where the time goes:
time: 402 us; the launch traced here: 398 us
  waiting for transfers between devices  221 us (55%)
  blocking collectives  70.3 us (17%)
  starting transfers between devices  34.9 us (9%)
  local copies, waits for them, and re-layouts  23.1 us (6%)
  matrix products  21.5 us (5%)
  between operations  15 us (4%)
  other arithmetic  12 us (3%)
    all_gather x1, waiting for transfers between devices, shards(): lax.all_gather(embedding, 'req', axis=1, tiled=True)  163 us
    all_to_all x1, waiting for transfers between devices, shards(): lax.all_to_all(hidden, 'req', split_axis=1, concat_axis=0, tiled=True)  37.4 us
    unnamed x1, blocking collectives  33.3 us
    dot_general x1, matrix products, shards(): lax.dot_general(normed, lax.all_gather(embedding, 'req', axis=1, tiled=Tr...  21.5 us
    pmax x1, blocking collectives, shards(): row_top = lax.pmax(local_top, 'vocab')  14.1 us
    psum x1, blocking collectives, shards(): lax.psum((factor * local_mass, factor * (local_spread + (local_top - row_...  13.3 us
    all_to_all x1, blocking collectives, shards(): lax.all_to_all(home_logprob, 'req', split_axis=0, concat_axis=1, tiled=True)  9.6 us
  transfers between devices with their start and end apart: 8, of which 7 were waited for; matrix products, arithmetic and copies ran while one was open for 6% of the time, Pallas kernels for 0%

commit v1 on v0

v1 whole, which is shorter than its diff:
```python
import functools

import jax
import jax.numpy as jnp
from jax import lax
from jax.sharding import PartitionSpec as P

CAP = 224


eps = 1e-06


def compact_plan(row_base, lengths, capacity):
    offsets = jnp.cumsum(lengths) - lengths
    counter = jnp.arange(capacity, dtype=jnp.int32)
    member = jnp.sum((counter[:, None] >= offsets[None, :]).astype(jnp.int32), axis=1) - 1
    member_hot = (member[:, None] == jnp.arange(lengths.shape[0], dtype=jnp.int32)[None, :]).astype(
        jnp.int32
    )
    row_index = jnp.sum(member_hot * (row_base - offsets)[None, :], axis=1) + counter
    in_span = counter < jnp.sum(lengths)
    return (row_index, in_span)


def normalize(rows, gain):
    wide_rows = rows.astype(jnp.float32)
    scale = lax.rsqrt(jnp.mean(wide_rows * wide_rows, axis=-1, keepdims=True) + eps)
    return (wide_rows * scale * gain).astype(jnp.bfloat16)


def shards(n_voc, hidden, gain, embedding, targets, span_start, span_len, deal_order):
    per_dev = hidden.shape[0]
    slot_len = hidden.shape[1]
    width = hidden.shape[2]
    total = deal_order.shape[0]
    n_req = total // per_dev
    voc_local = embedding.shape[0]
    piece = voc_local // n_req
    half = width // 2
    here = lax.axis_index("req")
    vhere = lax.axis_index("vocab")
    core = vhere % 2
    positions = jnp.arange(total, dtype=jnp.int32)
    source_of = jnp.sum(
        jnp.where(deal_order[None, :] == positions[:, None], positions[None, :], 0), axis=1
    )

    emb_piece = lax.all_to_all(embedding, "req", split_axis=0, concat_axis=1, tiled=True)

    meta = jnp.concatenate([targets, span_start[:, None], span_len[:, None]], axis=1)
    meta_all = lax.all_gather(meta, "req", axis=0, tiled=True)
    all_targets = meta_all[:, :slot_len]
    all_starts = meta_all[:, slot_len]
    all_lengths = meta_all[:, slot_len + 1]

    normed_home = normalize(hidden, gain)
    my_half = lax.dynamic_slice_in_dim(normed_home, core * half, half, axis=2)
    spread_rows = lax.all_to_all(my_half, "req", split_axis=1, concat_axis=0, tiled=True)
    dealt_rows = jnp.take(spread_rows, source_of, axis=0)
    home_rows = lax.all_to_all(dealt_rows, "req", split_axis=0, concat_axis=1, tiled=True)

    my_slots = here * per_dev + jnp.arange(per_dev, dtype=jnp.int32)
    members = jnp.take(source_of, my_slots)
    lengths = jnp.take(all_lengths, members)
    starts = jnp.take(all_starts, members)
    row_base = jnp.arange(per_dev, dtype=jnp.int32) * slot_len + starts
    row_index, in_span = compact_plan(row_base, lengths, CAP)
    safe_index = jnp.where(in_span, row_index, 0)
    compact_half = jnp.take(home_rows.reshape(per_dev * slot_len, half), safe_index, axis=0)

    rows_mine = lax.all_gather(compact_half, "req", axis=0, tiled=True)
    pairs = [(2 * k + j, 2 * k + 1 - j) for k in range(n_voc // 2) for j in range(2)]
    rows_other = lax.ppermute(rows_mine, "vocab", pairs)

    emb_mine = lax.dynamic_slice_in_dim(emb_piece, core * half, half, axis=1)
    emb_other = lax.dynamic_slice_in_dim(emb_piece, (1 - core) * half, half, axis=1)
    dims = (((1,), (1,)), ((), ()))
    logits = lax.dot_general(rows_mine, emb_mine, dims, preferred_element_type=jnp.float32)
    logits = logits + lax.dot_general(rows_other, emb_other, dims, preferred_element_type=jnp.float32)

    dealt_members = source_of.reshape(n_req, per_dev)
    dealt_lengths = jnp.take(all_lengths, dealt_members)
    dealt_base = dealt_members * slot_len + jnp.take(all_starts, dealt_members)
    all_index, all_in = jax.vmap(lambda b, l: compact_plan(b, l, CAP))(dealt_base, dealt_lengths)
    all_index = jnp.where(all_in, all_index, 0).reshape(-1)
    target_ids = jnp.take(all_targets.reshape(-1), all_index)

    local_top = jnp.max(logits, axis=1)
    shifted = logits - local_top[:, None]
    weights = jnp.exp(shifted)
    local_mass = jnp.sum(weights, axis=1)
    local_spread = jnp.sum(weights * shifted, axis=1)
    local_ids = target_ids - (vhere * voc_local + here * piece)
    local_target = jnp.sum(
        jnp.where(jnp.arange(piece, dtype=jnp.int32)[None, :] == local_ids[:, None], logits, 0.0),
        axis=1,
    )
    both = ("req", "vocab")
    row_top = lax.pmax(local_top, both)
    factor = jnp.exp(local_top - row_top)
    row_mass, row_spread, row_target = lax.psum(
        (
            factor * local_mass,
            factor * (local_spread + (local_top - row_top) * local_mass),
            local_target,
        ),
        both,
    )
    log_mass = jnp.log(row_mass)
    all_logprob = row_target - row_top - log_mass
    all_entropy = log_mass - row_spread / row_mass

    offsets = (jnp.cumsum(dealt_lengths, axis=1) - dealt_lengths).reshape(-1)
    my_reqs = here * per_dev + jnp.arange(per_dev, dtype=jnp.int32)
    my_deal = jnp.take(deal_order, my_reqs)
    my_start = jnp.take(all_starts, my_reqs)
    my_len = jnp.take(all_lengths, my_reqs)
    pos = jnp.arange(slot_len, dtype=jnp.int32)[None, :]
    inside = (pos >= my_start[:, None]) & (pos < (my_start + my_len)[:, None])
    flat = (my_deal // per_dev)[:, None] * CAP + jnp.take(offsets, my_deal)[:, None] + pos - my_start[:, None]
    flat = jnp.where(inside, flat, 0)
    out_logprob = jnp.where(inside, jnp.take(all_logprob, flat), 0.0)
    out_entropy = jnp.where(inside, jnp.take(all_entropy, flat), 0.0)
    return (out_logprob, out_entropy)


def solution(mesh):
    in_specs = (
        P("req", None, None),
        P(),
        P("vocab", "req"),
        P("req", None),
        P("req"),
        P("req"),
        P(),
    )
    out_specs = (P("req", None), P("req", None))
    body = functools.partial(shards, mesh.shape["vocab"])
    return jax.shard_map(body, mesh=mesh, in_specs=in_specs, out_specs=out_specs, check_vma=False)
```

time: 402 us -> 353 us (0.88); the launches traced: 398 us -> 353 us
  waiting for transfers between devices: 221 us -> 90 us
  blocking collectives: 70.3 us -> 156 us
  starting transfers between devices: 34.9 us -> 17.8 us
  local copies, waits for them, and re-layouts: 23.1 us -> 34.9 us
  other arithmetic: 12 us -> 22.5 us
  matrix products: 21.5 us -> 17.1 us
    all_gather x1, waiting for transfers between devices: 163 us -> 70.5 us  [shards(): rows_mine = lax.all_gather(compact_half, 'req', axis=0, tiled=True)]
    pmax x1, blocking collectives: 14.1 us -> 66.4 us  [shards(): row_top = lax.pmax(local_top, both)]
    psum x1, blocking collectives: 13.3 us -> 64.3 us  [shards(): lax.psum((factor * local_mass, factor * (local_spread + (local_top - row_...]
    all_to_all x6 -> x2, waiting for transfers between devices: 57.1 us -> 9.28 us  [the longest x1 9.28 us: shards(): lax.all_to_all(embedding, 'req', split_axis=0, concat_axis=1, tiled=True)]
    unnamed x1 -> x0, blocking collectives: 33.3 us -> none
    gather x5 -> x15, local copies, waits for them, and re-layouts: 4.99 us -> 32.4 us  [the longest x1 18.9 us: shards(): target_ids = jnp.take(all_targets.reshape(-1), all_index)]
    all_gather x0 -> x1, blocking collectives: none -> 25.3 us  [shards(): meta_all = lax.all_gather(meta, 'req', axis=0, tiled=True)]
    all_to_all x6 -> x2, starting transfers between devices: 28.3 us -> 12.6 us  [the longest x1 7.57 us: shards(): lax.all_to_all(my_half, 'req', split_axis=1, concat_axis=0, tiled=True)]
  transfers between devices with their start and end apart: 8 -> 5, of which waited for: 7 -> 3; matrix products, arithmetic and copies ran while one was open for 6% -> 10% of each run, Pallas kernels for 0% -> 0%
where the time goes in v1:
time: 353 us
  blocking collectives  156 us (44%)
  waiting for transfers between devices  90 us (25%)
  local copies, waits for them, and re-layouts  34.9 us (10%)
  other arithmetic  22.5 us (6%)
  starting transfers between devices  17.8 us (5%)
  matrix products  17.1 us (5%)
  between operations  14.4 us (4%)
    all_gather x1, waiting for transfers between devices, shards(): rows_mine = lax.all_gather(compact_half, 'req', axis=0, tiled=True)  70.5 us
    pmax x1, blocking collectives, shards(): row_top = lax.pmax(local_top, both)  66.4 us
    psum x1, blocking collectives, shards(): lax.psum((factor * local_mass, factor * (local_spread + (local_top - row_...  64.3 us
    all_gather x1, blocking collectives, shards(): meta_all = lax.all_gather(meta, 'req', axis=0, tiled=True)  25.3 us
    gather x1, local copies, waits for them, and re-layouts, shards(): target_ids = jnp.take(all_targets.reshape(-1), all_index)  18.9 us
    all_to_all x1, waiting for transfers between devices, shards(): lax.all_to_all(dealt_rows, 'req', split_axis=0, concat_axis=1, tiled=True)  10.3 us
    dot_general x1, matrix products, shards(): lax.dot_general(rows_other, emb_other, dims, preferred_element_type=jnp.f...  10.2 us
    all_to_all x1, waiting for transfers between devices, shards(): lax.all_to_all(embedding, 'req', split_axis=0, concat_axis=1, tiled=True)  9.28 us
  transfers between devices with their start and end apart: 5, of which 3 were waited for; matrix products, arithmetic and copies ran while one was open for 10% of the time, Pallas kernels for 0%

profile of v1, /device:TPU:1, one launch (start us, length us, event | category | flops | bytes accessed | tf_op | source)
XLA Modules:
  0.0 352.8 jit_solution(17315659532683955452)
XLA Ops:
  7.2 3.2 multiply_reduce_fusion
  10.4 5.1 %copy_convert_fusion = f32[4,128,2048]{2,0,1:T(4,128)} fusion(bf16[4,128,2048]{2,1,0:T(8,128)(2,1)} %param.13), kind=kLoop, calls=%fused_computation.25 | loop fusion | flops 1048576 | bytes 6291456 | tf_op jit(solution)/shard_map/convert_element_type | solution.py:27
  15.6 3.1 fusion.2
  18.7 7.6 %all-to-all-start = ((bf16[4,128,1024]{2,0,1:T(4,128)(2,1)}), bf16[4,128,1024]{2,0,1:T(4,128)(2,1)S(1)}, u32[]{:S(2)}, u32[]{:S(2)}) async-start(bf16[4,128,1024]{2,0,1:T(4,128)(2,1)} %fusion.2), calls=%async_computation | async-start | bytes 2097152 | tf_op jit(solution)/shard_map/all_to_all | solution.py:59
  26.3 0.1 select_reduce_fusion.2
  26.4 0.1 copy.58
  26.5 0.1 copy.59
  26.6 0.6 gather_fusion.10
  27.3 0.6 gather_fusion.7
  28.0 25.3 %all-gather = s32[16,4,130]{2,1,0:T(4,128)S(1)} all-gather(s32[1,4,130]{2,1,0:T(4,128)S(1)} %add_bitcast_fusion), channel_id=1, replica_groups=mesh['req'=16,'vocab'=8] {'req'}, dimensions={0}, use_global_device_ids=true | all-gather | bytes 35360 | tf_op jit(solution)/shard_map/all_gather | solution.py:52
  53.6 0.6 gather_fusion.8
  54.2 0.6 gather_fusion.9
  54.9 0.6 fusion.18
  55.5 0.2 reduce-window.9
  55.7 0.3 copy.80
  56.1 0.1 copy.68
  56.2 0.6 gather_fusion.1
  56.8 1.2 broadcast_select_fusion
  57.9 4.4 %all-to-all-start.1 = ((bf16[64,8,1024]{2,1,0:T(8,128)(2,1)}), bf16[64,8,1024]{2,1,0:T(8,128)(2,1)S(1)}, u32[]{:S(2)}, u32[]{:S(2)}) async-start(bf16[64,8,1024]{2,1,0:T(8,128)(2,1)} %broadcast_select_fusion), calls=%async_computation.1 | async-start | bytes 2097152 | tf_op jit(solution)/shard_map/all_to_all | solution.py:61
  62.5 0.7 compare_select_fusion.3
  63.2 0.7 compare_and_fusion.5
  63.9 10.3 %all-to-all-done.1 = bf16[64,8,1024]{2,1,0:T(8,128)(2,1)S(1)} async-done(((bf16[64,8,1024]{2,1,0:T(8,128)(2,1)}), bf16[64,8,1024]{2,1,0:T(8,128)(2,1)S(1)}, u32[]{:S(2)}, u32[]{:S(2)}) %all-to-all-start.1) | async-done | bytes 1048608 | tf_op jit(solution)/shard_map/all_to_all | solution.py:61
  74.2 1.1 gather_fusion.2
  75.3 0.9 broadcast_select_fusion.1
  76.2 70.5 %all-gather.3.cloned.1.call-done = bf16[3584,1024]{1,0:T(8,128)(2,1)} async-done(((bf16[224,1024]{1,0:T(8,128)(2,1)}), bf16[3584,1024]{1,0:T(8,128)(2,1)}) %all-gather.3.cloned.1.call-update) | async-done | bytes 7340048 | tf_op jit(solution)/shard_map/all_gather | solution.py:72
  146.7 0.8 collective-permute-start
  147.5 5.0 %all-to-all-start.2 = ((bf16[16,600,128]{2,1,0:T(8,128)(2,1)}), bf16[16,600,128]{2,1,0:T(8,128)(2,1)S(1)}, u32[]{:S(2)}, u32[]{:S(2)}) async-start(bf16[16,600,128]{2,1,0:T(8,128)(2,1)} %bitcast.59), calls=%async_computation.2 | async-start | bytes 4915200 | tf_op jit(solution)/shard_map/all_to_all | solution.py:49
  152.6 0.1 reshape.370
  152.7 0.8 gather_fusion.5
  153.5 0.8 gather_fusion.6
  154.4 0.1 fusion.19
  154.6 0.2 reduce_window_sum.20
  154.7 0.6 gather_fusion.4
  155.4 0.6 gather_fusion.3
  156.0 0.1 reshape.236
  156.5 0.1 select_n.167
  156.7 0.6 gather_fusion.11
  157.4 18.9 %gather_fusion = s32[3584]{0:T(1024)S(1)} fusion(s32[8192]{0:T(1024)S(1)} %slice_bitcast_fusion, s32[4096]{0:T(1024)S(1)} %pad_clamp_fusion), kind=kCustom, calls=%fused_computation.11 | custom fusion | bytes 43008 | tf_op jit(solution)/shard_map/jit(_take)/gather | solution.py:87
  176.4 9.3 %all-to-all-done.2 = bf16[16,600,128]{2,1,0:T(8,128)(2,1)S(1)} async-done(((bf16[16,600,128]{2,1,0:T(8,128)(2,1)}), bf16[16,600,128]{2,1,0:T(8,128)(2,1)S(1)}, u32[]{:S(2)}, u32[]{:S(2)}) %all-to-all-start.2) | async-done | bytes 2457632 | tf_op jit(solution)/shard_map/all_to_all | solution.py:49
  185.7 0.3 copy_bitcast_fusion
  186.0 7.0 %fusion.4 = f32[3584,600]{0,1:T(8,128)S(1)} fusion(bf16[3584,1024]{1,0:T(8,128)(2,1)} %all-gather.3.cloned.1.call-done, bf16[600,2048]{1,0:T(8,128)(2,1)S(1)} %copy_bitcast_fusion, s32[]{:T(128)S(6)} %select_n.174), kind=kOutput, calls=%fused_computation.27 | convolution fusion | flops 4404019200 | bytes 17170436 | tf_op jit(solution)/shard_map/dot_general | solution.py:79
  193.0 10.2 %fusion.21 = (f32[3584]{0:T(1024)S(1)}, f32[3584,600]{0,1:T(8,128)}) fusion(f32[3584,600]{0,1:T(8,128)S(1)} %fusion.4, bf16[3584,1024]{1,0:T(8,128)(2,1)} %collective-permute-done, bf16[600,2048]{1,0:T(8,128)(2,1)S(1)} %copy_bitcast_fusion, s32[]{:T(128)S(6)} %select_n.180), kind=kOutput, calls=%fused_computation.113 | convolution fusion | flops 4408316416 | bytes 25786372 | tf_op jit(solution)/shard_map/dot_general | solution.py:80
  203.2 66.4 %pmax.7 = f32[3584]{0:T(1024)S(1)} all-reduce(f32[3584]{0:T(1024)S(1)} %get-tuple-element.29), channel_id=1, replica_groups=mesh['req'=16,'vocab'=8] {'req','vocab'}, use_global_device_ids=true, to_apply=%region_13.16 | all-reduce | flops 3584 | bytes 28672 | tf_op jit(solution)/shard_map/pmax | solution.py:100
  269.6 5.1 %fusion = (f32[3584]{0:T(1024)S(1)}, f32[3584]{0:T(1024)S(1)}, f32[3584]{0:T(1024)S(1)}) fusion(f32[3584,600]{0,1:T(8,128)} %get-tuple-element.30, f32[3584]{0:T(1024)S(1)} %get-tuple-element.29, s32[3584]{0:T(1024)S(1)} %select_subtract_fusion), kind=kLoop, calls=%fused_computation.16 | loop fusion | flops 15042048 | bytes 8673280 | tf_op jit(solution)/shard_map/reduce_sum | solution.py:93
  274.7 64.3 %all-reduce = (f32[3584]{0:T(1024)S(1)}, f32[3584]{0:T(1024)S(1)}, f32[3584]{0:T(1024)S(1)}) all-reduce(f32[3584]{0:T(1024)S(1)} %get-tuple-element.7, f32[3584]{0:T(1024)S(1)} %get-tuple-element.20, f32[3584]{0:T(1024)S(1)} %get-tuple-element.19), channel_id=1, replica_groups=mesh['req'=16,'vocab'=8] {'req','vocab'}, use_global_device_ids=true, to_apply=%region_11.14 | all-reduce | flops 10752 | bytes 86016 | tf_op jit(solution)/shard_map/psum | solution.py:102
  339.0 3.1 gather_fusion.13
  342.2 3.1 gather_fusion.12
  345.3 0.7 fusion.8
  (58 shorter events, 1.7 us)
Async XLA Ops:
  7.2 8.4 %copy-start.2 = (f32[2048]{0:T(1024)S(1)}, f32[2048]{0:T(1024)}, u32[]{:S(2)}) copy-start(f32[2048]{0:T(1024)} %param.14) | copy-start | bytes 24580
  15.5 10.8 %copy-start = (s32[64]{0:T(128)S(1)}, s32[64]{0:T(128)}, u32[]{:S(2)}) copy-start(s32[64]{0:T(128)} %param.19) | copy-start | bytes 772
  15.5 10.9 %copy-start.3 = (s32[4]{0:T(128)S(1)}, s32[4]{0:T(128)}, u32[]{:S(2)}) copy-start(s32[4]{0:T(128)} %param.17) | copy-start | bytes 52
  15.5 11.0 %copy-start.4 = (s32[4]{0:T(128)S(1)}, s32[4]{0:T(128)}, u32[]{:S(2)}) copy-start(s32[4]{0:T(128)} %param.18) | copy-start | bytes 52
  15.5 12.4 %copy-start.1 = (s32[4,128]{1,0:T(4,128)S(1)}, s32[4,128]{1,0:T(4,128)}, u32[]{:S(2)}) copy-start(s32[4,128]{1,0:T(4,128)} %param.16) | copy-start | bytes 6148
  18.7 37.0 %all-to-all-start = ((bf16[4,128,1024]{2,0,1:T(4,128)(2,1)}), bf16[4,128,1024]{2,0,1:T(4,128)(2,1)S(1)}, u32[]{:S(2)}, u32[]{:S(2)}) async-start(bf16[4,128,1024]{2,0,1:T(4,128)(2,1)} %fusion.2), calls=%async_computation | async-start | bytes 2097152 | tf_op jit(solution)/shard_map/all_to_all | solution.py:59
  57.9 16.2 %all-to-all-start.1 = ((bf16[64,8,1024]{2,1,0:T(8,128)(2,1)}), bf16[64,8,1024]{2,1,0:T(8,128)(2,1)S(1)}, u32[]{:S(2)}, u32[]{:S(2)}) async-start(bf16[64,8,1024]{2,1,0:T(8,128)(2,1)} %broadcast_select_fusion), calls=%async_computation.1 | async-start | bytes 2097152 | tf_op jit(solution)/shard_map/all_to_all | solution.py:61
  62.3 84.4 %all-gather.3.cloned.1.call-start = ((), (), s32[]{:S(2)}) async-start(), calls=%async_computation.3 | async-start | bytes 7798784 | tf_op jit(solution)/shard_map/all_gather | solution.py:72
  146.7 46.3 %collective-permute-start = (bf16[3584,1024]{1,0:T(8,128)(2,1)}, bf16[3584,1024]{1,0:T(8,128)(2,1)}, u32[]{:S(2)}, u32[]{:S(2)}) collective-permute-start(bf16[3584,1024]{1,0:T(8,128)(2,1)} %all-gather.3.cloned.1.call-done), channel_id=1, source_target_pairs={{0,1},{1,0},{2,3},{3,2},{4,5},{5,4},{6,7},{7,6},{8,9},{9,8},{10,11... | collective-permute-start | bytes 22020104 | tf_op jit(solution)/shard_map/ppermute | solution.py:74
  147.5 38.2 %all-to-all-start.2 = ((bf16[16,600,128]{2,1,0:T(8,128)(2,1)}), bf16[16,600,128]{2,1,0:T(8,128)(2,1)S(1)}, u32[]{:S(2)}, u32[]{:S(2)}) async-start(bf16[16,600,128]{2,1,0:T(8,128)(2,1)} %bitcast.59), calls=%async_computation.2 | async-start | bytes 4915200 | tf_op jit(solution)/shard_map/all_to_all | solution.py:49
Sparse Core Ops, SparseCore 0:
  76.3 70.2 all-gather.2

commit v2 on v1

--- a/solution.py
+++ b/solution.py
@@ -49,7 +49,7 @@
     emb_piece = lax.all_to_all(embedding, "req", split_axis=0, concat_axis=1, tiled=True)
 
     meta = jnp.concatenate([targets, span_start[:, None], span_len[:, None]], axis=1)
-    meta_all = lax.all_gather(meta, "req", axis=0, tiled=True)
+    meta_all = lax.all_gather(meta.astype(jnp.float32), "req", axis=0, tiled=True).astype(jnp.int32)
     all_targets = meta_all[:, :slot_len]
     all_starts = meta_all[:, slot_len]
     all_lengths = meta_all[:, slot_len + 1]
@@ -81,10 +81,16 @@
 
     dealt_members = source_of.reshape(n_req, per_dev)
     dealt_lengths = jnp.take(all_lengths, dealt_members)
-    dealt_base = dealt_members * slot_len + jnp.take(all_starts, dealt_members)
-    all_index, all_in = jax.vmap(lambda b, l: compact_plan(b, l, CAP))(dealt_base, dealt_lengths)
-    all_index = jnp.where(all_in, all_index, 0).reshape(-1)
-    target_ids = jnp.take(all_targets.reshape(-1), all_index)
+    dealt_offsets = jnp.cumsum(dealt_lengths, axis=1) - dealt_lengths
+    dealt_starts = jnp.take(all_starts, dealt_members)
+    padded_targets = jnp.pad(jnp.take(all_targets, source_of, axis=0), ((0, 0), (CAP, CAP)))
+    window_at = (dealt_starts - dealt_offsets + CAP).reshape(-1)
+    windows = jax.vmap(lambda row, at: lax.dynamic_slice_in_dim(row, at, CAP))(padded_targets, window_at)
+    counter = jnp.arange(CAP, dtype=jnp.int32)
+    in_member = (counter[None, None, :] >= dealt_offsets[:, :, None]) & (
+        counter[None, None, :] < (dealt_offsets + dealt_lengths)[:, :, None]
+    )
+    target_ids = jnp.sum(jnp.where(in_member, windows.reshape(n_req, per_dev, CAP), 0), axis=1).reshape(-1)
 
     local_top = jnp.max(logits, axis=1)
     shifted = logits - local_top[:, None]
@@ -96,32 +102,36 @@
         jnp.where(jnp.arange(piece, dtype=jnp.int32)[None, :] == local_ids[:, None], logits, 0.0),
         axis=1,
     )
-    both = ("req", "vocab")
-    row_top = lax.pmax(local_top, both)
-    factor = jnp.exp(local_top - row_top)
-    row_mass, row_spread, row_target = lax.psum(
-        (
-            factor * local_mass,
-            factor * (local_spread + (local_top - row_top) * local_mass),
-            local_target,
-        ),
-        both,
-    )
+
+    def merge(stats):
+        top_each, mass_each, spread_each, target_each = stats[:, 0], stats[:, 1], stats[:, 2], stats[:, 3]
+        top = jnp.max(top_each, axis=0)
+        gap = top_each - top[None, :]
+        factor = jnp.exp(gap)
+        mass = jnp.sum(factor * mass_each, axis=0)
+        spread = jnp.sum(factor * (spread_each + gap * mass_each), axis=0)
+        return jnp.stack([top, mass, spread, jnp.sum(target_each, axis=0)])
+
+    local_stats = jnp.stack([local_top, local_mass, local_spread, local_target]).reshape(4, n_req, CAP)
+    by_req = lax.all_to_all(local_stats.transpose(1, 0, 2), "req", split_axis=0, concat_axis=0, tiled=True)
+    group_stats = merge(lax.all_gather(merge(by_req), "vocab", axis=0))
+    row_top, row_mass, row_spread, row_target = group_stats[0], group_stats[1], group_stats[2], group_stats[3]
     log_mass = jnp.log(row_mass)
-    all_logprob = row_target - row_top - log_mass
-    all_entropy = log_mass - row_spread / row_mass
+    group_out = jnp.stack([row_target - row_top - log_mass, log_mass - row_spread / row_mass])
+    all_out = lax.all_gather(group_out, "req", axis=1, tiled=True)
 
-    offsets = (jnp.cumsum(dealt_lengths, axis=1) - dealt_lengths).reshape(-1)
+    offsets = dealt_offsets.reshape(-1)
     my_reqs = here * per_dev + jnp.arange(per_dev, dtype=jnp.int32)
     my_deal = jnp.take(deal_order, my_reqs)
     my_start = jnp.take(all_starts, my_reqs)
     my_len = jnp.take(all_lengths, my_reqs)
     pos = jnp.arange(slot_len, dtype=jnp.int32)[None, :]
     inside = (pos >= my_start[:, None]) & (pos < (my_start + my_len)[:, None])
-    flat = (my_deal // per_dev)[:, None] * CAP + jnp.take(offsets, my_deal)[:, None] + pos - my_start[:, None]
-    flat = jnp.where(inside, flat, 0)
-    out_logprob = jnp.where(inside, jnp.take(all_logprob, flat), 0.0)
-    out_entropy = jnp.where(inside, jnp.take(all_entropy, flat), 0.0)
+    padded_out = jnp.pad(all_out, ((0, 0), (slot_len, slot_len)))
+    out_at = (my_deal // per_dev) * CAP + jnp.take(offsets, my_deal) - my_start + slot_len
+    picked = jax.vmap(lambda at: lax.dynamic_slice_in_dim(padded_out, at, slot_len, axis=1))(out_at)
+    out_logprob = jnp.where(inside, picked[:, 0], 0.0)
+    out_entropy = jnp.where(inside, picked[:, 1], 0.0)
     return (out_logprob, out_entropy)
 
 

time: 353 us -> 387 us (1.096); the launches traced: 353 us -> 380 us
  local copies, waits for them, and re-layouts: 34.9 us -> 151 us
  blocking collectives: 156 us -> 56.1 us
  waiting for transfers between devices: 90 us -> 96.2 us
    gather x6 -> x276, local copies, waits for them, and re-layouts: 26.6 us -> 142 us  [the longest x1 18.9 us: shards(): target_ids = jnp.take(all_targets.reshape(-1), all_index)]
    pmax x1 -> x0, blocking collectives: 66.4 us -> none  [shards(): row_top = lax.pmax(local_top, both)]
    psum x1 -> x0, blocking collectives: 64.3 us -> none  [shards(): lax.psum((factor * local_mass, factor * (local_spread + (local_top - row_...]
    all_gather x1 -> x3, blocking collectives: 25.3 us -> 56.1 us  [the longest x1 25.3 us: shards(): lax.all_gather(meta.astype(jnp.float32), 'req', axis=0, tiled=True)]
    all_to_all x1, waiting for transfers between devices: 9.28 us -> 0.01 us  [shards(): lax.all_to_all(embedding, 'req', split_axis=0, concat_axis=1, tiled=True)]
    all_gather x1, waiting for transfers between devices: 70.5 us -> 79.5 us  [shards(): rows_mine = lax.all_gather(compact_half, 'req', axis=0, tiled=True)]
    all_to_all x0 -> x1, waiting for transfers between devices: none -> 6.47 us  [shards(): lax.all_to_all(local_stats.transpose(1, 0, 2), 'req', split_axis=0, conca...]
    all_to_all x0 -> x1, starting transfers between devices: none -> 4.98 us  [shards(): lax.all_to_all(local_stats.transpose(1, 0, 2), 'req', split_axis=0, conca...]
  transfers between devices with their start and end apart: 5 -> 6, of which waited for: 3 -> 3; matrix products, arithmetic and copies ran while one was open for 10% -> 40% of each run, Pallas kernels for 0% -> 0%
where the time goes in v2:
time: 387 us; the launch traced here: 380 us
  local copies, waits for them, and re-layouts  151 us (39%)
  waiting for transfers between devices  96.2 us (25%)
  blocking collectives  56.1 us (14%)
  other arithmetic  23.1 us (6%)
  starting transfers between devices  21.5 us (6%)
  matrix products  17 us (4%)
  between operations  14.5 us (4%)
    gather x272, local copies, waits for them, and re-layouts  140 us
    all_gather x1, waiting for transfers between devices, shards(): rows_mine = lax.all_gather(compact_half, 'req', axis=0, tiled=True)  79.5 us
    all_gather x1, blocking collectives, shards(): lax.all_gather(meta.astype(jnp.float32), 'req', axis=0, tiled=True)  25.3 us
    all_gather x1, blocking collectives, shards(): all_out = lax.all_gather(group_out, 'req', axis=1, tiled=True)  16.1 us
    all_gather x1, blocking collectives, shards(): group_stats = merge(lax.all_gather(merge(by_req), 'vocab', axis=0))  14.7 us
    all_to_all x1, waiting for transfers between devices, shards(): lax.all_to_all(dealt_rows, 'req', split_axis=0, concat_axis=1, tiled=True)  10.3 us
    dot_general x1, matrix products, shards(): lax.dot_general(rows_other, emb_other, dims, preferred_element_type=jnp.f...  10 us
  transfers between devices with their start and end apart: 6, of which 3 were waited for; matrix products, arithmetic and copies ran while one was open for 40% of the time, Pallas kernels for 0%

profile of v2, /device:TPU:1, one launch (start us, length us, event | category | flops | bytes accessed | tf_op | source)
XLA Modules:
  0.0 380.4 jit_solution(6498885822886947417)
XLA Ops:
  7.2 3.2 multiply_reduce_fusion
  10.4 5.1 %copy_convert_fusion = f32[4,128,2048]{2,0,1:T(4,128)} fusion(bf16[4,128,2048]{2,1,0:T(8,128)(2,1)} %param.11), kind=kLoop, calls=%fused_computation.26 | loop fusion | flops 1048576 | bytes 6291456 | tf_op jit(solution)/shard_map/convert_element_type | solution.py:27
  15.6 3.1 fusion.2
  18.7 7.6 %all-to-all-start = ((bf16[4,128,1024]{2,0,1:T(4,128)(2,1)}), bf16[4,128,1024]{2,0,1:T(4,128)(2,1)S(1)}, u32[]{:S(2)}, u32[]{:S(2)}) async-start(bf16[4,128,1024]{2,0,1:T(4,128)(2,1)} %fusion.2), calls=%async_computation | async-start | bytes 2097152 | tf_op jit(solution)/shard_map/all_to_all | solution.py:59
  28.0 25.3 %all-gather.1 = f32[16,4,130]{2,1,0:T(4,128)S(1)} all-gather(f32[1,4,130]{2,1,0:T(4,128)S(1)} %fusion.16), channel_id=1, replica_groups=mesh['req'=16,'vocab'=8] {'req'}, dimensions={0}, use_global_device_ids=true | all-gather | bytes 35360 | tf_op jit(solution)/shard_map/all_gather | solution.py:52
  57.9 4.4 %all-to-all-start.1 = ((bf16[64,8,1024]{2,1,0:T(8,128)(2,1)}), bf16[64,8,1024]{2,1,0:T(8,128)(2,1)S(1)}, u32[]{:S(2)}, u32[]{:S(2)}) async-start(bf16[64,8,1024]{2,1,0:T(8,128)(2,1)} %broadcast_select_fusion), calls=%async_computation.1 | async-start | bytes 2097152 | tf_op jit(solution)/shard_map/all_to_all | solution.py:61
  63.8 10.3 %all-to-all-done.1 = bf16[64,8,1024]{2,1,0:T(8,128)(2,1)S(1)} async-done(((bf16[64,8,1024]{2,1,0:T(8,128)(2,1)}), bf16[64,8,1024]{2,1,0:T(8,128)(2,1)S(1)}, u32[]{:S(2)}, u32[]{:S(2)}) %all-to-all-start.1) | async-done | bytes 1048608 | tf_op jit(solution)/shard_map/all_to_all | solution.py:61
  76.2 3.7 all-to-all-start.2
  83.0 79.5 %all-gather.6.cloned.1.call-done = bf16[3584,1024]{1,0:T(8,128)(2,1)} async-done(((bf16[224,1024]{1,0:T(8,128)(2,1)}), bf16[3584,1024]{1,0:T(8,128)(2,1)}) %all-gather.6.cloned.1.call-update) | async-done | bytes 7340048 | tf_op jit(solution)/shard_map/all_gather | solution.py:72
  163.3 135.9 %while.2 = (s32[]{:T(128)}, s32[64,576]{1,0:T(8,128)S(1)}, s32[64,2]{0,1:T(2,128)S(1)}, s32[64,224]{1,0:T(8,128)S(1)}, s32[]{:T(128)}, /*index=5*/s32[]{:T(128)}) while((s32[]{:T(128)}, s32[64,576]{1,0:T(8,128)S(1)}, s32[64,2]{0,1:T(2,128)S(1)}, s32[64,224]{1,0:T(8,128)S(1)}, s32[]{:T(128)}, /*index=5*/s32[]{:T(128)}) %tuple.61), condition=%wide.while_cond, body=%wide.while_body.sunk | while | flops 2 | bytes 3705 | solution.py:88
  163.9 1.4 dynamic-slice.16
  166.0 1.4 dynamic-slice.16
  168.2 1.4 dynamic-slice.16
  170.3 1.4 dynamic-slice.16
  172.4 1.4 dynamic-slice.16
  174.5 1.4 dynamic-slice.16
  176.7 1.4 dynamic-slice.16
  178.8 1.4 dynamic-slice.16
  180.9 1.4 dynamic-slice.16
  183.0 1.4 dynamic-slice.16
  185.2 1.4 dynamic-slice.16
  187.3 1.4 dynamic-slice.16
  189.4 1.4 dynamic-slice.16
  191.5 1.4 dynamic-slice.16
  193.7 1.4 dynamic-slice.16
  195.8 1.4 dynamic-slice.16
  197.9 1.4 dynamic-slice.16
  200.0 1.4 dynamic-slice.16
  202.2 1.4 dynamic-slice.16
  210.6 1.4 dynamic-slice.16
  221.3 1.4 dynamic-slice.16
  229.8 1.4 dynamic-slice.16
  231.9 1.4 dynamic-slice.16
  240.4 1.4 dynamic-slice.16
  251.0 1.4 dynamic-slice.16
  261.6 1.4 dynamic-slice.16
  270.1 1.4 dynamic-slice.16
  272.2 1.4 dynamic-slice.16
  280.7 1.4 dynamic-slice.16
  291.3 1.4 dynamic-slice.16
  301.8 6.9 %fusion.4 = f32[3584,600]{0,1:T(8,128)S(1)} fusion(bf16[3584,1024]{1,0:T(8,128)(2,1)} %all-gather.6.cloned.1.call-done, bf16[600,2048]{1,0:T(8,128)(2,1)S(1)} %copy_bitcast_fusion, s32[]{:T(128)S(6)} %select_n.130), kind=kOutput, calls=%fused_computation.28 | convolution fusion | flops 4404019200 | bytes 17170436 | tf_op jit(solution)/shard_map/dot_general | solution.py:79
  308.7 10.0 %fusion.29 = (f32[3584]{0:T(1024)S(1)}, f32[3584,600]{0,1:T(8,128)}) fusion(f32[3584,600]{0,1:T(8,128)S(1)} %fusion.4, bf16[3584,1024]{1,0:T(8,128)(2,1)} %collective-permute-done, bf16[600,2048]{1,0:T(8,128)(2,1)S(1)} %copy_bitcast_fusion, s32[]{:T(128)S(6)} %select_n.136), kind=kOutput, calls=%fused_computation.130 | convolution fusion | flops 4408316416 | bytes 25786372 | tf_op jit(solution)/shard_map/dot_general | solution.py:80
  318.9 5.1 %exponential_reduce_fusion = (f32[3584]{0:T(1024)S(1)}, f32[3584]{0:T(1024)S(1)}, f32[3584]{0:T(1024)S(1)}) fusion(f32[3584,600]{0,1:T(8,128)} %get-tuple-element.77, f32[3584]{0:T(1024)S(1)} %get-tuple-element.76, s32[3584]{0:T(1024)S(1)} %sub.110), kind=kLoop, calls=%fused_computation.16 | loop fusion | flops 15042048 | bytes 8673280 | tf_op jit(solution)/shard_map/reduce_sum | solution.py:98
  324.9 5.0 %all-to-all-start.3 = ((f32[16,4,224]{2,1,0:T(4,128)}), f32[16,4,224]{2,1,0:T(4,128)S(1)}, u32[]{:S(2)}, u32[]{:S(2)}) async-start(f32[16,4,224]{2,1,0:T(4,128)} %maximum_bitcast_fusion), calls=%async_computation.3 | async-start | bytes 131072 | tf_op jit(solution)/shard_map/all_to_all | solution.py:116
  330.0 6.5 %all-to-all-done.3 = f32[16,4,224]{2,1,0:T(4,128)S(1)} async-done(((f32[16,4,224]{2,1,0:T(4,128)}), f32[16,4,224]{2,1,0:T(4,128)S(1)}, u32[]{:S(2)}, u32[]{:S(2)}) %all-to-all-start.3) | async-done | bytes 57376 | tf_op jit(solution)/shard_map/all_to_all | solution.py:116
  336.5 14.7 %all-gather.2 = f32[8,4,224]{2,1,0:T(4,128)S(1)} all-gather(f32[1,4,224]{2,1,0:T(4,128)S(1)} %maximum_bitcast_fusion.1), channel_id=2, replica_groups=mesh['req'=16,'vocab'=8] {'vocab'}, dimensions={0}, use_global_device_ids=true | all-gather | bytes 32256 | tf_op jit(solution)/shard_map/all_gather | solution.py:117
  351.3 16.1 %all-gather.3 = f32[16,224,2]{1,2,0:T(2,128)S(1)} all-gather(f32[1,224,2]{1,2,0:T(2,128)S(1)} %maximum_bitcast_fusion.2), channel_id=1, replica_groups=mesh['req'=16,'vocab'=8] {'req'}, dimensions={0}, use_global_device_ids=true | all-gather | bytes 30464 | tf_op jit(solution)/shard_map/all_gather | solution.py:121
  367.5 5.4 %while.3 = (s32[]{:T(128)}, f32[2,3840]{1,0:T(2,128)S(1)}, s32[4,2]{0,1:T(2,128)S(1)}, f32[4,2,128]{2,0,1:T(4,128)S(1)}, s32[]{:T(128)}, /*index=5*/s32[]{:T(128)}) while((s32[]{:T(128)}, f32[2,3840]{1,0:T(2,128)S(1)}, s32[4,2]{0,1:T(2,128)S(1)}, f32[4,2,128]{2,0,1:T(4,128)S(1)}, s32[]{:T(128)}, /*index=5*/s32[]{:T(128)}) %tuple.64), condition=%wide.while_cond.1, body=%wide.while_body.1.sunk | while | flops 2 | bytes 4209 | solution.py:132
  (346 shorter events, 116.1 us)
Async XLA Ops:
  7.2 8.4 %copy-start.3 = (f32[2048]{0:T(1024)S(1)}, f32[2048]{0:T(1024)}, u32[]{:S(2)}) copy-start(f32[2048]{0:T(1024)} %param.12) | copy-start | bytes 24580
  15.5 10.8 %copy-start = (s32[64]{0:T(128)S(1)}, s32[64]{0:T(128)}, u32[]{:S(2)}) copy-start(s32[64]{0:T(128)} %param.17) | copy-start | bytes 772
  15.5 10.9 %copy-start.4 = (s32[4]{0:T(128)S(1)}, s32[4]{0:T(128)}, u32[]{:S(2)}) copy-start(s32[4]{0:T(128)} %param.15) | copy-start | bytes 52
  15.5 11.0 %copy-start.5 = (s32[4]{0:T(128)S(1)}, s32[4]{0:T(128)}, u32[]{:S(2)}) copy-start(s32[4]{0:T(128)} %param.16) | copy-start | bytes 52
  15.5 12.4 %copy-start.2 = (s32[4,128]{1,0:T(4,128)S(1)}, s32[4,128]{1,0:T(4,128)}, u32[]{:S(2)}) copy-start(s32[4,128]{1,0:T(4,128)} %param.14) | copy-start | bytes 6148
  18.7 37.0 %all-to-all-start = ((bf16[4,128,1024]{2,0,1:T(4,128)(2,1)}), bf16[4,128,1024]{2,0,1:T(4,128)(2,1)S(1)}, u32[]{:S(2)}, u32[]{:S(2)}) async-start(bf16[4,128,1024]{2,0,1:T(4,128)(2,1)} %fusion.2), calls=%async_computation | async-start | bytes 2097152 | tf_op jit(solution)/shard_map/all_to_all | solution.py:59
  53.4 26.7 %copy-start.1 = (s32[64,130]{1,0:T(8,128)}, s32[64,130]{1,0:T(8,128)S(1)}, u32[]{:S(2)}) copy-start(s32[64,130]{1,0:T(8,128)S(1)} %reshape.378) | copy-start | bytes 99844
  57.9 16.2 %all-to-all-start.1 = ((bf16[64,8,1024]{2,1,0:T(8,128)(2,1)}), bf16[64,8,1024]{2,1,0:T(8,128)(2,1)S(1)}, u32[]{:S(2)}, u32[]{:S(2)}) async-start(bf16[64,8,1024]{2,1,0:T(8,128)(2,1)} %broadcast_select_fusion), calls=%async_computation.1 | async-start | bytes 2097152 | tf_op jit(solution)/shard_map/all_to_all | solution.py:61
  62.3 100.2 %all-gather.6.cloned.1.call-start = ((), (), s32[]{:S(2)}) async-start(), calls=%async_computation.4 | async-start | bytes 7798784 | tf_op jit(solution)/shard_map/all_gather | solution.py:72
  76.2 225.3 %all-to-all-start.2 = ((bf16[16,600,128]{2,1,0:T(8,128)(2,1)}), bf16[16,600,128]{2,1,0:T(8,128)(2,1)S(1)}, u32[]{:S(2)}, u32[]{:S(2)}) async-start(bf16[16,600,128]{2,1,0:T(8,128)(2,1)} %bitcast.118), calls=%async_computation.2 | async-start | bytes 4915200 | tf_op jit(solution)/shard_map/all_to_all | solution.py:49
  80.9 0.8 slice-start
  162.4 146.3 %collective-permute-start = (bf16[3584,1024]{1,0:T(8,128)(2,1)}, bf16[3584,1024]{1,0:T(8,128)(2,1)}, u32[]{:S(2)}, u32[]{:S(2)}) collective-permute-start(bf16[3584,1024]{1,0:T(8,128)(2,1)} %all-gather.6.cloned.1.call-done), channel_id=1, source_target_pairs={{0,1},{1,0},{2,3},{3,2},{4,5},{5,4},{6,7},{7,6},{8,9},{9,8},{10,11... | collective-permute-start | bytes 22020104 | tf_op jit(solution)/shard_map/ppermute | solution.py:74
  324.9 11.5 %all-to-all-start.3 = ((f32[16,4,224]{2,1,0:T(4,128)}), f32[16,4,224]{2,1,0:T(4,128)S(1)}, u32[]{:S(2)}, u32[]{:S(2)}) async-start(f32[16,4,224]{2,1,0:T(4,128)} %maximum_bitcast_fusion), calls=%async_computation.3 | async-start | bytes 131072 | tf_op jit(solution)/shard_map/all_to_all | solution.py:116
Sparse Core Ops, SparseCore 0:
  76.3 86.0 all-gather.5

commit v3 on v2

--- a/solution.py
+++ b/solution.py
@@ -29,6 +29,11 @@
     return (wide_rows * scale * gain).astype(jnp.bfloat16)
 
 
+def gather_by_all_to_all(x, axis, n):
+    tiles = jnp.broadcast_to(x[None], (n,) + x.shape)
+    return lax.all_to_all(tiles, axis, split_axis=0, concat_axis=0, tiled=True)
+
+
 def shards(n_voc, hidden, gain, embedding, targets, span_start, span_len, deal_order):
     per_dev = hidden.shape[0]
     slot_len = hidden.shape[1]
@@ -49,7 +54,7 @@
     emb_piece = lax.all_to_all(embedding, "req", split_axis=0, concat_axis=1, tiled=True)
 
     meta = jnp.concatenate([targets, span_start[:, None], span_len[:, None]], axis=1)
-    meta_all = lax.all_gather(meta.astype(jnp.float32), "req", axis=0, tiled=True).astype(jnp.int32)
+    meta_all = gather_by_all_to_all(meta, "req", n_req).reshape(total, slot_len + 2)
     all_targets = meta_all[:, :slot_len]
     all_starts = meta_all[:, slot_len]
     all_lengths = meta_all[:, slot_len + 1]
@@ -83,14 +88,15 @@
     dealt_lengths = jnp.take(all_lengths, dealt_members)
     dealt_offsets = jnp.cumsum(dealt_lengths, axis=1) - dealt_lengths
     dealt_starts = jnp.take(all_starts, dealt_members)
-    padded_targets = jnp.pad(jnp.take(all_targets, source_of, axis=0), ((0, 0), (CAP, CAP)))
-    window_at = (dealt_starts - dealt_offsets + CAP).reshape(-1)
-    windows = jax.vmap(lambda row, at: lax.dynamic_slice_in_dim(row, at, CAP))(padded_targets, window_at)
+    member_targets = jnp.take(all_targets, source_of, axis=0).reshape(n_req, per_dev, slot_len)
     counter = jnp.arange(CAP, dtype=jnp.int32)
+    source_pos = counter[None, None, :] - dealt_offsets[:, :, None] + dealt_starts[:, :, None]
     in_member = (counter[None, None, :] >= dealt_offsets[:, :, None]) & (
         counter[None, None, :] < (dealt_offsets + dealt_lengths)[:, :, None]
     )
-    target_ids = jnp.sum(jnp.where(in_member, windows.reshape(n_req, per_dev, CAP), 0), axis=1).reshape(-1)
+    slot_ids = jnp.arange(slot_len, dtype=jnp.int32)
+    hit = (source_pos[..., None] == slot_ids) & in_member[..., None]
+    target_ids = jnp.sum(jnp.where(hit, member_targets[:, :, None, :], 0), axis=(1, 3)).reshape(-1)
 
     local_top = jnp.max(logits, axis=1)
     shifted = logits - local_top[:, None]
@@ -114,11 +120,11 @@
 
     local_stats = jnp.stack([local_top, local_mass, local_spread, local_target]).reshape(4, n_req, CAP)
     by_req = lax.all_to_all(local_stats.transpose(1, 0, 2), "req", split_axis=0, concat_axis=0, tiled=True)
-    group_stats = merge(lax.all_gather(merge(by_req), "vocab", axis=0))
+    group_stats = merge(gather_by_all_to_all(merge(by_req), "vocab", n_voc))
     row_top, row_mass, row_spread, row_target = group_stats[0], group_stats[1], group_stats[2], group_stats[3]
     log_mass = jnp.log(row_mass)
     group_out = jnp.stack([row_target - row_top - log_mass, log_mass - row_spread / row_mass])
-    all_out = lax.all_gather(group_out, "req", axis=1, tiled=True)
+    all_out = gather_by_all_to_all(group_out, "req", n_req).transpose(1, 0, 2).reshape(2, n_req * CAP)
 
     offsets = dealt_offsets.reshape(-1)
     my_reqs = here * per_dev + jnp.arange(per_dev, dtype=jnp.int32)
@@ -127,11 +133,12 @@
     my_len = jnp.take(all_lengths, my_reqs)
     pos = jnp.arange(slot_len, dtype=jnp.int32)[None, :]
     inside = (pos >= my_start[:, None]) & (pos < (my_start + my_len)[:, None])
-    padded_out = jnp.pad(all_out, ((0, 0), (slot_len, slot_len)))
-    out_at = (my_deal // per_dev) * CAP + jnp.take(offsets, my_deal) - my_start + slot_len
-    picked = jax.vmap(lambda at: lax.dynamic_slice_in_dim(padded_out, at, slot_len, axis=1))(out_at)
-    out_logprob = jnp.where(inside, picked[:, 0], 0.0)
-    out_entropy = jnp.where(inside, picked[:, 1], 0.0)
+    group_rows = jnp.take(all_out.reshape(2, n_req, CAP), my_deal // per_dev, axis=1)
+    at = (jnp.take(offsets, my_deal) - my_start)[:, None] + pos
+    pick = at[:, :, None] == jnp.arange(CAP, dtype=jnp.int32)
+    picked = jnp.sum(jnp.where(pick[None], group_rows[:, :, None, :], 0.0), axis=3)
+    out_logprob = jnp.where(inside, picked[0], 0.0)
+    out_entropy = jnp.where(inside, picked[1], 0.0)
     return (out_logprob, out_entropy)
 
 

time: 387 us -> 250 us (0.65); the launches traced: 380 us -> 248 us
  local copies, waits for them, and re-layouts: 151 us -> 14.3 us
  blocking collectives: 56.1 us -> 0 us
  waiting for transfers between devices: 96.2 us -> 132 us
  starting transfers between devices: 21.5 us -> 41.4 us
  other arithmetic: 23.1 us -> 29.2 us
    gather x274 -> x3, local copies, waits for them, and re-layouts: 141 us -> 1.82 us  [the longest x1 0.64 us: shards(): at = (jnp.take(offsets, my_deal) - my_start)[:, None] + pos]
    all_gather x3 -> x0, blocking collectives: 56.1 us -> none  [the longest x1 25.3 us: shards(): lax.all_gather(meta.astype(jnp.float32), 'req', axis=0, tiled=True)]
    all_to_all x1, waiting for transfers between devices: 0.01 us -> 21 us  [shards(): lax.all_to_all(embedding, 'req', split_axis=0, concat_axis=1, tiled=True)]
    all_to_all x0 -> x3, starting transfers between devices: none -> 18.1 us  [gather_by_all_to_all(): return lax.all_to_all(tiles, axis, split_axis=0, concat_axis=0, tiled=True)]
    all_to_all x1, waiting for transfers between devices: 0.01 us -> 13 us  [shards(): lax.all_to_all(my_half, 'req', split_axis=1, concat_axis=0, tiled=True)]
    all_gather x1, waiting for transfers between devices: 79.5 us -> 67.7 us  [shards(): rows_mine = lax.all_gather(compact_half, 'req', axis=0, tiled=True)]
    all_to_all x0 -> x3, waiting for transfers between devices: none -> 11 us  [gather_by_all_to_all(): return lax.all_to_all(tiles, axis, split_axis=0, concat_axis=0, tiled=True)]
    reduce_sum x1 -> x2, other arithmetic: 0.13 us -> 6.65 us  [the longest x1 6.33 us: shards(): jnp.sum(jnp.where(hit, member_targets[:, :, None, :], 0), axis=(1, 3))]
  transfers between devices with their start and end apart: 6 -> 9, of which waited for: 3 -> 7; matrix products, arithmetic and copies ran while one was open for 40% -> 14% of each run, Pallas kernels for 0% -> 0%
where the time goes in v3:
time: 250 us; the launch traced here: 248 us
  waiting for transfers between devices  132 us (53%)
  starting transfers between devices  41.4 us (17%)
  other arithmetic  29.2 us (12%)
  matrix products  17 us (7%)
  between operations  14.5 us (6%)
  local copies, waits for them, and re-layouts  14.3 us (6%)
    all_gather x1, waiting for transfers between devices, shards(): rows_mine = lax.all_gather(compact_half, 'req', axis=0, tiled=True)  67.7 us
    all_to_all x1, waiting for transfers between devices, shards(): lax.all_to_all(embedding, 'req', split_axis=0, concat_axis=1, tiled=True)  21 us
    all_to_all x3, starting transfers between devices, gather_by_all_to_all(): return lax.all_to_all(tiles, axis, split_axis=0, concat_axis=0, tiled=True)  18.1 us
    all_to_all x1, waiting for transfers between devices, shards(): lax.all_to_all(dealt_rows, 'req', split_axis=0, concat_axis=1, tiled=True)  13 us
    all_to_all x1, waiting for transfers between devices, shards(): lax.all_to_all(my_half, 'req', split_axis=1, concat_axis=0, tiled=True)  13 us
    all_to_all x3, waiting for transfers between devices, gather_by_all_to_all(): return lax.all_to_all(tiles, axis, split_axis=0, concat_axis=0, tiled=True)  11 us
    dot_general x1, matrix products, shards(): lax.dot_general(rows_other, emb_other, dims, preferred_element_type=jnp.f...  10 us
    dot_general x1, matrix products, shards(): lax.dot_general(rows_mine, emb_mine, dims, preferred_element_type=jnp.flo...  6.93 us
  transfers between devices with their start and end apart: 9, of which 7 were waited for; matrix products, arithmetic and copies ran while one was open for 14% of the time, Pallas kernels for 0%

profile of v3, /device:TPU:1, one launch (start us, length us, event | category | flops | bytes accessed | tf_op | source)
XLA Modules:
  0.0 248.4 jit_solution(9717828840741539713)
XLA Ops:
  7.2 0.9 copy.77
  8.1 0.7 copy.78
  8.8 0.8 pad_add_fusion
  9.6 0.6 broadcast_in_dim.169
  10.2 7.6 %all-to-all-start = ((s32[16,4,130]{2,1,0:T(4,128)}), s32[16,4,130]{2,1,0:T(4,128)S(1)}, u32[]{:S(2)}, u32[]{:S(2)}) async-start(s32[16,4,130]{2,1,0:T(4,128)} %broadcast_in_dim.169), calls=%async_computation | async-start | bytes 131072 | tf_op jit(solution)/shard_map/all_to_all | solution.py:34
  17.8 5.1 %copy_convert_fusion = f32[4,128,2048]{2,0,1:T(4,128)} fusion(bf16[4,128,2048]{2,1,0:T(8,128)(2,1)} %param.11), kind=kLoop, calls=%fused_computation.27 | loop fusion | flops 1048576 | bytes 6291456 | tf_op jit(solution)/shard_map/convert_element_type | solution.py:27
  23.0 1.6 multiply_reduce_fusion
  24.8 3.1 %fusion.3 = bf16[4,128,1024]{2,0,1:T(4,128)(2,1)} fusion(f32[4,128,2048]{2,0,1:T(4,128)} %copy_convert_fusion, s32[]{:T(128)S(6)} %select_n.142, f32[1024]{0:T(1024)S(1)} %dynamic-slice, f32[4,128]{0,1:T(8,128)S(1)} %add_rsqrt_fusion), kind=kLoop, calls=%fused_computation.26 | loop fusion | flops 1572864 | bytes 3151876 | tf_op jit(solution)/shard_map/convert_element_type | solution.py:29
  27.9 0.6 gather_fusion.9
  28.5 6.6 %all-to-all-start.1 = ((bf16[4,128,1024]{2,0,1:T(4,128)(2,1)}), bf16[4,128,1024]{2,0,1:T(4,128)(2,1)S(1)}, u32[]{:S(2)}, u32[]{:S(2)}) async-start(bf16[4,128,1024]{2,0,1:T(4,128)(2,1)} %fusion.3), calls=%async_computation.1 | async-start | bytes 2097152 | tf_op jit(solution)/shard_map/all_to_all | solution.py:64
  35.4 0.6 gather_fusion.10
  36.1 0.6 fusion.23
  36.9 0.6 gather_fusion.11
  37.5 13.0 %all-to-all-done.1 = bf16[4,128,1024]{2,0,1:T(4,128)(2,1)S(1)} async-done(((bf16[4,128,1024]{2,0,1:T(4,128)(2,1)}), bf16[4,128,1024]{2,0,1:T(4,128)(2,1)S(1)}, u32[]{:S(2)}, u32[]{:S(2)}) %all-to-all-start.1) | async-done | bytes 1048608 | tf_op jit(solution)/shard_map/all_to_all | solution.py:64
  50.9 0.6 gather_fusion
  51.5 1.2 broadcast_select_fusion
  52.7 4.0 %all-to-all-start.2 = ((bf16[64,8,1024]{2,1,0:T(8,128)(2,1)}), bf16[64,8,1024]{2,1,0:T(8,128)(2,1)S(1)}, u32[]{:S(2)}, u32[]{:S(2)}) async-start(bf16[64,8,1024]{2,1,0:T(8,128)(2,1)} %broadcast_select_fusion), calls=%async_computation.2 | async-start | bytes 2097152 | tf_op jit(solution)/shard_map/all_to_all | solution.py:66
  57.0 0.7 compare_select_fusion.1
  57.7 0.7 compare_and_fusion.4
  58.3 13.0 %all-to-all-done.2 = bf16[64,8,1024]{2,1,0:T(8,128)(2,1)S(1)} async-done(((bf16[64,8,1024]{2,1,0:T(8,128)(2,1)}), bf16[64,8,1024]{2,1,0:T(8,128)(2,1)S(1)}, u32[]{:S(2)}, u32[]{:S(2)}) %all-to-all-start.2) | async-done | bytes 1048608 | tf_op jit(solution)/shard_map/all_to_all | solution.py:66
  71.4 1.1 gather_fusion.1
  72.5 0.9 broadcast_select_fusion.1
  73.4 67.7 %all-gather.2.cloned.1.call-done = bf16[3584,1024]{1,0:T(8,128)(2,1)} async-done(((bf16[224,1024]{1,0:T(8,128)(2,1)}), bf16[3584,1024]{1,0:T(8,128)(2,1)}) %all-gather.2.cloned.1.call-update) | async-done | bytes 7340048 | tf_op jit(solution)/shard_map/all_gather | solution.py:77
  141.1 0.8 collective-permute-start
  141.9 5.0 %all-to-all-start.3 = ((bf16[16,600,128]{2,1,0:T(8,128)(2,1)}), bf16[16,600,128]{2,1,0:T(8,128)(2,1)S(1)}, u32[]{:S(2)}, u32[]{:S(2)}) async-start(bf16[16,600,128]{2,1,0:T(8,128)(2,1)} %bitcast.96), calls=%async_computation.3 | async-start | bytes 4915200 | tf_op jit(solution)/shard_map/all_to_all | solution.py:54
  147.0 0.6 gather_fusion.7
  147.9 0.8 gather_fusion.6
  148.6 0.8 gather_fusion.12
  149.4 0.6 gather_fusion.4
  150.1 0.6 gather_fusion.5
  151.0 0.6 gather_fusion.2
  152.1 6.3 %select_reduce_fusion.1 = s32[16,224]{1,0:T(8,128)S(1)} fusion(s32[16,4,128]{2,1,0:T(4,128)S(1)} %broadcast_select_fusion.2, s32[16,4,224]{2,1,0:T(4,128)S(1)} %subtract_add_fusion, pred[16,4,224]{2,1,0:T(4,128)(4,1)S(1)} %fusion.7), kind=kLoop, calls=%fused_computation.18 | loop fusion | flops 7336448 | bytes 118784 | tf_op jit(solution)/shard_map/reduce_sum | solution.py:99
  158.5 0.6 gather_fusion.8
  159.1 21.0 %all-to-all-done.3 = bf16[16,600,128]{2,1,0:T(8,128)(2,1)S(1)} async-done(((bf16[16,600,128]{2,1,0:T(8,128)(2,1)}), bf16[16,600,128]{2,1,0:T(8,128)(2,1)S(1)}, u32[]{:S(2)}, u32[]{:S(2)}) %all-to-all-start.3) | async-done | bytes 2457632 | tf_op jit(solution)/shard_map/all_to_all | solution.py:54
  180.4 6.9 %fusion.5 = f32[3584,600]{0,1:T(8,128)S(1)} fusion(bf16[3584,1024]{1,0:T(8,128)(2,1)} %all-gather.2.cloned.1.call-done, bf16[600,2048]{1,0:T(8,128)(2,1)S(1)} %copy_bitcast_fusion, s32[]{:T(128)S(6)} %select_n.142), kind=kOutput, calls=%fused_computation.29 | convolution fusion | flops 4404019200 | bytes 17170436 | tf_op jit(solution)/shard_map/dot_general | solution.py:84
  187.4 10.0 %fusion.26 = (f32[3584]{0:T(1024)S(1)}, f32[3584,600]{0,1:T(8,128)}) fusion(f32[3584,600]{0,1:T(8,128)S(1)} %fusion.5, bf16[3584,1024]{1,0:T(8,128)(2,1)} %collective-permute-done, bf16[600,2048]{1,0:T(8,128)(2,1)S(1)} %copy_bitcast_fusion, s32[]{:T(128)S(6)} %select_n.148), kind=kOutput, calls=%fused_computation.131 | convolution fusion | flops 4408316416 | bytes 25786372 | tf_op jit(solution)/shard_map/dot_general | solution.py:85
  197.5 5.1 %exponential_reduce_fusion = (f32[3584]{0:T(1024)S(1)}, f32[3584]{0:T(1024)S(1)}, f32[3584]{0:T(1024)S(1)}) fusion(f32[3584,600]{0,1:T(8,128)} %get-tuple-element.42, f32[3584]{0:T(1024)S(1)} %get-tuple-element.41, s32[3584]{0:T(1024)S(1)} %sub.134), kind=kLoop, calls=%fused_computation.14 | loop fusion | flops 15042048 | bytes 8673280 | tf_op jit(solution)/shard_map/reduce_sum | solution.py:104
  202.9 0.7 maximum_bitcast_fusion
  203.6 6.7 %all-to-all-start.4 = ((f32[16,4,224]{2,1,0:T(4,128)}), f32[16,4,224]{2,1,0:T(4,128)S(1)}, u32[]{:S(2)}, u32[]{:S(2)}) async-start(f32[16,4,224]{2,1,0:T(4,128)} %maximum_bitcast_fusion), calls=%async_computation.4 | async-start | bytes 131072 | tf_op jit(solution)/shard_map/all_to_all | solution.py:122
  210.4 6.5 %all-to-all-done.4 = f32[16,4,224]{2,1,0:T(4,128)S(1)} async-done(((f32[16,4,224]{2,1,0:T(4,128)}), f32[16,4,224]{2,1,0:T(4,128)S(1)}, u32[]{:S(2)}, u32[]{:S(2)}) %all-to-all-start.4) | async-done | bytes 57376 | tf_op jit(solution)/shard_map/all_to_all | solution.py:122
  217.0 0.6 broadcast_in_dim.185
  217.6 7.0 %all-to-all-start.5 = ((f32[8,4,224]{2,1,0:T(4,128)}), f32[8,4,224]{2,1,0:T(4,128)S(1)}, u32[]{:S(2)}, u32[]{:S(2)}) async-start(f32[8,4,224]{2,1,0:T(4,128)} %broadcast_in_dim.185), calls=%async_computation.5 | async-start | bytes 65536 | tf_op jit(solution)/shard_map/all_to_all | solution.py:34
  224.7 4.6 %all-to-all-done.5 = f32[8,4,224]{2,1,0:T(4,128)S(1)} async-done(((f32[8,4,224]{2,1,0:T(4,128)}), f32[8,4,224]{2,1,0:T(4,128)S(1)}, u32[]{:S(2)}, u32[]{:S(2)}) %all-to-all-start.5) | async-done | bytes 28704 | tf_op jit(solution)/shard_map/all_to_all | solution.py:34
  229.4 0.6 broadcast_in_dim.186
  230.0 3.5 %all-to-all-start.6 = ((f32[16,2,224]{2,1,0:T(2,128)}), f32[16,2,224]{2,1,0:T(2,128)S(1)}, u32[]{:S(2)}, u32[]{:S(2)}) async-start(f32[16,2,224]{2,1,0:T(2,128)} %broadcast_in_dim.186), calls=%async_computation.6 | async-start | bytes 65536 | tf_op jit(solution)/shard_map/all_to_all | solution.py:34
  233.6 6.3 %all-to-all-done.6 = f32[16,2,224]{2,1,0:T(2,128)S(1)} async-done(((f32[16,2,224]{2,1,0:T(2,128)}), f32[16,2,224]{2,1,0:T(2,128)S(1)}, u32[]{:S(2)}, u32[]{:S(2)}) %all-to-all-start.6) | async-done | bytes 28704 | tf_op jit(solution)/shard_map/all_to_all | solution.py:34
  239.9 0.6 gather_fusion.3
  240.9 0.7 fusion.14
  (71 shorter events, 3.7 us)
Async XLA Ops:
  7.2 15.8 %copy-start.1 = (bf16[4,128,2048]{2,1,0:T(8,128)(2,1)S(1)}, bf16[4,128,2048]{2,1,0:T(8,128)(2,1)}, u32[]{:S(2)}) copy-start(bf16[4,128,2048]{2,1,0:T(8,128)(2,1)} %param.11) | copy-start | bytes 6291460
  10.2 18.3 %all-to-all-start = ((s32[16,4,130]{2,1,0:T(4,128)}), s32[16,4,130]{2,1,0:T(4,128)S(1)}, u32[]{:S(2)}, u32[]{:S(2)}) async-start(s32[16,4,130]{2,1,0:T(4,128)} %broadcast_in_dim.169), calls=%async_computation | async-start | bytes 131072 | tf_op jit(solution)/shard_map/all_to_all | solution.py:34
  17.8 6.8 %copy-start = (s32[64]{0:T(128)S(1)}, s32[64]{0:T(128)}, u32[]{:S(2)}) copy-start(s32[64]{0:T(128)} %param.17) | copy-start | bytes 772
  17.8 6.9 %copy-start.2 = (f32[2048]{0:T(1024)S(1)}, f32[2048]{0:T(1024)}, u32[]{:S(2)}) copy-start(f32[2048]{0:T(1024)} %param.12) | copy-start | bytes 24580
  28.5 22.0 %all-to-all-start.1 = ((bf16[4,128,1024]{2,0,1:T(4,128)(2,1)}), bf16[4,128,1024]{2,0,1:T(4,128)(2,1)S(1)}, u32[]{:S(2)}, u32[]{:S(2)}) async-start(bf16[4,128,1024]{2,0,1:T(4,128)(2,1)} %fusion.3), calls=%async_computation.1 | async-start | bytes 2097152 | tf_op jit(solution)/shard_map/all_to_all | solution.py:64
  52.7 18.6 %all-to-all-start.2 = ((bf16[64,8,1024]{2,1,0:T(8,128)(2,1)}), bf16[64,8,1024]{2,1,0:T(8,128)(2,1)S(1)}, u32[]{:S(2)}, u32[]{:S(2)}) async-start(bf16[64,8,1024]{2,1,0:T(8,128)(2,1)} %broadcast_select_fusion), calls=%async_computation.2 | async-start | bytes 2097152 | tf_op jit(solution)/shard_map/all_to_all | solution.py:66
  56.8 84.3 %all-gather.2.cloned.1.call-start = ((), (), s32[]{:S(2)}) async-start(), calls=%async_computation.7 | async-start | bytes 7798784 | tf_op jit(solution)/shard_map/all_gather | solution.py:77
  141.1 46.3 %collective-permute-start = (bf16[3584,1024]{1,0:T(8,128)(2,1)}, bf16[3584,1024]{1,0:T(8,128)(2,1)}, u32[]{:S(2)}, u32[]{:S(2)}) collective-permute-start(bf16[3584,1024]{1,0:T(8,128)(2,1)} %all-gather.2.cloned.1.call-done), channel_id=1, source_target_pairs={{0,1},{1,0},{2,3},{3,2},{4,5},{5,4},{6,7},{7,6},{8,9},{9,8},{10,11... | collective-permute-start | bytes 22020104 | tf_op jit(solution)/shard_map/ppermute | solution.py:79
  141.9 38.2 %all-to-all-start.3 = ((bf16[16,600,128]{2,1,0:T(8,128)(2,1)}), bf16[16,600,128]{2,1,0:T(8,128)(2,1)S(1)}, u32[]{:S(2)}, u32[]{:S(2)}) async-start(bf16[16,600,128]{2,1,0:T(8,128)(2,1)} %bitcast.96), calls=%async_computation.3 | async-start | bytes 4915200 | tf_op jit(solution)/shard_map/all_to_all | solution.py:54
  203.6 13.3 %all-to-all-start.4 = ((f32[16,4,224]{2,1,0:T(4,128)}), f32[16,4,224]{2,1,0:T(4,128)S(1)}, u32[]{:S(2)}, u32[]{:S(2)}) async-start(f32[16,4,224]{2,1,0:T(4,128)} %maximum_bitcast_fusion), calls=%async_computation.4 | async-start | bytes 131072 | tf_op jit(solution)/shard_map/all_to_all | solution.py:122
  217.6 11.7 %all-to-all-start.5 = ((f32[8,4,224]{2,1,0:T(4,128)}), f32[8,4,224]{2,1,0:T(4,128)S(1)}, u32[]{:S(2)}, u32[]{:S(2)}) async-start(f32[8,4,224]{2,1,0:T(4,128)} %broadcast_in_dim.185), calls=%async_computation.5 | async-start | bytes 65536 | tf_op jit(solution)/shard_map/all_to_all | solution.py:34
  230.0 9.9 %all-to-all-start.6 = ((f32[16,2,224]{2,1,0:T(2,128)}), f32[16,2,224]{2,1,0:T(2,128)S(1)}, u32[]{:S(2)}, u32[]{:S(2)}) async-start(f32[16,2,224]{2,1,0:T(2,128)} %broadcast_in_dim.186), calls=%async_computation.6 | async-start | bytes 65536 | tf_op jit(solution)/shard_map/all_to_all | solution.py:34
Sparse Core Ops, SparseCore 0:
  73.6 67.5 all-gather.1

commit v4 on v3

--- a/solution.py
+++ b/solution.py
@@ -51,17 +51,32 @@
         jnp.where(deal_order[None, :] == positions[:, None], positions[None, :], 0), axis=1
     )
 
-    emb_piece = lax.all_to_all(embedding, "req", split_axis=0, concat_axis=1, tiled=True)
-
-    meta = jnp.concatenate([targets, span_start[:, None], span_len[:, None]], axis=1)
-    meta_all = gather_by_all_to_all(meta, "req", n_req).reshape(total, slot_len + 2)
-    all_targets = meta_all[:, :slot_len]
-    all_starts = meta_all[:, slot_len]
-    all_lengths = meta_all[:, slot_len + 1]
-
     normed_home = normalize(hidden, gain)
     my_half = lax.dynamic_slice_in_dim(normed_home, core * half, half, axis=2)
-    spread_rows = lax.all_to_all(my_half, "req", split_axis=1, concat_axis=0, tiled=True)
+    block = slot_len // n_req
+    hid_chunks = my_half.reshape(per_dev, n_req, block, half).transpose(1, 0, 2, 3).reshape(n_req, -1)
+    emb_chunks = embedding.reshape(n_req, piece * embedding.shape[1])
+    digits = jnp.stack([targets // 16384, (targets // 128) % 128, targets % 128], axis=1)
+    bounds = jnp.zeros((per_dev, 1, slot_len), jnp.int32)
+    bounds = bounds.at[:, 0, 0].set(span_start).at[:, 0, 1].set(span_len)
+    meta = jnp.concatenate([digits, bounds], axis=1).astype(jnp.bfloat16).reshape(1, -1)
+    meta_chunks = jnp.broadcast_to(meta, (n_req, meta.shape[1]))
+    packed = jnp.concatenate([hid_chunks, emb_chunks, meta_chunks], axis=1)
+    received = lax.all_to_all(packed, "req", split_axis=0, concat_axis=0, tiled=True)
+    n_hid = hid_chunks.shape[1]
+    n_emb = emb_chunks.shape[1]
+    spread_rows = received[:, :n_hid].reshape(total, block, half)
+    emb_piece = (
+        received[:, n_hid : n_hid + n_emb]
+        .reshape(n_req, piece, embedding.shape[1])
+        .transpose(1, 0, 2)
+        .reshape(piece, width)
+    )
+    meta_all = received[:, n_hid + n_emb :].astype(jnp.int32).reshape(total, 4, slot_len)
+    all_targets = meta_all[:, 0] * 16384 + meta_all[:, 1] * 128 + meta_all[:, 2]
+    all_starts = meta_all[:, 3, 0]
+    all_lengths = meta_all[:, 3, 1]
+
     dealt_rows = jnp.take(spread_rows, source_of, axis=0)
     home_rows = lax.all_to_all(dealt_rows, "req", split_axis=0, concat_axis=1, tiled=True)
 

time: 250 us -> 296 us (1.18)
  local copies, waits for them, and re-layouts: 14.3 us -> 45.7 us
  other arithmetic: 29.2 us -> 40.4 us
  waiting for transfers between devices: 132 us -> 142 us
  starting transfers between devices: 41.4 us -> 34.7 us
    unnamed x6 -> x18, local copies, waits for them, and re-layouts: 0.02 us -> 26.2 us
    all_to_all x0 -> x2, other arithmetic: none -> 13.9 us  [shards(): lax.all_to_all(packed, 'req', split_axis=0, concat_axis=0, tiled=True)]
    all_to_all x2 -> x1, waiting for transfers between devices: 34 us -> 44.2 us  [shards(): lax.all_to_all(packed, 'req', split_axis=0, concat_axis=0, tiled=True)]
    all_to_all x3 -> x2, starting transfers between devices: 18.1 us -> 9.35 us  [gather_by_all_to_all(): return lax.all_to_all(tiles, axis, split_axis=0, concat_axis=0, tiled=True)]
    all_to_all x1, starting transfers between devices: 4.04 us -> 11.7 us  [shards(): lax.all_to_all(dealt_rows, 'req', split_axis=0, concat_axis=1, tiled=True)]
    all_to_all x2 -> x1, starting transfers between devices: 11.6 us -> 7.76 us  [shards(): lax.all_to_all(packed, 'req', split_axis=0, concat_axis=0, tiled=True)]
    reshape x1 -> x4, local copies, waits for them, and re-layouts: 0.02 us -> 3.66 us  [the longest x1 2.35 us: shards(): emb_chunks = embedding.reshape(n_req, piece * embedding.shape[1])]
    convert_element_type x1 -> x0, other arithmetic: 3.12 us -> none  [normalize(): return (wide_rows * scale * gain).astype(jnp.bfloat16)]
  transfers between devices with their start and end apart: 9 -> 7, of which waited for: 7 -> 6; matrix products, arithmetic and copies ran while one was open for 14% -> 8% of each run, Pallas kernels for 0% -> 0%
where the time goes in v4:
time: 296 us; the launch traced here: 295 us
  waiting for transfers between devices  142 us (48%)
  local copies, waits for them, and re-layouts  45.7 us (15%)
  other arithmetic  40.4 us (14%)
  starting transfers between devices  34.7 us (12%)
  matrix products  17.1 us (6%)
  between operations  14.6 us (5%)
    all_gather x1, waiting for transfers between devices, shards(): rows_mine = lax.all_gather(compact_half, 'req', axis=0, tiled=True)  67.3 us
    all_to_all x1, waiting for transfers between devices, shards(): lax.all_to_all(packed, 'req', split_axis=0, concat_axis=0, tiled=True)  44.2 us
    unnamed x18, local copies, waits for them, and re-layouts  26.2 us
    all_to_all x2, other arithmetic, shards(): lax.all_to_all(packed, 'req', split_axis=0, concat_axis=0, tiled=True)  13.9 us
    all_to_all x1, waiting for transfers between devices, shards(): lax.all_to_all(dealt_rows, 'req', split_axis=0, concat_axis=1, tiled=True)  13.3 us
    all_to_all x1, starting transfers between devices, shards(): lax.all_to_all(dealt_rows, 'req', split_axis=0, concat_axis=1, tiled=True)  11.7 us
    all_to_all x2, waiting for transfers between devices, gather_by_all_to_all(): return lax.all_to_all(tiles, axis, split_axis=0, concat_axis=0, tiled=True)  11 us
    dot_general x1, matrix products, shards(): lax.dot_general(rows_other, emb_other, dims, preferred_element_type=jnp.f...  10.1 us
  transfers between devices with their start and end apart: 7, of which 6 were waited for; matrix products, arithmetic and copies ran while one was open for 8% of the time, Pallas kernels for 0%

profile of v4, /device:TPU:1, one launch (start us, length us, event | category | flops | bytes accessed | tf_op | source)
XLA Modules:
  0.0 295.0 jit_solution(3302759064845836705)
XLA Ops:
  7.2 2.1 multiply_reduce_fusion
  9.3 4.1 %convert_element_type.19 = f32[4,128,2048]{2,1,0:T(8,128)} convert(bf16[4,128,2048]{2,1,0:T(8,128)(2,1)} %param.15) | non-fusion elementwise | flops 1048576 | bytes 6291456 | tf_op jit(solution)/shard_map/convert_element_type | solution.py:27
  14.1 0.8 scatter.9
  15.0 2.4 reshape.344
  17.4 1.8 fusion.7
  20.0 7.8 %maximum_bitcast_fusion = bf16[16,1,111616]{2,0,1:T(8,128)(2,1)} fusion(bf16[16,76800]{1,0:T(8,128)(2,1)S(1)} %reshape.344, bf16[16,32768]{1,0:T(8,128)(2,1)S(1)} %bitcast.118, bf16[111616]{0:T(1024)(128)(2,1)S(1)} %pad.19.clone), kind=kLoop, calls=%fused_computation.23 | loop fusion | flops 10715136 | bytes 7301120 | tf_op jit(solution)/shard_map/all_to_all | solution.py:65
  28.3 6.0 %reduce.12 = bf16[16,111616]{1,0:T(8,128)(2,1)} reduce(bf16[16,1,111616]{2,0,1:T(8,128)(2,1)} %maximum_bitcast_fusion, bf16[]{:T(256)} %broadcast.503), dimensions={1}, to_apply=%copy.154.reduce_sub_computation | reduce | bytes 7143426 | tf_op jit(solution)/shard_map/all_to_all | solution.py:65
  34.3 5.9 %reshape.502 = bf16[16,2,55808]{2,1,0:T(2,128)(2,1)} reshape(bf16[16,111616]{1,0:T(8,128)(2,1)} %reduce.12) | data formatting | bytes 7143424
  40.2 7.8 %all-to-all-start = ((bf16[16,2,55808]{2,1,0:T(2,128)(2,1)}), bf16[16,2,55808]{2,1,0:T(2,128)(2,1)}, u32[]{:S(2)}, u32[]{:S(2)}) async-start(bf16[16,2,55808]{2,1,0:T(2,128)(2,1)} %reshape.502), calls=%async_computation | async-start | bytes 7143424 | tf_op jit(solution)/shard_map/all_to_all | solution.py:65
  48.0 0.6 gather_fusion.7
  48.8 0.6 gather_fusion.9
  49.5 44.2 %all-to-all-done = bf16[16,2,55808]{2,1,0:T(2,128)(2,1)} async-done(((bf16[16,2,55808]{2,1,0:T(2,128)(2,1)}), bf16[16,2,55808]{2,1,0:T(2,128)(2,1)}, u32[]{:S(2)}, u32[]{:S(2)}) %all-to-all-start) | async-done | bytes 3571744 | tf_op jit(solution)/shard_map/all_to_all | solution.py:65
  93.7 11.7 %reshape.503 = bf16[16,1,111616]{2,1,0:T(2,128)(2,1)} reshape(bf16[16,2,55808]{2,1,0:T(2,128)(2,1)} %all-to-all-done) | data formatting | bytes 7143424
  105.4 4.2 %copy.210 = bf16[16,1,111616]{2,0,1:T(8,128)(2,1)S(1)} copy(bf16[16,1,111616]{2,1,0:T(2,128)(2,1)} %reshape.503) | data formatting | bytes 7143424
  109.6 1.7 copy-done.1
  111.5 2.4 slice_reduce_fusion.1
  113.9 0.6 gather_fusion.10
  114.6 0.6 gather_fusion.11
  115.2 0.6 fusion.32
  116.5 0.6 gather_fusion
  117.2 1.1 broadcast_select_fusion
  118.3 11.7 %all-to-all-start.1 = ((bf16[64,8,1024]{2,1,0:T(8,128)(2,1)}), bf16[64,8,1024]{2,1,0:T(8,128)(2,1)S(1)}, u32[]{:S(2)}, u32[]{:S(2)}) async-start(bf16[64,8,1024]{2,1,0:T(8,128)(2,1)} %broadcast_select_fusion), calls=%async_computation.1 | async-start | bytes 2097152 | tf_op jit(solution)/shard_map/all_to_all | solution.py:81
  130.3 0.7 compare_select_fusion.1
  131.0 0.7 compare_and_fusion.4
  131.6 13.3 %all-to-all-done.1 = bf16[64,8,1024]{2,1,0:T(8,128)(2,1)S(1)} async-done(((bf16[64,8,1024]{2,1,0:T(8,128)(2,1)}), bf16[64,8,1024]{2,1,0:T(8,128)(2,1)S(1)}, u32[]{:S(2)}, u32[]{:S(2)}) %all-to-all-start.1) | async-done | bytes 1048608 | tf_op jit(solution)/shard_map/all_to_all | solution.py:81
  145.1 1.1 gather_fusion.1
  146.1 0.9 broadcast_select_fusion.1
  147.1 67.3 %all-gather.2.cloned.1.call-done = bf16[3584,1024]{1,0:T(8,128)(2,1)} async-done(((bf16[224,1024]{1,0:T(8,128)(2,1)}), bf16[3584,1024]{1,0:T(8,128)(2,1)}) %all-gather.2.cloned.1.call-update) | async-done | bytes 7340048 | tf_op jit(solution)/shard_map/all_gather | solution.py:92
  214.4 0.8 collective-permute-start
  215.5 0.8 gather_fusion.12
  216.3 0.8 gather_fusion.6
  217.1 0.6 gather_fusion.5
  217.7 0.6 gather_fusion.4
  219.8 6.3 %select_reduce_fusion.1 = s32[16,224]{1,0:T(8,128)S(1)} fusion(s32[16,4,128]{2,1,0:T(4,128)S(1)} %broadcast_select_fusion.2, s32[16,4,224]{2,1,0:T(4,128)S(1)} %subtract_add_fusion, pred[16,4,224]{2,1,0:T(4,128)(4,1)S(1)} %fusion.8), kind=kLoop, calls=%fused_computation.18 | loop fusion | flops 7336448 | bytes 118784 | tf_op jit(solution)/shard_map/reduce_sum | solution.py:114
  226.2 1.9 slice_bitcast_fusion
  228.4 0.7 copy.211
  229.1 0.6 gather_fusion.8
  229.8 7.0 %fusion.5 = f32[3584,600]{0,1:T(8,128)S(1)} fusion(bf16[3584,1024]{1,0:T(8,128)(2,1)} %all-gather.2.cloned.1.call-done, bf16[600,2048]{1,0:T(8,128)(2,1)S(1)} %bitcast.121, s32[]{:T(128)S(6)} %select_n.154), kind=kOutput, calls=%fused_computation.31 | convolution fusion | flops 4404019200 | bytes 17170436 | tf_op jit(solution)/shard_map/dot_general | solution.py:99
  236.8 10.1 %fusion.36 = (f32[3584]{0:T(1024)S(1)}, f32[3584,600]{0,1:T(8,128)}) fusion(f32[3584,600]{0,1:T(8,128)S(1)} %fusion.5, bf16[3584,1024]{1,0:T(8,128)(2,1)} %collective-permute-done, bf16[600,2048]{1,0:T(8,128)(2,1)S(1)} %bitcast.122, s32[]{:T(128)S(6)} %select_n.170), kind=kOutput, calls=%fused_computation.157 | convolution fusion | flops 4408316416 | bytes 25786372 | tf_op jit(solution)/shard_map/dot_general | solution.py:100
  247.0 5.1 %exponential_reduce_fusion = (f32[3584]{0:T(1024)S(1)}, f32[3584]{0:T(1024)S(1)}, f32[3584]{0:T(1024)S(1)}) fusion(f32[3584,600]{0,1:T(8,128)} %get-tuple-element.72, f32[3584]{0:T(1024)S(1)} %get-tuple-element.71, s32[3584]{0:T(1024)S(1)} %sub.146), kind=kLoop, calls=%fused_computation.14 | loop fusion | flops 15042048 | bytes 8673280 | tf_op jit(solution)/shard_map/reduce_sum | solution.py:119
  252.4 0.7 maximum_bitcast_fusion.1
  253.0 5.0 %all-to-all-start.2 = ((f32[16,4,224]{2,1,0:T(4,128)}), f32[16,4,224]{2,1,0:T(4,128)S(1)}, u32[]{:S(2)}, u32[]{:S(2)}) async-start(f32[16,4,224]{2,1,0:T(4,128)} %maximum_bitcast_fusion.1), calls=%async_computation.2 | async-start | bytes 131072 | tf_op jit(solution)/shard_map/all_to_all | solution.py:137
  258.0 6.5 %all-to-all-done.2 = f32[16,4,224]{2,1,0:T(4,128)S(1)} async-done(((f32[16,4,224]{2,1,0:T(4,128)}), f32[16,4,224]{2,1,0:T(4,128)S(1)}, u32[]{:S(2)}, u32[]{:S(2)}) %all-to-all-start.2) | async-done | bytes 57376 | tf_op jit(solution)/shard_map/all_to_all | solution.py:137
  265.3 5.9 %all-to-all-start.3 = ((f32[8,4,224]{2,1,0:T(4,128)}), f32[8,4,224]{2,1,0:T(4,128)S(1)}, u32[]{:S(2)}, u32[]{:S(2)}) async-start(f32[8,4,224]{2,1,0:T(4,128)} %broadcast_in_dim.177), calls=%async_computation.3 | async-start | bytes 65536 | tf_op jit(solution)/shard_map/all_to_all | solution.py:34
  271.2 4.6 %all-to-all-done.3 = f32[8,4,224]{2,1,0:T(4,128)S(1)} async-done(((f32[8,4,224]{2,1,0:T(4,128)}), f32[8,4,224]{2,1,0:T(4,128)S(1)}, u32[]{:S(2)}, u32[]{:S(2)}) %all-to-all-start.3) | async-done | bytes 28704 | tf_op jit(solution)/shard_map/all_to_all | solution.py:34
  276.6 3.5 %all-to-all-start.4 = ((f32[16,2,224]{2,1,0:T(2,128)}), f32[16,2,224]{2,1,0:T(2,128)S(1)}, u32[]{:S(2)}, u32[]{:S(2)}) async-start(f32[16,2,224]{2,1,0:T(2,128)} %broadcast_in_dim.178), calls=%async_computation.4 | async-start | bytes 65536 | tf_op jit(solution)/shard_map/all_to_all | solution.py:34
  280.1 6.3 %all-to-all-done.4 = f32[16,2,224]{2,1,0:T(2,128)S(1)} async-done(((f32[16,2,224]{2,1,0:T(2,128)}), f32[16,2,224]{2,1,0:T(2,128)S(1)}, u32[]{:S(2)}, u32[]{:S(2)}) %all-to-all-start.4) | async-done | bytes 28704 | tf_op jit(solution)/shard_map/all_to_all | solution.py:34
  287.4 0.7 fusion.20
  (95 shorter events, 8.3 us)
Async XLA Ops:
  7.2 6.8 %copy-start.4 = (s32[4]{0:T(128)S(1)}, s32[4]{0:T(128)}, u32[]{:S(2)}) copy-start(s32[4]{0:T(128)} %param.19) | copy-start | bytes 52
  7.2 6.9 %copy-start.5 = (s32[4]{0:T(128)S(1)}, s32[4]{0:T(128)}, u32[]{:S(2)}) copy-start(s32[4]{0:T(128)} %param.20) | copy-start | bytes 52
  7.2 7.7 %copy-start.3 = (s32[4,128]{1,0:T(4,128)S(1)}, s32[4,128]{1,0:T(4,128)}, u32[]{:S(2)}) copy-start(s32[4,128]{1,0:T(4,128)} %param.18) | copy-start | bytes 6148
  9.3 8.1 %copy-start.2 = (f32[2048]{0:T(1024)S(1)}, f32[2048]{0:T(1024)}, u32[]{:S(2)}) copy-start(f32[2048]{0:T(1024)} %param.16) | copy-start | bytes 24580
  40.2 7.8 %copy-start = (s32[64]{0:T(128)S(1)}, s32[64]{0:T(128)}, u32[]{:S(2)}) copy-start(s32[64]{0:T(128)} %param.21) | copy-start | bytes 772
  40.2 53.5 %all-to-all-start = ((bf16[16,2,55808]{2,1,0:T(2,128)(2,1)}), bf16[16,2,55808]{2,1,0:T(2,128)(2,1)}, u32[]{:S(2)}, u32[]{:S(2)}) async-start(bf16[16,2,55808]{2,1,0:T(2,128)(2,1)} %reshape.502), calls=%async_computation | async-start | bytes 7143424 | tf_op jit(solution)/shard_map/all_to_all | solution.py:65
  109.6 1.8 copy-start.1
  118.3 26.7 %all-to-all-start.1 = ((bf16[64,8,1024]{2,1,0:T(8,128)(2,1)}), bf16[64,8,1024]{2,1,0:T(8,128)(2,1)S(1)}, u32[]{:S(2)}, u32[]{:S(2)}) async-start(bf16[64,8,1024]{2,1,0:T(8,128)(2,1)} %broadcast_select_fusion), calls=%async_computation.1 | async-start | bytes 2097152 | tf_op jit(solution)/shard_map/all_to_all | solution.py:81
  130.0 84.4 %all-gather.2.cloned.1.call-start = ((), (), s32[]{:S(2)}) async-start(), calls=%async_computation.5 | async-start | bytes 7798784 | tf_op jit(solution)/shard_map/all_gather | solution.py:92
  214.4 22.3 %collective-permute-start = (bf16[3584,1024]{1,0:T(8,128)(2,1)}, bf16[3584,1024]{1,0:T(8,128)(2,1)}, u32[]{:S(2)}, u32[]{:S(2)}) collective-permute-start(bf16[3584,1024]{1,0:T(8,128)(2,1)} %all-gather.2.cloned.1.call-done), channel_id=1, source_target_pairs={{0,1},{1,0},{2,3},{3,2},{4,5},{5,4},{6,7},{7,6},{8,9},{9,8},{10,11... | collective-permute-start | bytes 22020104 | tf_op jit(solution)/shard_map/ppermute | solution.py:94
  253.0 11.5 %all-to-all-start.2 = ((f32[16,4,224]{2,1,0:T(4,128)}), f32[16,4,224]{2,1,0:T(4,128)S(1)}, u32[]{:S(2)}, u32[]{:S(2)}) async-start(f32[16,4,224]{2,1,0:T(4,128)} %maximum_bitcast_fusion.1), calls=%async_computation.2 | async-start | bytes 131072 | tf_op jit(solution)/shard_map/all_to_all | solution.py:137
  265.3 10.6 %all-to-all-start.3 = ((f32[8,4,224]{2,1,0:T(4,128)}), f32[8,4,224]{2,1,0:T(4,128)S(1)}, u32[]{:S(2)}, u32[]{:S(2)}) async-start(f32[8,4,224]{2,1,0:T(4,128)} %broadcast_in_dim.177), calls=%async_computation.3 | async-start | bytes 65536 | tf_op jit(solution)/shard_map/all_to_all | solution.py:34
  276.6 9.9 %all-to-all-start.4 = ((f32[16,2,224]{2,1,0:T(2,128)}), f32[16,2,224]{2,1,0:T(2,128)S(1)}, u32[]{:S(2)}, u32[]{:S(2)}) async-start(f32[16,2,224]{2,1,0:T(2,128)} %broadcast_in_dim.178), calls=%async_computation.4 | async-start | bytes 65536 | tf_op jit(solution)/shard_map/all_to_all | solution.py:34
Sparse Core Ops, SparseCore 0:
  147.2 67.1 all-gather.1

commit v5 on v3

--- a/solution.py
+++ b/solution.py
@@ -53,15 +53,24 @@
 
     emb_piece = lax.all_to_all(embedding, "req", split_axis=0, concat_axis=1, tiled=True)
 
-    meta = jnp.concatenate([targets, span_start[:, None], span_len[:, None]], axis=1)
-    meta_all = gather_by_all_to_all(meta, "req", n_req).reshape(total, slot_len + 2)
-    all_targets = meta_all[:, :slot_len]
-    all_starts = meta_all[:, slot_len]
-    all_lengths = meta_all[:, slot_len + 1]
-
     normed_home = normalize(hidden, gain)
     my_half = lax.dynamic_slice_in_dim(normed_home, core * half, half, axis=2)
-    spread_rows = lax.all_to_all(my_half, "req", split_axis=1, concat_axis=0, tiled=True)
+    block = slot_len // n_req
+    digits = jnp.stack([targets // 16384, (targets // 128) % 128, targets % 128], axis=1)
+    bounds = jnp.zeros((per_dev, 1, slot_len), jnp.int32)
+    bounds = bounds.at[:, 0, 0].set(span_start).at[:, 0, 1].set(span_len)
+    meta = jnp.concatenate([digits, bounds], axis=1).astype(jnp.bfloat16).reshape(per_dev, 1, 1, -1)
+    meta = jnp.pad(meta, ((0, 0), (0, 0), (0, 0), (0, half - meta.shape[3])))
+    blocks = jnp.concatenate(
+        [my_half.reshape(per_dev, n_req, block, half), jnp.broadcast_to(meta, (per_dev, n_req, 1, half))],
+        axis=2,
+    ).reshape(per_dev, n_req * (block + 1), half)
+    received = lax.all_to_all(blocks, "req", split_axis=1, concat_axis=0, tiled=True)
+    spread_rows = received[:, :block]
+    meta_all = received[:, block, : 4 * slot_len].astype(jnp.int32).reshape(total, 4, slot_len)
+    all_targets = meta_all[:, 0] * 16384 + meta_all[:, 1] * 128 + meta_all[:, 2]
+    all_starts = meta_all[:, 3, 0]
+    all_lengths = meta_all[:, 3, 1]
     dealt_rows = jnp.take(spread_rows, source_of, axis=0)
     home_rows = lax.all_to_all(dealt_rows, "req", split_axis=0, concat_axis=1, tiled=True)
 
@@ -112,33 +121,30 @@
     def merge(stats):
         top_each, mass_each, spread_each, target_each = stats[:, 0], stats[:, 1], stats[:, 2], stats[:, 3]
         top = jnp.max(top_each, axis=0)
-        gap = top_each - top[None, :]
+        gap = top_each - top[None]
         factor = jnp.exp(gap)
         mass = jnp.sum(factor * mass_each, axis=0)
         spread = jnp.sum(factor * (spread_each + gap * mass_each), axis=0)
         return jnp.stack([top, mass, spread, jnp.sum(target_each, axis=0)])
 
+    offsets = dealt_offsets.reshape(-1)
+    pos = jnp.arange(slot_len, dtype=jnp.int32)[None, :]
     local_stats = jnp.stack([local_top, local_mass, local_spread, local_target]).reshape(4, n_req, CAP)
-    by_req = lax.all_to_all(local_stats.transpose(1, 0, 2), "req", split_axis=0, concat_axis=0, tiled=True)
-    group_stats = merge(gather_by_all_to_all(merge(by_req), "vocab", n_voc))
-    row_top, row_mass, row_spread, row_target = group_stats[0], group_stats[1], group_stats[2], group_stats[3]
+    request_rows = jnp.take(local_stats, deal_order // per_dev, axis=1)
+    at = (jnp.take(offsets, deal_order) - all_starts)[:, None] + pos
+    pick = at[:, :, None] == jnp.arange(CAP, dtype=jnp.int32)
+    picked = jnp.sum(jnp.where(pick[None], request_rows[:, :, None, :], 0.0), axis=3)
+    to_home = picked.reshape(4, n_req, per_dev, slot_len).transpose(1, 0, 2, 3)
+    by_req = merge(lax.all_to_all(to_home, "req", split_axis=0, concat_axis=0, tiled=True))
+    row_top, row_mass, row_spread, row_target = merge(gather_by_all_to_all(by_req, "vocab", n_voc))
     log_mass = jnp.log(row_mass)
-    group_out = jnp.stack([row_target - row_top - log_mass, log_mass - row_spread / row_mass])
-    all_out = gather_by_all_to_all(group_out, "req", n_req).transpose(1, 0, 2).reshape(2, n_req * CAP)
 
-    offsets = dealt_offsets.reshape(-1)
     my_reqs = here * per_dev + jnp.arange(per_dev, dtype=jnp.int32)
-    my_deal = jnp.take(deal_order, my_reqs)
     my_start = jnp.take(all_starts, my_reqs)
     my_len = jnp.take(all_lengths, my_reqs)
-    pos = jnp.arange(slot_len, dtype=jnp.int32)[None, :]
     inside = (pos >= my_start[:, None]) & (pos < (my_start + my_len)[:, None])
-    group_rows = jnp.take(all_out.reshape(2, n_req, CAP), my_deal // per_dev, axis=1)
-    at = (jnp.take(offsets, my_deal) - my_start)[:, None] + pos
-    pick = at[:, :, None] == jnp.arange(CAP, dtype=jnp.int32)
-    picked = jnp.sum(jnp.where(pick[None], group_rows[:, :, None, :], 0.0), axis=3)
-    out_logprob = jnp.where(inside, picked[0], 0.0)
-    out_entropy = jnp.where(inside, picked[1], 0.0)
+    out_logprob = jnp.where(inside, row_target - row_top - log_mass, 0.0)
+    out_entropy = jnp.where(inside, log_mass - row_spread / row_mass, 0.0)
     return (out_logprob, out_entropy)
 
 

time: 250 us -> 246 us (0.984)
  starting transfers between devices: 41.4 us -> 31.3 us
  other arithmetic: 29.2 us -> 35.9 us
  waiting for transfers between devices: 132 us -> 127 us
  local copies, waits for them, and re-layouts: 14.3 us -> 18.9 us
    all_to_all x3 -> x1, starting transfers between devices: 18.1 us -> 7 us  [gather_by_all_to_all(): return lax.all_to_all(tiles, axis, split_axis=0, concat_axis=0, tiled=True)]
    reduce_sum x1 -> x4, other arithmetic: 0.32 us -> 9 us  [the longest x1 8.94 us: shards(): jnp.sum(jnp.where(pick[None], request_rows[:, :, None, :], 0.0), axis=3)]
    all_to_all x3 -> x1, waiting for transfers between devices: 11 us -> 4.84 us  [gather_by_all_to_all(): return lax.all_to_all(tiles, axis, split_axis=0, concat_axis=0, tiled=True)]
    convert_element_type x1, other arithmetic: 3.12 us -> 0.02 us  [shards(): received[:, block, :4 * slot_len].astype(jnp.int32)]
  transfers between devices with their start and end apart: 9 -> 7, of which waited for: 7 -> 6; matrix products, arithmetic and copies ran while one was open for 14% -> 10% of each run, Pallas kernels for 0% -> 0%
where the time goes in v5:
time: 246 us; the launch traced here: 245 us
  waiting for transfers between devices  127 us (52%)
  other arithmetic  35.9 us (15%)
  starting transfers between devices  31.3 us (13%)
  local copies, waits for them, and re-layouts  18.9 us (8%)
  matrix products  17 us (7%)
  between operations  14.6 us (6%)
    all_gather x1, waiting for transfers between devices, shards(): rows_mine = lax.all_gather(compact_half, 'req', axis=0, tiled=True)  67.8 us
    all_to_all x1, waiting for transfers between devices, shards(): lax.all_to_all(embedding, 'req', split_axis=0, concat_axis=1, tiled=True)  20.2 us
    all_to_all x1, waiting for transfers between devices, shards(): lax.all_to_all(blocks, 'req', split_axis=1, concat_axis=0, tiled=True)  16.1 us
    all_to_all x1, waiting for transfers between devices, shards(): lax.all_to_all(dealt_rows, 'req', split_axis=0, concat_axis=1, tiled=True)  12.9 us
    dot_general x1, matrix products, shards(): lax.dot_general(rows_other, emb_other, dims, preferred_element_type=jnp.f...  10 us
    reduce_sum x1, other arithmetic, shards(): jnp.sum(jnp.where(pick[None], request_rows[:, :, None, :], 0.0), axis=3)  8.94 us
    all_to_all x1, starting transfers between devices, shards(): lax.all_to_all(blocks, 'req', split_axis=1, concat_axis=0, tiled=True)  7.57 us
    all_to_all x1, starting transfers between devices, gather_by_all_to_all(): return lax.all_to_all(tiles, axis, split_axis=0, concat_axis=0, tiled=True)  7 us
  transfers between devices with their start and end apart: 7, of which 6 were waited for; matrix products, arithmetic and copies ran while one was open for 10% of the time, Pallas kernels for 0%

profile of v5, /device:TPU:1, one launch (start us, length us, event | category | flops | bytes accessed | tf_op | source)
XLA Modules:
  0.0 245.1 jit_solution(8373988246229299107)
XLA Ops:
  7.2 4.2 %convert_element_type.30 = f32[4,128,2048]{2,1,0:T(8,128)} convert(bf16[4,128,2048]{2,1,0:T(8,128)(2,1)} %param.15) | non-fusion elementwise | flops 1048576 | bytes 6291456 | tf_op jit(solution)/shard_map/convert_element_type | solution.py:27
  11.4 0.5 multiply_reduce_fusion
  12.2 0.6 slice.88
  12.8 0.8 scatter.9
  13.6 1.8 fusion.7
  15.6 0.4 pad_maximum_fusion
  16.0 2.1 copy.174
  18.1 7.6 %all-to-all-start = ((bf16[4,144,1024]{2,0,1:T(4,128)(2,1)}), bf16[4,144,1024]{2,0,1:T(4,128)(2,1)S(1)}, u32[]{:S(2)}, u32[]{:S(2)}) async-start(bf16[4,144,1024]{2,0,1:T(4,128)(2,1)} %bitcast.8), calls=%async_computation | async-start | bytes 2359296 | tf_op jit(solution)/shard_map/all_to_all | solution.py:68
  25.8 0.6 gather_fusion.8
  26.5 16.1 %all-to-all-done = bf16[4,144,1024]{2,0,1:T(4,128)(2,1)S(1)} async-done(((bf16[4,144,1024]{2,0,1:T(4,128)(2,1)}), bf16[4,144,1024]{2,0,1:T(4,128)(2,1)S(1)}, u32[]{:S(2)}, u32[]{:S(2)}) %all-to-all-start) | async-done | bytes 1179680 | tf_op jit(solution)/shard_map/all_to_all | solution.py:68
  42.7 0.5 copy.175
  43.6 2.4 slice_reduce_fusion.2
  46.1 0.6 gather_fusion.9
  46.7 0.6 fusion.32
  47.5 0.6 gather_fusion.10
  48.2 0.6 copy.196
  48.7 0.6 gather_fusion.1
  49.4 1.2 broadcast_select_fusion
  50.5 4.1 %all-to-all-start.1 = ((bf16[64,8,1024]{2,1,0:T(8,128)(2,1)}), bf16[64,8,1024]{2,1,0:T(8,128)(2,1)S(1)}, u32[]{:S(2)}, u32[]{:S(2)}) async-start(bf16[64,8,1024]{2,1,0:T(8,128)(2,1)} %broadcast_select_fusion), calls=%async_computation.1 | async-start | bytes 2097152 | tf_op jit(solution)/shard_map/all_to_all | solution.py:75
  54.9 0.7 compare_select_fusion.1
  55.6 0.7 compare_and_fusion.4
  56.2 12.9 %all-to-all-done.1 = bf16[64,8,1024]{2,1,0:T(8,128)(2,1)S(1)} async-done(((bf16[64,8,1024]{2,1,0:T(8,128)(2,1)}), bf16[64,8,1024]{2,1,0:T(8,128)(2,1)S(1)}, u32[]{:S(2)}, u32[]{:S(2)}) %all-to-all-start.1) | async-done | bytes 1048608 | tf_op jit(solution)/shard_map/all_to_all | solution.py:75
  69.3 1.1 gather_fusion.2
  70.4 0.9 broadcast_select_fusion.1
  71.2 67.8 %all-gather.2.cloned.1.call-done = bf16[3584,1024]{1,0:T(8,128)(2,1)} async-done(((bf16[224,1024]{1,0:T(8,128)(2,1)}), bf16[3584,1024]{1,0:T(8,128)(2,1)}) %all-gather.2.cloned.1.call-update) | async-done | bytes 7340048 | tf_op jit(solution)/shard_map/all_gather | solution.py:86
  139.0 0.8 collective-permute-start
  139.8 5.0 %all-to-all-start.2 = ((bf16[16,600,128]{2,1,0:T(8,128)(2,1)}), bf16[16,600,128]{2,1,0:T(8,128)(2,1)S(1)}, u32[]{:S(2)}, u32[]{:S(2)}) async-start(bf16[16,600,128]{2,1,0:T(8,128)(2,1)} %bitcast.121), calls=%async_computation.2 | async-start | bytes 4915200 | tf_op jit(solution)/shard_map/all_to_all | solution.py:54
  145.1 0.8 gather_fusion.7
  145.9 0.8 gather_fusion.11
  147.1 0.6 gather_fusion.3
  148.1 6.3 %select_reduce_fusion.2 = s32[16,224]{1,0:T(8,128)S(1)} fusion(s32[16,4,128]{2,1,0:T(4,128)S(1)} %broadcast_select_fusion.2, s32[16,4,224]{2,1,0:T(4,128)S(1)} %subtract_add_fusion, pred[16,4,224]{2,1,0:T(4,128)(4,1)S(1)} %fusion.8), kind=kLoop, calls=%fused_computation.18 | loop fusion | flops 7336448 | bytes 118784 | tf_op jit(solution)/shard_map/reduce_sum | solution.py:108
  154.6 0.8 gather_fusion
  155.4 2.4 iota_compare_fusion.2
  157.8 20.2 %all-to-all-done.2 = bf16[16,600,128]{2,1,0:T(8,128)(2,1)S(1)} async-done(((bf16[16,600,128]{2,1,0:T(8,128)(2,1)}), bf16[16,600,128]{2,1,0:T(8,128)(2,1)S(1)}, u32[]{:S(2)}, u32[]{:S(2)}) %all-to-all-start.2) | async-done | bytes 2457632 | tf_op jit(solution)/shard_map/all_to_all | solution.py:54
  178.4 6.9 %fusion.5 = f32[3584,600]{0,1:T(8,128)S(1)} fusion(bf16[3584,1024]{1,0:T(8,128)(2,1)} %all-gather.2.cloned.1.call-done, bf16[600,2048]{1,0:T(8,128)(2,1)S(1)} %copy_bitcast_fusion, s32[]{:T(128)S(6)} %select_n.164), kind=kOutput, calls=%fused_computation.30 | convolution fusion | flops 4404019200 | bytes 17170436 | tf_op jit(solution)/shard_map/dot_general | solution.py:93
  185.3 10.0 %fusion.34 = (f32[3584]{0:T(1024)S(1)}, f32[3584,600]{0,1:T(8,128)}) fusion(f32[3584,600]{0,1:T(8,128)S(1)} %fusion.5, bf16[3584,1024]{1,0:T(8,128)(2,1)} %collective-permute-done, bf16[600,2048]{1,0:T(8,128)(2,1)S(1)} %copy_bitcast_fusion, s32[]{:T(128)S(6)} %select_n.182), kind=kOutput, calls=%fused_computation.149 | convolution fusion | flops 4408316416 | bytes 25786372 | tf_op jit(solution)/shard_map/dot_general | solution.py:94
  195.4 5.2 %exponential_reduce_fusion = (f32[3584]{0:T(1024)S(1)}, f32[3584]{0:T(1024)S(1)}, f32[3584]{0:T(1024)S(1)}) fusion(f32[3584,600]{0,1:T(8,128)} %get-tuple-element.56, f32[3584]{0:T(1024)S(1)} %get-tuple-element.55, s32[3584]{0:T(1024)S(1)} %sub.122), kind=kLoop, calls=%fused_computation.14 | loop fusion | flops 15042048 | bytes 8673280 | tf_op jit(solution)/shard_map/reduce_sum | solution.py:113
  201.0 0.7 gather_fusion.4
  202.0 8.9 %select_reduce_fusion = f32[4,64,128]{2,1,0:T(8,128)S(1)} fusion(f32[4,64,224]{2,1,0:T(8,128)S(1)} %copy.182, pred[64,128,224]{1,2,0:T(8,128)(4,1)S(1)} %copy-done.1), kind=kLoop, calls=%fused_computation.12 | loop fusion | flops 14647296 | bytes 2195456 | tf_op jit(solution)/shard_map/reduce_sum | solution.py:136
  210.9 0.7 copy.183
  211.6 6.7 %all-to-all-start.3 = ((f32[16,4,4,128]{3,2,1,0:T(4,128)}), f32[16,4,4,128]{3,2,1,0:T(4,128)S(1)}, u32[]{:S(2)}, u32[]{:S(2)}) async-start(f32[16,4,4,128]{3,2,1,0:T(4,128)} %copy.183), calls=%async_computation.3 | async-start | bytes 262144 | tf_op jit(solution)/shard_map/all_to_all | solution.py:138
  218.3 0.6 gather_fusion.5
  219.0 0.6 gather_fusion.6
  219.6 5.4 %all-to-all-done.3 = f32[16,4,4,128]{3,2,1,0:T(4,128)S(1)} async-done(((f32[16,4,4,128]{3,2,1,0:T(4,128)}), f32[16,4,4,128]{3,2,1,0:T(4,128)S(1)}, u32[]{:S(2)}, u32[]{:S(2)}) %all-to-all-start.3) | async-done | bytes 131104 | tf_op jit(solution)/shard_map/all_to_all | solution.py:138
  225.1 0.6 broadcast_in_dim.188
  225.7 7.0 %all-to-all-start.4 = ((f32[8,4,4,128]{3,2,1,0:T(4,128)}), f32[8,4,4,128]{3,2,1,0:T(4,128)S(1)}, u32[]{:S(2)}, u32[]{:S(2)}) async-start(f32[8,4,4,128]{3,2,1,0:T(4,128)} %broadcast_in_dim.188), calls=%async_computation.4 | async-start | bytes 131072 | tf_op jit(solution)/shard_map/all_to_all | solution.py:34
  232.7 4.8 %all-to-all-done.4 = f32[8,4,4,128]{3,2,1,0:T(4,128)S(1)} async-done(((f32[8,4,4,128]{3,2,1,0:T(4,128)}), f32[8,4,4,128]{3,2,1,0:T(4,128)S(1)}, u32[]{:S(2)}, u32[]{:S(2)}) %all-to-all-start.4) | async-done | bytes 65568 | tf_op jit(solution)/shard_map/all_to_all | solution.py:34
  237.6 0.7 subtract_select_fusion
  (92 shorter events, 3.8 us)
Async XLA Ops:
  7.2 4.2 %copy-start = (bf16[4,128,2048]{2,1,0:T(8,128)(2,1)S(1)}, bf16[4,128,2048]{2,1,0:T(8,128)(2,1)}, u32[]{:S(2)}) copy-start(bf16[4,128,2048]{2,1,0:T(8,128)(2,1)} %param.15) | copy-start | bytes 6291460
  7.2 4.7 %copy-start.3 = (s32[4,128]{1,0:T(4,128)S(1)}, s32[4,128]{1,0:T(4,128)}, u32[]{:S(2)}) copy-start(s32[4,128]{1,0:T(4,128)} %param.18) | copy-start | bytes 6148
  7.2 4.8 %copy-start.4 = (s32[4]{0:T(128)S(1)}, s32[4]{0:T(128)}, u32[]{:S(2)}) copy-start(s32[4]{0:T(128)} %param.19) | copy-start | bytes 52
  7.2 4.9 %copy-start.5 = (s32[4]{0:T(128)S(1)}, s32[4]{0:T(128)}, u32[]{:S(2)}) copy-start(s32[4]{0:T(128)} %param.20) | copy-start | bytes 52
  7.2 6.4 %copy-start.2 = (f32[2048]{0:T(1024)S(1)}, f32[2048]{0:T(1024)}, u32[]{:S(2)}) copy-start(f32[2048]{0:T(1024)} %param.16) | copy-start | bytes 24580
  15.6 10.1 %copy-start.6 = (s32[64]{0:T(128)S(1)}, s32[64]{0:T(128)}, u32[]{:S(2)}) copy-start(s32[64]{0:T(128)} %param.21) | copy-start | bytes 772
  18.1 24.6 %all-to-all-start = ((bf16[4,144,1024]{2,0,1:T(4,128)(2,1)}), bf16[4,144,1024]{2,0,1:T(4,128)(2,1)S(1)}, u32[]{:S(2)}, u32[]{:S(2)}) async-start(bf16[4,144,1024]{2,0,1:T(4,128)(2,1)} %bitcast.8), calls=%async_computation | async-start | bytes 2359296 | tf_op jit(solution)/shard_map/all_to_all | solution.py:68
  50.5 18.7 %all-to-all-start.1 = ((bf16[64,8,1024]{2,1,0:T(8,128)(2,1)}), bf16[64,8,1024]{2,1,0:T(8,128)(2,1)S(1)}, u32[]{:S(2)}, u32[]{:S(2)}) async-start(bf16[64,8,1024]{2,1,0:T(8,128)(2,1)} %broadcast_select_fusion), calls=%async_computation.1 | async-start | bytes 2097152 | tf_op jit(solution)/shard_map/all_to_all | solution.py:75
  54.7 84.3 %all-gather.2.cloned.1.call-start = ((), (), s32[]{:S(2)}) async-start(), calls=%async_computation.5 | async-start | bytes 7798784 | tf_op jit(solution)/shard_map/all_gather | solution.py:86
  139.0 46.3 %collective-permute-start = (bf16[3584,1024]{1,0:T(8,128)(2,1)}, bf16[3584,1024]{1,0:T(8,128)(2,1)}, u32[]{:S(2)}, u32[]{:S(2)}) collective-permute-start(bf16[3584,1024]{1,0:T(8,128)(2,1)} %all-gather.2.cloned.1.call-done), channel_id=1, source_target_pairs={{0,1},{1,0},{2,3},{3,2},{4,5},{5,4},{6,7},{7,6},{8,9},{9,8},{10,11... | collective-permute-start | bytes 22020104 | tf_op jit(solution)/shard_map/ppermute | solution.py:88
  139.8 38.2 %all-to-all-start.2 = ((bf16[16,600,128]{2,1,0:T(8,128)(2,1)}), bf16[16,600,128]{2,1,0:T(8,128)(2,1)S(1)}, u32[]{:S(2)}, u32[]{:S(2)}) async-start(bf16[16,600,128]{2,1,0:T(8,128)(2,1)} %bitcast.121), calls=%async_computation.2 | async-start | bytes 4915200 | tf_op jit(solution)/shard_map/all_to_all | solution.py:54
  195.4 6.5 %copy-start.1 = (pred[64,128,224]{1,2,0:T(8,128)(4,1)S(1)}, pred[64,128,224]{1,2,0:T(8,128)(4,1)}, u32[]{:S(2)}) copy-start(pred[64,128,224]{1,2,0:T(8,128)(4,1)} %iota_compare_fusion.2) | copy-start | bytes 5505028
  211.6 13.4 %all-to-all-start.3 = ((f32[16,4,4,128]{3,2,1,0:T(4,128)}), f32[16,4,4,128]{3,2,1,0:T(4,128)S(1)}, u32[]{:S(2)}, u32[]{:S(2)}) async-start(f32[16,4,4,128]{3,2,1,0:T(4,128)} %copy.183), calls=%async_computation.3 | async-start | bytes 262144 | tf_op jit(solution)/shard_map/all_to_all | solution.py:138
  225.7 11.8 %all-to-all-start.4 = ((f32[8,4,4,128]{3,2,1,0:T(4,128)}), f32[8,4,4,128]{3,2,1,0:T(4,128)S(1)}, u32[]{:S(2)}, u32[]{:S(2)}) async-start(f32[8,4,4,128]{3,2,1,0:T(4,128)} %broadcast_in_dim.188), calls=%async_computation.4 | async-start | bytes 131072 | tf_op jit(solution)/shard_map/all_to_all | solution.py:34
Sparse Core Ops, SparseCore 0:
  71.4 67.5 all-gather.1

commit v6 on v5

--- a/solution.py
+++ b/solution.py
@@ -51,7 +51,17 @@
         jnp.where(deal_order[None, :] == positions[:, None], positions[None, :], 0), axis=1
     )
 
-    emb_piece = lax.all_to_all(embedding, "req", split_axis=0, concat_axis=1, tiled=True)
+    emb_chunks = embedding.reshape(n_req, piece, embedding.shape[1])
+    by_source = [lax.dynamic_index_in_dim(emb_chunks, here, keepdims=False)]
+    for shift in range(1, n_req):
+        outgoing = lax.dynamic_index_in_dim(emb_chunks, (here + shift) % n_req, keepdims=False)
+        perm = [(i, (i + shift) % n_req) for i in range(n_req)]
+        by_source.append(lax.ppermute(outgoing, "req", perm))
+    stacked = jnp.stack(by_source)
+    order = (here - jnp.arange(n_req, dtype=jnp.int32)) % n_req
+    emb_piece = (
+        jnp.zeros_like(stacked).at[order].set(stacked).transpose(1, 0, 2).reshape(piece, width)
+    )
 
     normed_home = normalize(hidden, gain)
     my_half = lax.dynamic_slice_in_dim(normed_home, core * half, half, axis=2)

time: 246 us -> 259 us (1.053)
  waiting for transfers between devices: 127 us -> 103 us
  local copies, waits for them, and re-layouts: 18.9 us -> 37.6 us
  starting transfers between devices: 31.3 us -> 46.6 us
    ppermute x0 -> x15, starting transfers between devices: none -> 20.9 us  [shards(): by_source.append(lax.ppermute(outgoing, 'req', perm))]
    all_to_all x1 -> x0, waiting for transfers between devices: 20.2 us -> none  [shards(): lax.all_to_all(embedding, 'req', split_axis=0, concat_axis=1, tiled=True)]
    all_gather x1, waiting for transfers between devices: 67.8 us -> 51.2 us  [shards(): rows_mine = lax.all_gather(compact_half, 'req', axis=0, tiled=True)]
    ppermute x0 -> x15, waiting for transfers between devices: none -> 14.7 us  [shards(): by_source.append(lax.ppermute(outgoing, 'req', perm))]
    unnamed x15 -> x51, local copies, waits for them, and re-layouts: 0.61 us -> 10.2 us
    all_to_all x1 -> x0, starting transfers between devices: 4.98 us -> none  [shards(): lax.all_to_all(embedding, 'req', split_axis=0, concat_axis=1, tiled=True)]
    scatter x0 -> x1, local copies, waits for them, and re-layouts: none -> 3.75 us  [shards(): jnp.zeros_like(stacked).at[order].set(stacked).transpose(1, 0, 2)]
  transfers between devices with their start and end apart: 7 -> 21, of which waited for: 6 -> 11; matrix products, arithmetic and copies ran while one was open for 10% -> 17% of each run, Pallas kernels for 0% -> 0%
where the time goes in v6:
time: 259 us; the launch traced here: 258 us
  waiting for transfers between devices  103 us (40%)
  starting transfers between devices  46.6 us (18%)
  other arithmetic  38.4 us (15%)
  local copies, waits for them, and re-layouts  37.6 us (15%)
  matrix products  17.6 us (7%)
  between operations  14.9 us (6%)
    all_gather x1, waiting for transfers between devices, shards(): rows_mine = lax.all_gather(compact_half, 'req', axis=0, tiled=True)  51.2 us
    ppermute x15, starting transfers between devices, shards(): by_source.append(lax.ppermute(outgoing, 'req', perm))  20.9 us
    all_to_all x1, waiting for transfers between devices, shards(): lax.all_to_all(blocks, 'req', split_axis=1, concat_axis=0, tiled=True)  14.8 us
    ppermute x15, waiting for transfers between devices, shards(): by_source.append(lax.ppermute(outgoing, 'req', perm))  14.7 us
    all_to_all x1, waiting for transfers between devices, shards(): lax.all_to_all(dealt_rows, 'req', split_axis=0, concat_axis=1, tiled=True)  12.3 us
    unnamed x51, local copies, waits for them, and re-layouts  10.2 us
    dot_general x1, matrix products, shards(): lax.dot_general(rows_other, emb_other, dims, preferred_element_type=jnp.f...  10.2 us
    reduce_sum x1, other arithmetic, shards(): jnp.sum(jnp.where(pick[None], request_rows[:, :, None, :], 0.0), axis=3)  8.94 us
  transfers between devices with their start and end apart: 21, of which 11 were waited for; matrix products, arithmetic and copies ran while one was open for 17% of the time, Pallas kernels for 0%

profile of v6, /device:TPU:1, one launch (start us, length us, event | category | flops | bytes accessed | tf_op | source)
XLA Modules:
  0.0 258.4 jit_solution(14471191142234279652)
XLA Ops:
  7.2 4.2 %convert_element_type.30 = f32[4,128,2048]{2,1,0:T(8,128)} convert(bf16[4,128,2048]{2,1,0:T(8,128)(2,1)} %param.15) | non-fusion elementwise | flops 1048576 | bytes 6291456 | tf_op jit(solution)/shard_map/convert_element_type | solution.py:27
  13.6 1.8 fusion.7
  16.0 2.1 copy.174
  18.1 7.6 %all-to-all-start = ((bf16[4,144,1024]{2,0,1:T(4,128)(2,1)}), bf16[4,144,1024]{2,0,1:T(4,128)(2,1)S(1)}, u32[]{:S(2)}, u32[]{:S(2)}) async-start(bf16[4,144,1024]{2,0,1:T(4,128)(2,1)} %bitcast.8), calls=%async_computation | async-start | bytes 2359296 | tf_op jit(solution)/shard_map/all_to_all | solution.py:78
  27.8 14.8 %all-to-all-done = bf16[4,144,1024]{2,0,1:T(4,128)(2,1)S(1)} async-done(((bf16[4,144,1024]{2,0,1:T(4,128)(2,1)}), bf16[4,144,1024]{2,0,1:T(4,128)(2,1)S(1)}, u32[]{:S(2)}, u32[]{:S(2)}) %all-to-all-start) | async-done | bytes 1179680 | tf_op jit(solution)/shard_map/all_to_all | solution.py:78
  43.7 2.4 slice_reduce_fusion.2
  49.4 1.1 broadcast_select_fusion
  50.6 4.1 %all-to-all-start.1 = ((bf16[64,8,1024]{2,1,0:T(8,128)(2,1)}), bf16[64,8,1024]{2,1,0:T(8,128)(2,1)S(1)}, u32[]{:S(2)}, u32[]{:S(2)}) async-start(bf16[64,8,1024]{2,1,0:T(8,128)(2,1)} %broadcast_select_fusion), calls=%async_computation.1 | async-start | bytes 2097152 | tf_op jit(solution)/shard_map/all_to_all | solution.py:85
  56.9 12.3 %all-to-all-done.1 = bf16[64,8,1024]{2,1,0:T(8,128)(2,1)S(1)} async-done(((bf16[64,8,1024]{2,1,0:T(8,128)(2,1)}), bf16[64,8,1024]{2,1,0:T(8,128)(2,1)S(1)}, u32[]{:S(2)}, u32[]{:S(2)}) %all-to-all-start.1) | async-done | bytes 1048608 | tf_op jit(solution)/shard_map/all_to_all | solution.py:85
  69.3 1.9 gather_fusion.2
  71.2 1.9 broadcast_select_fusion.1
  73.3 1.4 dynamic-slice_bitcast_fusion
  74.8 1.4 collective-permute-start.1
  76.2 1.3 collective-permute-start.2
  77.5 1.0 collective-permute-start.3
  78.5 2.0 collective-permute-start.4
  81.6 1.9 collective-permute-done
  84.2 3.1 %collective-permute-start.6 = (bf16[600,128]{1,0:T(8,128)(2,1)}, bf16[600,128]{1,0:T(8,128)(2,1)S(1)}, u32[]{:S(2)}, u32[]{:S(2)}) collective-permute-start(bf16[600,128]{1,0:T(8,128)(2,1)} %get-tuple-element.51), channel_id=1, source_target_pairs={{0,56},{8,64},{16,72},{24,80},{32,88},{40,96},{48,104},{56,112},{6... | collective-permute-start | bytes 460808 | tf_op jit(solution)/shard_map/ppermute | solution.py:59
  88.0 2.0 collective-permute-start.7
  90.7 0.8 collective-permute-start.8
  92.1 4.6 %collective-permute-done.4 = bf16[600,128]{1,0:T(8,128)(2,1)S(1)} collective-permute-done((bf16[600,128]{1,0:T(8,128)(2,1)}, bf16[600,128]{1,0:T(8,128)(2,1)S(1)}, u32[]{:S(2)}, u32[]{:S(2)}) %collective-permute-start.4) | collective-permute-done | bytes 153632 | tf_op jit(solution)/shard_map/ppermute | solution.py:59
  97.5 2.6 collective-permute-done.5
  100.1 51.2 %all-gather.2.cloned.1.call-done = bf16[3584,1024]{1,0:T(8,128)(2,1)} async-done(((bf16[224,1024]{1,0:T(8,128)(2,1)}), bf16[3584,1024]{1,0:T(8,128)(2,1)}) %all-gather.2.cloned.1.call-update) | async-done | bytes 7340048 | tf_op jit(solution)/shard_map/all_gather | solution.py:96
  151.3 0.8 collective-permute-start.15
  152.8 3.3 %collective-permute-start.10 = (bf16[600,128]{1,0:T(8,128)(2,1)S(1)}, bf16[600,128]{1,0:T(8,128)(2,1)S(1)}, u32[]{:S(2)}, u32[]{:S(2)}) collective-permute-start(bf16[600,128]{1,0:T(8,128)(2,1)S(1)} %get-tuple-element.47), channel_id=1, source_target_pairs={{0,88},{8,96},{16,104},{24,112},{32,120},{40,0},{48,8},{56,16},{64... | collective-permute-start | bytes 460808 | tf_op jit(solution)/shard_map/ppermute | solution.py:59
  156.7 1.2 collective-permute-start.11
  159.3 2.3 collective-permute-start.13
  162.3 2.3 collective-permute-start.14
  166.7 2.6 %collective-permute-done.13 = bf16[600,128]{1,0:T(8,128)(2,1)S(1)} collective-permute-done((bf16[600,128]{1,0:T(8,128)(2,1)S(1)}, bf16[600,128]{1,0:T(8,128)(2,1)S(1)}, u32[]{:S(2)}, u32[]{:S(2)}) %collective-permute-start.13) | collective-permute-done | bytes 153632 | tf_op jit(solution)/shard_map/ppermute | solution.py:59
  170.0 2.9 %collective-permute-done.14 = bf16[600,128]{1,0:T(8,128)(2,1)S(1)} collective-permute-done((bf16[600,128]{1,0:T(8,128)(2,1)S(1)}, bf16[600,128]{1,0:T(8,128)(2,1)S(1)}, u32[]{:S(2)}, u32[]{:S(2)}) %collective-permute-start.14) | collective-permute-done | bytes 153632 | tf_op jit(solution)/shard_map/ppermute | solution.py:59
  173.9 3.7 %scatter_fusion = bf16[16,600,128]{2,1,0:T(8,128)(2,1)S(1)} fusion(bf16[16,600,128]{2,1,0:T(8,128)(2,1)S(1)} %broadcast_in_dim.183, s32[16]{0:T(128)} %fusion.31, bf16[16,600,128]{2,1,0:T(8,128)(2,1)} %bitcast_dynamic-update-slice_fusion), kind=kCustom, calls=%fused_computation.12 | custom fusion | bytes 7372864 | tf_op jit(solution)/shard_map/scatter | solution.py:63
  177.7 1.9 copy_bitcast_fusion
  179.5 0.8 gather_fusion.7
  180.3 0.8 gather_fusion.11
  182.8 6.3 %select_reduce_fusion.2 = s32[16,224]{1,0:T(8,128)S(1)} fusion(s32[16,4,128]{2,1,0:T(4,128)S(1)} %broadcast_select_fusion.2, s32[16,4,224]{2,1,0:T(4,128)S(1)} %subtract_add_fusion, pred[16,4,224]{2,1,0:T(4,128)(4,1)S(1)} %fusion.8), kind=kLoop, calls=%fused_computation.19 | loop fusion | flops 7336448 | bytes 118784 | tf_op jit(solution)/shard_map/reduce_sum | solution.py:118
  189.2 0.9 gather_fusion
  190.2 1.2 iota_compare_fusion.2
  191.4 7.4 %fusion.5 = f32[3584,600]{0,1:T(8,128)S(1)} fusion(bf16[3584,1024]{1,0:T(8,128)(2,1)} %all-gather.2.cloned.1.call-done, bf16[600,2048]{1,0:T(8,128)(2,1)} %copy_bitcast_fusion, s32[]{:T(128)S(6)} %select_n.296), kind=kOutput, calls=%fused_computation.31 | convolution fusion | flops 4404019200 | bytes 17170436 | tf_op jit(solution)/shard_map/dot_general | solution.py:103
  198.8 10.2 %fusion.36 = (f32[3584]{0:T(1024)S(1)}, f32[3584,600]{0,1:T(8,128)}) fusion(f32[3584,600]{0,1:T(8,128)S(1)} %fusion.5, bf16[3584,1024]{1,0:T(8,128)(2,1)} %collective-permute-done.15, bf16[600,2048]{1,0:T(8,128)(2,1)S(1)} %copy-done.2, s32[]{:T(128)S(6)} %select_n.347), kind=kOutput, calls=%fused_computation.187 | convolution fusion | flops 4408316416 | bytes 25786372 | tf_op jit(solution)/shard_map/dot_general | solution.py:104
  209.1 5.1 %exponential_reduce_fusion = (f32[3584]{0:T(1024)S(1)}, f32[3584]{0:T(1024)S(1)}, f32[3584]{0:T(1024)S(1)}) fusion(f32[3584,600]{0,1:T(8,128)} %get-tuple-element.72, f32[3584]{0:T(1024)S(1)} %get-tuple-element.71, s32[3584]{0:T(1024)S(1)} %sub.137), kind=kLoop, calls=%fused_computation.15 | loop fusion | flops 15042048 | bytes 8673280 | tf_op jit(solution)/shard_map/reduce_sum | solution.py:123
  214.6 0.8 gather_fusion.4
  215.6 8.9 %select_reduce_fusion = f32[4,64,128]{2,1,0:T(8,128)S(1)} fusion(f32[4,64,224]{2,1,0:T(8,128)S(1)} %copy.182, pred[64,128,224]{1,2,0:T(8,128)(4,1)S(1)} %iota_compare_fusion.2), kind=kLoop, calls=%fused_computation.13 | loop fusion | flops 14647296 | bytes 2195456 | tf_op jit(solution)/shard_map/reduce_sum | solution.py:146
  225.3 6.9 %all-to-all-start.2 = ((f32[16,4,4,128]{3,2,1,0:T(4,128)}), f32[16,4,4,128]{3,2,1,0:T(4,128)S(1)}, u32[]{:S(2)}, u32[]{:S(2)}) async-start(f32[16,4,4,128]{3,2,1,0:T(4,128)} %copy.183), calls=%async_computation.2 | async-start | bytes 262144 | tf_op jit(solution)/shard_map/all_to_all | solution.py:148
  232.2 0.8 gather_fusion.5
  232.9 0.8 gather_fusion.6
  233.7 5.3 %all-to-all-done.2 = f32[16,4,4,128]{3,2,1,0:T(4,128)S(1)} async-done(((f32[16,4,4,128]{3,2,1,0:T(4,128)}), f32[16,4,4,128]{3,2,1,0:T(4,128)S(1)}, u32[]{:S(2)}, u32[]{:S(2)}) %all-to-all-start.2) | async-done | bytes 131104 | tf_op jit(solution)/shard_map/all_to_all | solution.py:148
  239.7 6.2 %all-to-all-start.3 = ((f32[8,4,4,128]{3,2,1,0:T(4,128)}), f32[8,4,4,128]{3,2,1,0:T(4,128)S(1)}, u32[]{:S(2)}, u32[]{:S(2)}) async-start(f32[8,4,4,128]{3,2,1,0:T(4,128)} %broadcast_in_dim.193), calls=%async_computation.3 | async-start | bytes 131072 | tf_op jit(solution)/shard_map/all_to_all | solution.py:34
  246.0 4.8 %all-to-all-done.3 = f32[8,4,4,128]{3,2,1,0:T(4,128)S(1)} async-done(((f32[8,4,4,128]{3,2,1,0:T(4,128)}), f32[8,4,4,128]{3,2,1,0:T(4,128)S(1)}, u32[]{:S(2)}, u32[]{:S(2)}) %all-to-all-start.3) | async-done | bytes 65568 | tf_op jit(solution)/shard_map/all_to_all | solution.py:34
  (159 shorter events, 27.6 us)
Async XLA Ops:
  7.2 4.2 %copy-start = (bf16[4,128,2048]{2,1,0:T(8,128)(2,1)S(1)}, bf16[4,128,2048]{2,1,0:T(8,128)(2,1)}, u32[]{:S(2)}) copy-start(bf16[4,128,2048]{2,1,0:T(8,128)(2,1)} %param.15) | copy-start | bytes 6291460
  7.2 4.7 %copy-start.11 = (s32[4,128]{1,0:T(4,128)S(1)}, s32[4,128]{1,0:T(4,128)}, u32[]{:S(2)}) copy-start(s32[4,128]{1,0:T(4,128)} %param.18) | copy-start | bytes 6148
  7.2 4.8 %copy-start.13 = (s32[4]{0:T(128)S(1)}, s32[4]{0:T(128)}, u32[]{:S(2)}) copy-start(s32[4]{0:T(128)} %param.19) | copy-start | bytes 52
  7.2 4.9 %copy-start.14 = (s32[4]{0:T(128)S(1)}, s32[4]{0:T(128)}, u32[]{:S(2)}) copy-start(s32[4]{0:T(128)} %param.20) | copy-start | bytes 52
  7.2 6.4 %copy-start.10 = (f32[2048]{0:T(1024)S(1)}, f32[2048]{0:T(1024)}, u32[]{:S(2)}) copy-start(f32[2048]{0:T(1024)} %param.16) | copy-start | bytes 24580
  16.0 9.7 %copy-start.15 = (s32[64]{0:T(128)S(1)}, s32[64]{0:T(128)}, u32[]{:S(2)}) copy-start(s32[64]{0:T(128)} %param.21) | copy-start | bytes 772
  18.1 24.6 %all-to-all-start = ((bf16[4,144,1024]{2,0,1:T(4,128)(2,1)}), bf16[4,144,1024]{2,0,1:T(4,128)(2,1)S(1)}, u32[]{:S(2)}, u32[]{:S(2)}) async-start(bf16[4,144,1024]{2,0,1:T(4,128)(2,1)} %bitcast.8), calls=%async_computation | async-start | bytes 2359296 | tf_op jit(solution)/shard_map/all_to_all | solution.py:78
  25.9 16.8 %copy-start.6 = (s32[16,4]{1,0:T(8,128)}, s32[16,4]{1,0:T(8,128)S(1)}, u32[]{:S(2)}) copy-start(s32[16,4]{1,0:T(8,128)S(1)} %reshape.365) | copy-start | bytes 772
  26.0 17.5 %copy-start.8 = (s32[1024]{0:T(1024)}, s32[1024]{0:T(1024)S(1)}, u32[]{:S(2)}) copy-start(s32[1024]{0:T(1024)S(1)} %pad_clamp_fusion.6) | copy-start | bytes 12292
  27.3 21.5 %copy-start.9 = (s32[1024]{0:T(1024)}, s32[1024]{0:T(1024)S(1)}, u32[]{:S(2)}) copy-start(s32[1024]{0:T(1024)S(1)} %get-tuple-element.75) | copy-start | bytes 12292
  43.7 3.9 %copy-start.3 = (s32[64,4,128]{2,1,0:T(4,128)}, s32[64,4,128]{2,1,0:T(4,128)S(1)}, u32[]{:S(2)}) copy-start(s32[64,4,128]{2,1,0:T(4,128)S(1)} %reshape.373) | copy-start | bytes 393220
  50.6 18.7 %all-to-all-start.1 = ((bf16[64,8,1024]{2,1,0:T(8,128)(2,1)}), bf16[64,8,1024]{2,1,0:T(8,128)(2,1)S(1)}, u32[]{:S(2)}, u32[]{:S(2)}) async-start(bf16[64,8,1024]{2,1,0:T(8,128)(2,1)} %broadcast_select_fusion), calls=%async_computation.1 | async-start | bytes 2097152 | tf_op jit(solution)/shard_map/all_to_all | solution.py:85
  54.7 96.5 %all-gather.2.cloned.1.call-start = ((), (), s32[]{:S(2)}) async-start(), calls=%async_computation.4 | async-start | bytes 7798784 | tf_op jit(solution)/shard_map/all_gather | solution.py:96
  69.3 4.0 %copy-start.1 = (bf16[9600,128]{1,0:T(8,128)(2,1)S(1)}, bf16[9600,128]{1,0:T(8,128)(2,1)}, u32[]{:S(2)}) copy-start(bf16[9600,128]{1,0:T(8,128)(2,1)} %param.17) | copy-start | bytes 7372804
  73.3 7.2 %copy-start.16 = (s32[64]{0:T(128)S(1)}, s32[64]{0:T(128)}, u32[]{:S(2)}) copy-start(s32[64]{0:T(128)} %param.21) | copy-start | bytes 772
  74.7 8.8 %collective-permute-start = (bf16[600,128]{1,0:T(8,128)(2,1)}, bf16[600,128]{1,0:T(8,128)(2,1)S(1)}, u32[]{:S(2)}, u32[]{:S(2)}) collective-permute-start(bf16[600,128]{1,0:T(8,128)(2,1)} %get-tuple-element.57), channel_id=1, source_target_pairs={{0,8},{8,16},{16,24},{24,32},{32,40},{40,48},{48,56},{56,64},{64,7... | collective-permute-start | bytes 460808 | tf_op jit(solution)/shard_map/ppermute | solution.py:59
  74.8 9.4 %collective-permute-start.1 = (bf16[600,128]{1,0:T(8,128)(2,1)}, bf16[600,128]{1,0:T(8,128)(2,1)S(1)}, u32[]{:S(2)}, u32[]{:S(2)}) collective-permute-start(bf16[600,128]{1,0:T(8,128)(2,1)} %get-tuple-element.56), channel_id=1, source_target_pairs={{0,16},{8,24},{16,32},{24,40},{32,48},{40,56},{48,64},{56,72},{64,... | collective-permute-start | bytes 460808 | tf_op jit(solution)/shard_map/ppermute | solution.py:59
  76.2 11.8 %collective-permute-start.2 = (bf16[600,128]{1,0:T(8,128)(2,1)}, bf16[600,128]{1,0:T(8,128)(2,1)S(1)}, u32[]{:S(2)}, u32[]{:S(2)}) collective-permute-start(bf16[600,128]{1,0:T(8,128)(2,1)} %get-tuple-element.55), channel_id=1, source_target_pairs={{0,24},{8,32},{16,40},{24,48},{32,56},{40,64},{48,72},{56,80},{64,... | collective-permute-start | bytes 460808 | tf_op jit(solution)/shard_map/ppermute | solution.py:59
  77.5 13.1 %collective-permute-start.3 = (bf16[600,128]{1,0:T(8,128)(2,1)}, bf16[600,128]{1,0:T(8,128)(2,1)S(1)}, u32[]{:S(2)}, u32[]{:S(2)}) collective-permute-start(bf16[600,128]{1,0:T(8,128)(2,1)} %get-tuple-element.54), channel_id=1, source_target_pairs={{0,32},{8,40},{16,48},{24,56},{32,64},{40,72},{48,80},{56,88},{64,... | collective-permute-start | bytes 460808 | tf_op jit(solution)/shard_map/ppermute | solution.py:59
  78.5 18.3 %collective-permute-start.4 = (bf16[600,128]{1,0:T(8,128)(2,1)}, bf16[600,128]{1,0:T(8,128)(2,1)S(1)}, u32[]{:S(2)}, u32[]{:S(2)}) collective-permute-start(bf16[600,128]{1,0:T(8,128)(2,1)} %get-tuple-element.53), channel_id=1, source_target_pairs={{0,40},{8,48},{16,56},{24,64},{32,72},{40,80},{48,88},{56,96},{64,... | collective-permute-start | bytes 460808 | tf_op jit(solution)/shard_map/ppermute | solution.py:59
  83.5 16.6 %collective-permute-start.5 = (bf16[600,128]{1,0:T(8,128)(2,1)}, bf16[600,128]{1,0:T(8,128)(2,1)S(1)}, u32[]{:S(2)}, u32[]{:S(2)}) collective-permute-start(bf16[600,128]{1,0:T(8,128)(2,1)} %get-tuple-element.52), channel_id=1, source_target_pairs={{0,48},{8,56},{16,64},{24,72},{32,80},{40,88},{48,96},{56,104},{64... | collective-permute-start | bytes 460808 | tf_op jit(solution)/shard_map/ppermute | solution.py:59
  84.2 68.5 %collective-permute-start.6 = (bf16[600,128]{1,0:T(8,128)(2,1)}, bf16[600,128]{1,0:T(8,128)(2,1)S(1)}, u32[]{:S(2)}, u32[]{:S(2)}) collective-permute-start(bf16[600,128]{1,0:T(8,128)(2,1)} %get-tuple-element.51), channel_id=1, source_target_pairs={{0,56},{8,64},{16,72},{24,80},{32,88},{40,96},{48,104},{56,112},{6... | collective-permute-start | bytes 460808 | tf_op jit(solution)/shard_map/ppermute | solution.py:59
  88.0 68.8 %collective-permute-start.7 = (bf16[600,128]{1,0:T(8,128)(2,1)}, bf16[600,128]{1,0:T(8,128)(2,1)S(1)}, u32[]{:S(2)}, u32[]{:S(2)}) collective-permute-start(bf16[600,128]{1,0:T(8,128)(2,1)} %get-tuple-element.50), channel_id=1, source_target_pairs={{0,64},{8,72},{16,80},{24,88},{32,96},{40,104},{48,112},{56,120},{... | collective-permute-start | bytes 460808 | tf_op jit(solution)/shard_map/ppermute | solution.py:59
  90.7 67.9 %collective-permute-start.8 = (bf16[600,128]{1,0:T(8,128)(2,1)S(1)}, bf16[600,128]{1,0:T(8,128)(2,1)S(1)}, u32[]{:S(2)}, u32[]{:S(2)}) collective-permute-start(bf16[600,128]{1,0:T(8,128)(2,1)S(1)} %get-tuple-element.49), channel_id=1, source_target_pairs={{0,72},{8,80},{16,88},{24,96},{32,104},{40,112},{48,120},{56,0},{6... | collective-permute-start | bytes 460808 | tf_op jit(solution)/shard_map/ppermute | solution.py:59
  96.8 62.5 %collective-permute-start.9 = (bf16[600,128]{1,0:T(8,128)(2,1)S(1)}, bf16[600,128]{1,0:T(8,128)(2,1)S(1)}, u32[]{:S(2)}, u32[]{:S(2)}) collective-permute-start(bf16[600,128]{1,0:T(8,128)(2,1)S(1)} %get-tuple-element.48), channel_id=1, source_target_pairs={{0,80},{8,88},{16,96},{24,104},{32,112},{40,120},{48,0},{56,8},{64... | collective-permute-start | bytes 460808 | tf_op jit(solution)/shard_map/ppermute | solution.py:59
  151.3 47.6 %collective-permute-start.15 = (bf16[3584,1024]{1,0:T(8,128)(2,1)}, bf16[3584,1024]{1,0:T(8,128)(2,1)}, u32[]{:S(2)}, u32[]{:S(2)}) collective-permute-start(bf16[3584,1024]{1,0:T(8,128)(2,1)} %all-gather.2.cloned.1.call-done), channel_id=1, source_target_pairs={{0,1},{1,0},{2,3},{3,2},{4,5},{5,4},{6,7},{7,6},{8,9},{9,8},{10,11... | collective-permute-start | bytes 22020104 | tf_op jit(solution)/shard_map/ppermute | solution.py:98
  152.8 9.5 %collective-permute-start.10 = (bf16[600,128]{1,0:T(8,128)(2,1)S(1)}, bf16[600,128]{1,0:T(8,128)(2,1)S(1)}, u32[]{:S(2)}, u32[]{:S(2)}) collective-permute-start(bf16[600,128]{1,0:T(8,128)(2,1)S(1)} %get-tuple-element.47), channel_id=1, source_target_pairs={{0,88},{8,96},{16,104},{24,112},{32,120},{40,0},{48,8},{56,16},{64... | collective-permute-start | bytes 460808 | tf_op jit(solution)/shard_map/ppermute | solution.py:59
  156.7 8.5 %collective-permute-start.11 = (bf16[600,128]{1,0:T(8,128)(2,1)S(1)}, bf16[600,128]{1,0:T(8,128)(2,1)S(1)}, u32[]{:S(2)}, u32[]{:S(2)}) collective-permute-start(bf16[600,128]{1,0:T(8,128)(2,1)S(1)} %get-tuple-element.46), channel_id=1, source_target_pairs={{0,96},{8,104},{16,112},{24,120},{32,0},{40,8},{48,16},{56,24},{64... | collective-permute-start | bytes 460808 | tf_op jit(solution)/shard_map/ppermute | solution.py:59
  158.6 7.5 %collective-permute-start.12 = (bf16[600,128]{1,0:T(8,128)(2,1)S(1)}, bf16[600,128]{1,0:T(8,128)(2,1)S(1)}, u32[]{:S(2)}, u32[]{:S(2)}) collective-permute-start(bf16[600,128]{1,0:T(8,128)(2,1)S(1)} %get-tuple-element.45), channel_id=1, source_target_pairs={{0,104},{8,112},{16,120},{24,0},{32,8},{40,16},{48,24},{56,32},{64... | collective-permute-start | bytes 460808 | tf_op jit(solution)/shard_map/ppermute | solution.py:59
  159.3 10.1 %collective-permute-start.13 = (bf16[600,128]{1,0:T(8,128)(2,1)S(1)}, bf16[600,128]{1,0:T(8,128)(2,1)S(1)}, u32[]{:S(2)}, u32[]{:S(2)}) collective-permute-start(bf16[600,128]{1,0:T(8,128)(2,1)S(1)} %get-tuple-element.44), channel_id=1, source_target_pairs={{0,112},{8,120},{16,0},{24,8},{32,16},{40,24},{48,32},{56,40},{64,... | collective-permute-start | bytes 460808 | tf_op jit(solution)/shard_map/ppermute | solution.py:59
  162.3 10.6 %collective-permute-start.14 = (bf16[600,128]{1,0:T(8,128)(2,1)S(1)}, bf16[600,128]{1,0:T(8,128)(2,1)S(1)}, u32[]{:S(2)}, u32[]{:S(2)}) collective-permute-start(bf16[600,128]{1,0:T(8,128)(2,1)S(1)} %get-tuple-element.43), channel_id=1, source_target_pairs={{0,120},{8,0},{16,8},{24,16},{32,24},{40,32},{48,40},{56,48},{64,5... | collective-permute-start | bytes 460808 | tf_op jit(solution)/shard_map/ppermute | solution.py:59
  177.7 1.9 copy-start.5
  180.3 0.9 copy-start.4
  180.3 1.8 copy-start.7
  180.3 9.8 %copy-start.17 = (s32[64]{0:T(128)S(1)}, s32[64]{0:T(128)}, u32[]{:S(2)}) copy-start(s32[64]{0:T(128)} %param.21) | copy-start | bytes 772
  191.4 7.5 %copy-start.2 = (bf16[600,2048]{1,0:T(8,128)(2,1)S(1)}, bf16[600,2048]{1,0:T(8,128)(2,1)}, u32[]{:S(2)}) copy-start(bf16[600,2048]{1,0:T(8,128)(2,1)} %copy_bitcast_fusion) | copy-start | bytes 7372804
  209.1 6.3 %copy-start.12 = (pred[64]{0:T(512)(128)(4,1)S(1)}, pred[64]{0:T(512)(128)(4,1)}, u32[]{:S(2)}) copy-start(pred[64]{0:T(512)(128)(4,1)} %get-tuple-element.37) | copy-start | bytes 196
  225.3 13.7 %all-to-all-start.2 = ((f32[16,4,4,128]{3,2,1,0:T(4,128)}), f32[16,4,4,128]{3,2,1,0:T(4,128)S(1)}, u32[]{:S(2)}, u32[]{:S(2)}) async-start(f32[16,4,4,128]{3,2,1,0:T(4,128)} %copy.183), calls=%async_computation.2 | async-start | bytes 262144 | tf_op jit(solution)/shard_map/all_to_all | solution.py:148
  239.7 11.1 %all-to-all-start.3 = ((f32[8,4,4,128]{3,2,1,0:T(4,128)}), f32[8,4,4,128]{3,2,1,0:T(4,128)S(1)}, u32[]{:S(2)}, u32[]{:S(2)}) async-start(f32[8,4,4,128]{3,2,1,0:T(4,128)} %broadcast_in_dim.193), calls=%async_computation.3 | async-start | bytes 131072 | tf_op jit(solution)/shard_map/all_to_all | solution.py:34
Sparse Core Ops, SparseCore 0:
  73.2 77.9 all-gather.1

commit v7 on v5

--- a/solution.py
+++ b/solution.py
@@ -51,7 +51,8 @@
         jnp.where(deal_order[None, :] == positions[:, None], positions[None, :], 0), axis=1
     )
 
-    emb_piece = lax.all_to_all(embedding, "req", split_axis=0, concat_axis=1, tiled=True)
+    emb_blocks = lax.all_to_all(embedding, "req", split_axis=0, concat_axis=0, tiled=True)
+    emb_piece = emb_blocks.reshape(n_req, piece, -1).transpose(1, 0, 2).reshape(piece, width)
 
     normed_home = normalize(hidden, gain)
     my_half = lax.dynamic_slice_in_dim(normed_home, core * half, half, axis=2)
@@ -72,7 +73,7 @@
     all_starts = meta_all[:, 3, 0]
     all_lengths = meta_all[:, 3, 1]
     dealt_rows = jnp.take(spread_rows, source_of, axis=0)
-    home_rows = lax.all_to_all(dealt_rows, "req", split_axis=0, concat_axis=1, tiled=True)
+    home_rows = lax.all_to_all(dealt_rows, "req", split_axis=0, concat_axis=0, tiled=True)
 
     my_slots = here * per_dev + jnp.arange(per_dev, dtype=jnp.int32)
     members = jnp.take(source_of, my_slots)
@@ -81,7 +82,9 @@
     row_base = jnp.arange(per_dev, dtype=jnp.int32) * slot_len + starts
     row_index, in_span = compact_plan(row_base, lengths, CAP)
     safe_index = jnp.where(in_span, row_index, 0)
-    compact_half = jnp.take(home_rows.reshape(per_dev * slot_len, half), safe_index, axis=0)
+    request, position = safe_index // slot_len, safe_index % slot_len
+    block_index = (position // block) * (per_dev * block) + request * block + position % block
+    compact_half = jnp.take(home_rows.reshape(per_dev * slot_len, half), block_index, axis=0)
 
     rows_mine = lax.all_gather(compact_half, "req", axis=0, tiled=True)
     pairs = [(2 * k + j, 2 * k + 1 - j) for k in range(n_voc // 2) for j in range(2)]

time: 246 us -> 246 us (level)
  no operation moved by 1% of the time
where the time goes in v7:
time: 246 us; the launch traced here: 245 us
  waiting for transfers between devices  127 us (52%)
  other arithmetic  36 us (15%)
  starting transfers between devices  31.3 us (13%)
  local copies, waits for them, and re-layouts  18.9 us (8%)
  matrix products  17 us (7%)
  between operations  14.6 us (6%)
    all_gather x1, waiting for transfers between devices, shards(): rows_mine = lax.all_gather(compact_half, 'req', axis=0, tiled=True)  67.8 us
    all_to_all x1, waiting for transfers between devices, shards(): lax.all_to_all(embedding, 'req', split_axis=0, concat_axis=0, tiled=True)  20.2 us
    all_to_all x1, waiting for transfers between devices, shards(): lax.all_to_all(blocks, 'req', split_axis=1, concat_axis=0, tiled=True)  16.1 us
    all_to_all x1, waiting for transfers between devices, shards(): lax.all_to_all(dealt_rows, 'req', split_axis=0, concat_axis=0, tiled=True)  12.9 us
    dot_general x1, matrix products, shards(): lax.dot_general(rows_other, emb_other, dims, preferred_element_type=jnp.f...  10 us
    reduce_sum x1, other arithmetic, shards(): jnp.sum(jnp.where(pick[None], request_rows[:, :, None, :], 0.0), axis=3)  8.94 us
    all_to_all x1, starting transfers between devices, shards(): lax.all_to_all(blocks, 'req', split_axis=1, concat_axis=0, tiled=True)  7.57 us
    all_to_all x1, starting transfers between devices, gather_by_all_to_all(): return lax.all_to_all(tiles, axis, split_axis=0, concat_axis=0, tiled=True)  7.03 us
  transfers between devices with their start and end apart: 7, of which 6 were waited for; matrix products, arithmetic and copies ran while one was open for 10% of the time, Pallas kernels for 0%

profile of v7, /device:TPU:1, one launch (start us, length us, event | category | flops | bytes accessed | tf_op | source)
XLA Modules:
  0.0 245.1 jit_solution(2636089815094111766)
XLA Ops:
  7.2 4.2 %convert_element_type.30 = f32[4,128,2048]{2,1,0:T(8,128)} convert(bf16[4,128,2048]{2,1,0:T(8,128)(2,1)} %param.15) | non-fusion elementwise | flops 1048576 | bytes 6291456 | tf_op jit(solution)/shard_map/convert_element_type | solution.py:27
  11.4 0.5 multiply_reduce_fusion
  12.2 0.6 slice.88
  12.8 0.8 scatter.9
  13.6 1.8 fusion.7
  15.6 0.4 pad_maximum_fusion
  16.0 2.1 copy.166
  18.1 7.6 %all-to-all-start = ((bf16[4,144,1024]{2,0,1:T(4,128)(2,1)}), bf16[4,144,1024]{2,0,1:T(4,128)(2,1)S(1)}, u32[]{:S(2)}, u32[]{:S(2)}) async-start(bf16[4,144,1024]{2,0,1:T(4,128)(2,1)} %bitcast.8), calls=%async_computation | async-start | bytes 2359296 | tf_op jit(solution)/shard_map/all_to_all | solution.py:69
  25.8 0.6 gather_fusion.8
  26.5 16.1 %all-to-all-done = bf16[4,144,1024]{2,0,1:T(4,128)(2,1)S(1)} async-done(((bf16[4,144,1024]{2,0,1:T(4,128)(2,1)}), bf16[4,144,1024]{2,0,1:T(4,128)(2,1)S(1)}, u32[]{:S(2)}, u32[]{:S(2)}) %all-to-all-start) | async-done | bytes 1179680 | tf_op jit(solution)/shard_map/all_to_all | solution.py:69
  42.7 0.5 copy.167
  43.6 2.4 slice_reduce_fusion.2
  46.1 0.6 gather_fusion.9
  46.7 0.6 fusion.34
  47.5 0.6 gather_fusion.10
  48.2 0.6 copy.187
  48.7 0.6 gather_fusion.1
  49.4 1.2 broadcast_select_fusion
  50.5 4.1 %all-to-all-start.1 = ((bf16[64,8,1024]{2,1,0:T(8,128)(2,1)}), bf16[64,8,1024]{2,1,0:T(8,128)(2,1)S(1)}, u32[]{:S(2)}, u32[]{:S(2)}) async-start(bf16[64,8,1024]{2,1,0:T(8,128)(2,1)} %broadcast_select_fusion), calls=%async_computation.1 | async-start | bytes 2097152 | tf_op jit(solution)/shard_map/all_to_all | solution.py:76
  54.9 0.7 compare_select_fusion.1
  55.6 0.7 compare_and_fusion.4
  56.3 12.9 %all-to-all-done.1 = bf16[64,8,1024]{2,1,0:T(8,128)(2,1)S(1)} async-done(((bf16[64,8,1024]{2,1,0:T(8,128)(2,1)}), bf16[64,8,1024]{2,1,0:T(8,128)(2,1)S(1)}, u32[]{:S(2)}, u32[]{:S(2)}) %all-to-all-start.1) | async-done | bytes 1048608 | tf_op jit(solution)/shard_map/all_to_all | solution.py:76
  69.2 1.1 gather_fusion.2
  70.3 0.9 broadcast_select_fusion.1
  71.2 67.8 %all-gather.2.cloned.1.call-done = bf16[3584,1024]{1,0:T(8,128)(2,1)} async-done(((bf16[224,1024]{1,0:T(8,128)(2,1)}), bf16[3584,1024]{1,0:T(8,128)(2,1)}) %all-gather.2.cloned.1.call-update) | async-done | bytes 7340048 | tf_op jit(solution)/shard_map/all_gather | solution.py:89
  138.9 0.8 collective-permute-start
  139.8 5.0 %all-to-all-start.2 = ((bf16[16,600,128]{2,1,0:T(8,128)(2,1)}), bf16[16,600,128]{2,1,0:T(8,128)(2,1)S(1)}, u32[]{:S(2)}, u32[]{:S(2)}) async-start(bf16[16,600,128]{2,1,0:T(8,128)(2,1)} %bitcast.117), calls=%async_computation.2 | async-start | bytes 4915200 | tf_op jit(solution)/shard_map/all_to_all | solution.py:54
  145.0 0.8 gather_fusion.7
  145.8 0.8 gather_fusion.11
  147.0 0.6 gather_fusion.3
  148.0 6.3 %select_reduce_fusion.2 = s32[16,224]{1,0:T(8,128)S(1)} fusion(s32[16,4,128]{2,1,0:T(4,128)S(1)} %broadcast_select_fusion.2, s32[16,4,224]{2,1,0:T(4,128)S(1)} %subtract_add_fusion, pred[16,4,224]{2,1,0:T(4,128)(4,1)S(1)} %fusion.8), kind=kLoop, calls=%fused_computation.18 | loop fusion | flops 7336448 | bytes 118784 | tf_op jit(solution)/shard_map/reduce_sum | solution.py:111
  154.5 0.8 gather_fusion
  155.3 2.4 iota_compare_fusion.2
  157.7 20.2 %all-to-all-done.2 = bf16[16,600,128]{2,1,0:T(8,128)(2,1)S(1)} async-done(((bf16[16,600,128]{2,1,0:T(8,128)(2,1)}), bf16[16,600,128]{2,1,0:T(8,128)(2,1)S(1)}, u32[]{:S(2)}, u32[]{:S(2)}) %all-to-all-start.2) | async-done | bytes 2457632 | tf_op jit(solution)/shard_map/all_to_all | solution.py:54
  178.3 6.9 %fusion.5 = f32[3584,600]{0,1:T(8,128)S(1)} fusion(bf16[3584,1024]{1,0:T(8,128)(2,1)} %all-gather.2.cloned.1.call-done, bf16[600,2048]{1,0:T(8,128)(2,1)S(1)} %copy_bitcast_fusion, s32[]{:T(128)S(6)} %select_n.225), kind=kOutput, calls=%fused_computation.30 | convolution fusion | flops 4404019200 | bytes 17170436 | tf_op jit(solution)/shard_map/dot_general | solution.py:96
  185.2 10.0 %fusion.36 = (f32[3584]{0:T(1024)S(1)}, f32[3584,600]{0,1:T(8,128)}) fusion(f32[3584,600]{0,1:T(8,128)S(1)} %fusion.5, bf16[3584,1024]{1,0:T(8,128)(2,1)} %collective-permute-done, bf16[600,2048]{1,0:T(8,128)(2,1)S(1)} %copy_bitcast_fusion, s32[]{:T(128)S(6)} %select_n.251), kind=kOutput, calls=%fused_computation.171 | convolution fusion | flops 4408316416 | bytes 25786372 | tf_op jit(solution)/shard_map/dot_general | solution.py:97
  195.3 5.2 %exponential_reduce_fusion = (f32[3584]{0:T(1024)S(1)}, f32[3584]{0:T(1024)S(1)}, f32[3584]{0:T(1024)S(1)}) fusion(f32[3584,600]{0,1:T(8,128)} %get-tuple-element.56, f32[3584]{0:T(1024)S(1)} %get-tuple-element.55, s32[3584]{0:T(1024)S(1)} %sub.140), kind=kLoop, calls=%fused_computation.14 | loop fusion | flops 15042048 | bytes 8673280 | tf_op jit(solution)/shard_map/reduce_sum | solution.py:116
  200.9 0.7 gather_fusion.4
  201.9 8.9 %select_reduce_fusion = f32[4,64,128]{2,1,0:T(8,128)S(1)} fusion(f32[4,64,224]{2,1,0:T(8,128)S(1)} %copy.173, pred[64,128,224]{1,2,0:T(8,128)(4,1)S(1)} %copy-done.1), kind=kLoop, calls=%fused_computation.12 | loop fusion | flops 14647296 | bytes 2195456 | tf_op jit(solution)/shard_map/reduce_sum | solution.py:139
  210.8 0.7 copy.174
  211.5 6.7 %all-to-all-start.3 = ((f32[16,4,4,128]{3,2,1,0:T(4,128)}), f32[16,4,4,128]{3,2,1,0:T(4,128)S(1)}, u32[]{:S(2)}, u32[]{:S(2)}) async-start(f32[16,4,4,128]{3,2,1,0:T(4,128)} %copy.174), calls=%async_computation.3 | async-start | bytes 262144 | tf_op jit(solution)/shard_map/all_to_all | solution.py:141
  218.2 0.6 gather_fusion.5
  218.9 0.6 gather_fusion.6
  219.5 5.4 %all-to-all-done.3 = f32[16,4,4,128]{3,2,1,0:T(4,128)S(1)} async-done(((f32[16,4,4,128]{3,2,1,0:T(4,128)}), f32[16,4,4,128]{3,2,1,0:T(4,128)S(1)}, u32[]{:S(2)}, u32[]{:S(2)}) %all-to-all-start.3) | async-done | bytes 131104 | tf_op jit(solution)/shard_map/all_to_all | solution.py:141
  225.0 0.6 broadcast_in_dim.188
  225.6 7.0 %all-to-all-start.4 = ((f32[8,4,4,128]{3,2,1,0:T(4,128)}), f32[8,4,4,128]{3,2,1,0:T(4,128)S(1)}, u32[]{:S(2)}, u32[]{:S(2)}) async-start(f32[8,4,4,128]{3,2,1,0:T(4,128)} %broadcast_in_dim.188), calls=%async_computation.4 | async-start | bytes 131072 | tf_op jit(solution)/shard_map/all_to_all | solution.py:34
  232.7 4.8 %all-to-all-done.4 = f32[8,4,4,128]{3,2,1,0:T(4,128)S(1)} async-done(((f32[8,4,4,128]{3,2,1,0:T(4,128)}), f32[8,4,4,128]{3,2,1,0:T(4,128)S(1)}, u32[]{:S(2)}, u32[]{:S(2)}) %all-to-all-start.4) | async-done | bytes 65568 | tf_op jit(solution)/shard_map/all_to_all | solution.py:34
  237.6 0.7 subtract_select_fusion
  (91 shorter events, 3.8 us)
Async XLA Ops:
  7.2 4.2 %copy-start = (bf16[4,128,2048]{2,1,0:T(8,128)(2,1)S(1)}, bf16[4,128,2048]{2,1,0:T(8,128)(2,1)}, u32[]{:S(2)}) copy-start(bf16[4,128,2048]{2,1,0:T(8,128)(2,1)} %param.15) | copy-start | bytes 6291460
  7.2 4.7 %copy-start.3 = (s32[4,128]{1,0:T(4,128)S(1)}, s32[4,128]{1,0:T(4,128)}, u32[]{:S(2)}) copy-start(s32[4,128]{1,0:T(4,128)} %param.18) | copy-start | bytes 6148
  7.2 4.8 %copy-start.4 = (s32[4]{0:T(128)S(1)}, s32[4]{0:T(128)}, u32[]{:S(2)}) copy-start(s32[4]{0:T(128)} %param.19) | copy-start | bytes 52
  7.2 4.9 %copy-start.5 = (s32[4]{0:T(128)S(1)}, s32[4]{0:T(128)}, u32[]{:S(2)}) copy-start(s32[4]{0:T(128)} %param.20) | copy-start | bytes 52
  7.2 6.4 %copy-start.2 = (f32[2048]{0:T(1024)S(1)}, f32[2048]{0:T(1024)}, u32[]{:S(2)}) copy-start(f32[2048]{0:T(1024)} %param.16) | copy-start | bytes 24580
  15.6 10.1 %copy-start.6 = (s32[64]{0:T(128)S(1)}, s32[64]{0:T(128)}, u32[]{:S(2)}) copy-start(s32[64]{0:T(128)} %param.21) | copy-start | bytes 772
  18.1 24.6 %all-to-all-start = ((bf16[4,144,1024]{2,0,1:T(4,128)(2,1)}), bf16[4,144,1024]{2,0,1:T(4,128)(2,1)S(1)}, u32[]{:S(2)}, u32[]{:S(2)}) async-start(bf16[4,144,1024]{2,0,1:T(4,128)(2,1)} %bitcast.8), calls=%async_computation | async-start | bytes 2359296 | tf_op jit(solution)/shard_map/all_to_all | solution.py:69
  50.5 18.7 %all-to-all-start.1 = ((bf16[64,8,1024]{2,1,0:T(8,128)(2,1)}), bf16[64,8,1024]{2,1,0:T(8,128)(2,1)S(1)}, u32[]{:S(2)}, u32[]{:S(2)}) async-start(bf16[64,8,1024]{2,1,0:T(8,128)(2,1)} %broadcast_select_fusion), calls=%async_computation.1 | async-start | bytes 2097152 | tf_op jit(solution)/shard_map/all_to_all | solution.py:76
  54.7 84.3 %all-gather.2.cloned.1.call-start = ((), (), s32[]{:S(2)}) async-start(), calls=%async_computation.5 | async-start | bytes 7798784 | tf_op jit(solution)/shard_map/all_gather | solution.py:89
  138.9 46.3 %collective-permute-start = (bf16[3584,1024]{1,0:T(8,128)(2,1)}, bf16[3584,1024]{1,0:T(8,128)(2,1)}, u32[]{:S(2)}, u32[]{:S(2)}) collective-permute-start(bf16[3584,1024]{1,0:T(8,128)(2,1)} %all-gather.2.cloned.1.call-done), channel_id=1, source_target_pairs={{0,1},{1,0},{2,3},{3,2},{4,5},{5,4},{6,7},{7,6},{8,9},{9,8},{10,11... | collective-permute-start | bytes 22020104 | tf_op jit(solution)/shard_map/ppermute | solution.py:91
  139.8 38.2 %all-to-all-start.2 = ((bf16[16,600,128]{2,1,0:T(8,128)(2,1)}), bf16[16,600,128]{2,1,0:T(8,128)(2,1)S(1)}, u32[]{:S(2)}, u32[]{:S(2)}) async-start(bf16[16,600,128]{2,1,0:T(8,128)(2,1)} %bitcast.117), calls=%async_computation.2 | async-start | bytes 4915200 | tf_op jit(solution)/shard_map/all_to_all | solution.py:54
  195.3 6.5 %copy-start.1 = (pred[64,128,224]{1,2,0:T(8,128)(4,1)S(1)}, pred[64,128,224]{1,2,0:T(8,128)(4,1)}, u32[]{:S(2)}) copy-start(pred[64,128,224]{1,2,0:T(8,128)(4,1)} %iota_compare_fusion.2) | copy-start | bytes 5505028
  211.5 13.4 %all-to-all-start.3 = ((f32[16,4,4,128]{3,2,1,0:T(4,128)}), f32[16,4,4,128]{3,2,1,0:T(4,128)S(1)}, u32[]{:S(2)}, u32[]{:S(2)}) async-start(f32[16,4,4,128]{3,2,1,0:T(4,128)} %copy.174), calls=%async_computation.3 | async-start | bytes 262144 | tf_op jit(solution)/shard_map/all_to_all | solution.py:141
  225.6 11.9 %all-to-all-start.4 = ((f32[8,4,4,128]{3,2,1,0:T(4,128)}), f32[8,4,4,128]{3,2,1,0:T(4,128)S(1)}, u32[]{:S(2)}, u32[]{:S(2)}) async-start(f32[8,4,4,128]{3,2,1,0:T(4,128)} %broadcast_in_dim.188), calls=%async_computation.4 | async-start | bytes 131072 | tf_op jit(solution)/shard_map/all_to_all | solution.py:34
Sparse Core Ops, SparseCore 0:
  71.3 67.5 all-gather.1

commit v8 on v5

--- a/solution.py
+++ b/solution.py
@@ -64,10 +64,10 @@
     blocks = jnp.concatenate(
         [my_half.reshape(per_dev, n_req, block, half), jnp.broadcast_to(meta, (per_dev, n_req, 1, half))],
         axis=2,
-    ).reshape(per_dev, n_req * (block + 1), half)
-    received = lax.all_to_all(blocks, "req", split_axis=1, concat_axis=0, tiled=True)
-    spread_rows = received[:, :block]
-    meta_all = received[:, block, : 4 * slot_len].astype(jnp.int32).reshape(total, 4, slot_len)
+    ).transpose(1, 0, 2, 3)
+    received = lax.all_to_all(blocks, "req", split_axis=0, concat_axis=0, tiled=True)
+    spread_rows = received[:, :, :block].reshape(total, block, half)
+    meta_all = received[:, :, block, : 4 * slot_len].astype(jnp.int32).reshape(total, 4, slot_len)
     all_targets = meta_all[:, 0] * 16384 + meta_all[:, 1] * 128 + meta_all[:, 2]
     all_starts = meta_all[:, 3, 0]
     all_lengths = meta_all[:, 3, 1]
@@ -132,9 +132,15 @@
     local_stats = jnp.stack([local_top, local_mass, local_spread, local_target]).reshape(4, n_req, CAP)
     request_rows = jnp.take(local_stats, deal_order // per_dev, axis=1)
     at = (jnp.take(offsets, deal_order) - all_starts)[:, None] + pos
-    pick = at[:, :, None] == jnp.arange(CAP, dtype=jnp.int32)
-    picked = jnp.sum(jnp.where(pick[None], request_rows[:, :, None, :], 0.0), axis=3)
-    to_home = picked.reshape(4, n_req, per_dev, slot_len).transpose(1, 0, 2, 3)
+    pick = (jnp.arange(CAP, dtype=jnp.int32)[None, :, None] == at[:, None, :]).astype(jnp.float32)
+    picked = lax.dot_general(
+        request_rows.transpose(1, 0, 2),
+        pick,
+        (((2,), (1,)), ((0,), (0,))),
+        precision=lax.Precision.HIGHEST,
+        preferred_element_type=jnp.float32,
+    )
+    to_home = picked.reshape(n_req, per_dev, 4, slot_len).transpose(0, 2, 1, 3)
     by_req = merge(lax.all_to_all(to_home, "req", split_axis=0, concat_axis=0, tiled=True))
     row_top, row_mass, row_spread, row_target = merge(gather_by_all_to_all(by_req, "vocab", n_voc))
     log_mass = jnp.log(row_mass)

time: 246 us -> 240 us (0.976)
  other arithmetic: 35.9 us -> 24.5 us
  matrix products: 17 us -> 21.2 us
  waiting for transfers between devices: 127 us -> 130 us
    reduce_sum x1 -> x0, other arithmetic: 8.94 us -> none  [shards(): jnp.sum(jnp.where(pick[None], request_rows[:, :, None, :], 0.0), axis=3)]
    dot_general x0 -> x1, matrix products: none -> 4.07 us  [shards(): lax.dot_general(request_rows.transpose(1, 0, 2), pick, (((2,), (1,)), ((0...]
  transfers between devices with their start and end apart: 7 -> 7, of which waited for: 6 -> 6; matrix products, arithmetic and copies ran while one was open for 10% -> 9% of each run, Pallas kernels for 0% -> 0%
where the time goes in v8:
time: 240 us; the launch traced here: 239 us
  waiting for transfers between devices  130 us (54%)
  starting transfers between devices  31.3 us (13%)
  other arithmetic  24.5 us (10%)
  matrix products  21.2 us (9%)
  local copies, waits for them, and re-layouts  17.7 us (7%)
  between operations  14.6 us (6%)
    all_gather x1, waiting for transfers between devices, shards(): rows_mine = lax.all_gather(compact_half, 'req', axis=0, tiled=True)  67.8 us
    all_to_all x1, waiting for transfers between devices, shards(): lax.all_to_all(embedding, 'req', split_axis=0, concat_axis=1, tiled=True)  22.6 us
    all_to_all x1, waiting for transfers between devices, shards(): lax.all_to_all(blocks, 'req', split_axis=0, concat_axis=0, tiled=True)  16.1 us
    all_to_all x1, waiting for transfers between devices, shards(): lax.all_to_all(dealt_rows, 'req', split_axis=0, concat_axis=1, tiled=True)  12.9 us
    dot_general x1, matrix products, shards(): lax.dot_general(rows_other, emb_other, dims, preferred_element_type=jnp.f...  10.2 us
    all_to_all x1, starting transfers between devices, shards(): lax.all_to_all(blocks, 'req', split_axis=0, concat_axis=0, tiled=True)  7.57 us
    all_to_all x1, starting transfers between devices, gather_by_all_to_all(): return lax.all_to_all(tiles, axis, split_axis=0, concat_axis=0, tiled=True)  7.01 us
    dot_general x1, matrix products, shards(): lax.dot_general(rows_mine, emb_mine, dims, preferred_element_type=jnp.flo...  6.95 us
  transfers between devices with their start and end apart: 7, of which 6 were waited for; matrix products, arithmetic and copies ran while one was open for 9% of the time, Pallas kernels for 0%

profile of v8, /device:TPU:1, one launch (start us, length us, event | category | flops | bytes accessed | tf_op | source)
XLA Modules:
  0.0 239.0 jit_solution(15678099357484725961)
XLA Ops:
  7.2 4.2 %convert_element_type.31 = f32[4,128,2048]{2,1,0:T(8,128)} convert(bf16[4,128,2048]{2,1,0:T(8,128)(2,1)} %param.15) | non-fusion elementwise | flops 1048576 | bytes 6291456 | tf_op jit(solution)/shard_map/convert_element_type | solution.py:27
  11.4 0.5 multiply_reduce_fusion
  12.2 0.6 slice.88
  12.8 0.8 scatter.9
  13.6 1.8 fusion.9
  15.6 0.4 maximum_bitcast_fusion
  16.0 2.1 copy.158
  18.1 7.6 %all-to-all-start = ((bf16[16,4,9,1024]{3,1,2,0:T(4,128)(2,1)}), bf16[16,4,9,1024]{3,1,2,0:T(4,128)(2,1)S(1)}, u32[]{:S(2)}, u32[]{:S(2)}) async-start(bf16[16,4,9,1024]{3,1,2,0:T(4,128)(2,1)} %copy.158), calls=%async_computation | async-start | bytes 2359296 | tf_op jit(solution)/shard_map/all_to_all | solution.py:68
  25.8 0.6 gather_fusion.7
  26.5 16.1 %all-to-all-done = bf16[16,4,9,1024]{3,1,2,0:T(4,128)(2,1)S(1)} async-done(((bf16[16,4,9,1024]{3,1,2,0:T(4,128)(2,1)}), bf16[16,4,9,1024]{3,1,2,0:T(4,128)(2,1)S(1)}, u32[]{:S(2)}, u32[]{:S(2)}) %all-to-all-start) | async-done | bytes 1179680 | tf_op jit(solution)/shard_map/all_to_all | solution.py:68
  42.8 2.4 %slice_reduce_fusion.1 = (s32[64]{0:T(128)S(1)}, s32[64]{0:T(128)S(1)}) fusion(s32[64,4,128]{2,1,0:T(4,128)S(1)} %reshape.310), kind=kLoop, calls=%fused_computation.46 | loop fusion | bytes 1024 | tf_op jit(solution)/shard_map/slice | solution.py:73
  45.2 0.6 gather_fusion.8
  45.9 0.6 fusion.34
  46.5 0.2 reduce-window.9
  46.7 0.6 gather_fusion.9
  47.3 0.5 slice.131
  47.8 0.4 copy.177
  48.2 0.6 gather_fusion
  48.8 1.2 broadcast_select_fusion
  50.0 4.1 %all-to-all-start.1 = ((bf16[64,8,1024]{2,1,0:T(8,128)(2,1)}), bf16[64,8,1024]{2,1,0:T(8,128)(2,1)S(1)}, u32[]{:S(2)}, u32[]{:S(2)}) async-start(bf16[64,8,1024]{2,1,0:T(8,128)(2,1)} %broadcast_select_fusion), calls=%async_computation.1 | async-start | bytes 2097152 | tf_op jit(solution)/shard_map/all_to_all | solution.py:75
  54.4 0.7 compare_select_fusion.1
  55.1 0.7 compare_and_fusion.4
  55.7 12.9 %all-to-all-done.1 = bf16[64,8,1024]{2,1,0:T(8,128)(2,1)S(1)} async-done(((bf16[64,8,1024]{2,1,0:T(8,128)(2,1)}), bf16[64,8,1024]{2,1,0:T(8,128)(2,1)S(1)}, u32[]{:S(2)}, u32[]{:S(2)}) %all-to-all-start.1) | async-done | bytes 1048608 | tf_op jit(solution)/shard_map/all_to_all | solution.py:75
  68.7 1.1 gather_fusion.1
  69.8 0.9 broadcast_select_fusion.1
  70.7 67.8 %all-gather.2.cloned.1.call-done = bf16[3584,1024]{1,0:T(8,128)(2,1)} async-done(((bf16[224,1024]{1,0:T(8,128)(2,1)}), bf16[3584,1024]{1,0:T(8,128)(2,1)}) %all-gather.2.cloned.1.call-update) | async-done | bytes 7340048 | tf_op jit(solution)/shard_map/all_gather | solution.py:86
  138.5 0.8 collective-permute-start
  139.3 5.0 %all-to-all-start.2 = ((bf16[16,600,128]{2,1,0:T(8,128)(2,1)}), bf16[16,600,128]{2,1,0:T(8,128)(2,1)S(1)}, u32[]{:S(2)}, u32[]{:S(2)}) async-start(bf16[16,600,128]{2,1,0:T(8,128)(2,1)} %bitcast.94), calls=%async_computation.2 | async-start | bytes 4915200 | tf_op jit(solution)/shard_map/all_to_all | solution.py:54
  144.6 0.8 gather_fusion.11
  145.4 0.8 gather_fusion.10
  146.2 0.6 gather_fusion.2
  147.6 6.3 %select_reduce_fusion.1 = s32[16,224]{1,0:T(8,128)S(1)} fusion(s32[16,4,128]{2,1,0:T(4,128)S(1)} %broadcast_select_fusion.2, s32[16,4,224]{2,1,0:T(4,128)S(1)} %subtract_add_fusion, pred[16,4,224]{2,1,0:T(4,128)(4,1)S(1)} %fusion.13), kind=kLoop, calls=%fused_computation.18 | loop fusion | flops 7336448 | bytes 118784 | tf_op jit(solution)/shard_map/reduce_sum | solution.py:108
  154.0 0.8 gather_fusion.4
  154.9 22.6 %all-to-all-done.2 = bf16[16,600,128]{2,1,0:T(8,128)(2,1)S(1)} async-done(((bf16[16,600,128]{2,1,0:T(8,128)(2,1)}), bf16[16,600,128]{2,1,0:T(8,128)(2,1)S(1)}, u32[]{:S(2)}, u32[]{:S(2)}) %all-to-all-start.2) | async-done | bytes 2457632 | tf_op jit(solution)/shard_map/all_to_all | solution.py:54
  177.5 0.3 copy_bitcast_fusion
  177.8 7.0 %fusion.7 = f32[3584,600]{0,1:T(8,128)S(1)} fusion(bf16[3584,1024]{1,0:T(8,128)(2,1)} %all-gather.2.cloned.1.call-done, bf16[600,2048]{1,0:T(8,128)(2,1)S(1)} %copy_bitcast_fusion, s32[]{:T(128)S(6)} %select_n.160), kind=kOutput, calls=%fused_computation.31 | convolution fusion | flops 4404019200 | bytes 17170436 | tf_op jit(solution)/shard_map/dot_general | solution.py:93
  184.8 10.2 %fusion.37 = (f32[3584]{0:T(1024)S(1)}, f32[3584,600]{0,1:T(8,128)}) fusion(f32[3584,600]{0,1:T(8,128)S(1)} %fusion.7, bf16[3584,1024]{1,0:T(8,128)(2,1)} %collective-permute-done, bf16[600,2048]{1,0:T(8,128)(2,1)S(1)} %copy_bitcast_fusion, s32[]{:T(128)S(6)} %select_n.176), kind=kOutput, calls=%fused_computation.147 | convolution fusion | flops 4408316416 | bytes 25786372 | tf_op jit(solution)/shard_map/dot_general | solution.py:94
  195.1 5.1 %exponential_reduce_fusion = (f32[3584]{0:T(1024)S(1)}, f32[3584]{0:T(1024)S(1)}, f32[3584]{0:T(1024)S(1)}) fusion(f32[3584,600]{0,1:T(8,128)} %get-tuple-element.60, f32[3584]{0:T(1024)S(1)} %get-tuple-element.59, s32[3584]{0:T(1024)S(1)} %sub.121), kind=kLoop, calls=%fused_computation.13 | loop fusion | flops 15042048 | bytes 8673280 | tf_op jit(solution)/shard_map/reduce_sum | solution.py:113
  200.5 0.7 gather_fusion.3
  201.2 4.1 %fusion.2 = f32[64,4,128]{2,1,0:T(4,128)} fusion(s32[64,128]{1,0:T(8,128)S(1)} %iota_add_fusion, f32[64,4,224]{2,1,0:T(4,128)S(1)} %gather_fusion.3, pred[64]{0:T(512)(128)(4,1)S(1)} %get-tuple-element.37), kind=kOutput, calls=%fused_computation.21 | convolution fusion | flops 89972736 | bytes 393280 | tf_op jit(solution)/shard_map/dot_general | solution.py:136
  205.3 6.7 %all-to-all-start.3 = ((f32[16,4,4,128]{3,1,2,0:T(4,128)}), f32[16,4,4,128]{3,1,2,0:T(4,128)S(1)}, u32[]{:S(2)}, u32[]{:S(2)}) async-start(f32[16,4,4,128]{3,1,2,0:T(4,128)} %bitcast.24), calls=%async_computation.3 | async-start | bytes 262144 | tf_op jit(solution)/shard_map/all_to_all | solution.py:144
  212.1 0.6 gather_fusion.5
  212.7 0.6 gather_fusion.6
  213.3 5.4 %all-to-all-done.3 = f32[16,4,4,128]{3,1,2,0:T(4,128)S(1)} async-done(((f32[16,4,4,128]{3,1,2,0:T(4,128)}), f32[16,4,4,128]{3,1,2,0:T(4,128)S(1)}, u32[]{:S(2)}, u32[]{:S(2)}) %all-to-all-start.3) | async-done | bytes 131104 | tf_op jit(solution)/shard_map/all_to_all | solution.py:144
  218.9 0.6 broadcast_in_dim.163
  219.6 7.0 %all-to-all-start.4 = ((f32[8,4,4,128]{3,2,1,0:T(4,128)}), f32[8,4,4,128]{3,2,1,0:T(4,128)S(1)}, u32[]{:S(2)}, u32[]{:S(2)}) async-start(f32[8,4,4,128]{3,2,1,0:T(4,128)} %broadcast_in_dim.163), calls=%async_computation.4 | async-start | bytes 131072 | tf_op jit(solution)/shard_map/all_to_all | solution.py:34
  226.6 4.8 %all-to-all-done.4 = f32[8,4,4,128]{3,2,1,0:T(4,128)S(1)} async-done(((f32[8,4,4,128]{3,2,1,0:T(4,128)}), f32[8,4,4,128]{3,2,1,0:T(4,128)S(1)}, u32[]{:S(2)}, u32[]{:S(2)}) %all-to-all-start.4) | async-done | bytes 65568 | tf_op jit(solution)/shard_map/all_to_all | solution.py:34
  231.5 0.7 subtract_select_fusion
  (84 shorter events, 2.9 us)
Async XLA Ops:
  7.2 4.2 %copy-start = (bf16[4,128,2048]{2,1,0:T(8,128)(2,1)S(1)}, bf16[4,128,2048]{2,1,0:T(8,128)(2,1)}, u32[]{:S(2)}) copy-start(bf16[4,128,2048]{2,1,0:T(8,128)(2,1)} %param.15) | copy-start | bytes 6291460
  7.2 4.7 %copy-start.2 = (s32[4,128]{1,0:T(4,128)S(1)}, s32[4,128]{1,0:T(4,128)}, u32[]{:S(2)}) copy-start(s32[4,128]{1,0:T(4,128)} %param.18) | copy-start | bytes 6148
  7.2 4.8 %copy-start.3 = (s32[4]{0:T(128)S(1)}, s32[4]{0:T(128)}, u32[]{:S(2)}) copy-start(s32[4]{0:T(128)} %param.19) | copy-start | bytes 52
  7.2 4.9 %copy-start.4 = (s32[4]{0:T(128)S(1)}, s32[4]{0:T(128)}, u32[]{:S(2)}) copy-start(s32[4]{0:T(128)} %param.20) | copy-start | bytes 52
  7.2 6.4 %copy-start.1 = (f32[2048]{0:T(1024)S(1)}, f32[2048]{0:T(1024)}, u32[]{:S(2)}) copy-start(f32[2048]{0:T(1024)} %param.16) | copy-start | bytes 24580
  15.6 10.1 %copy-start.5 = (s32[64]{0:T(128)S(1)}, s32[64]{0:T(128)}, u32[]{:S(2)}) copy-start(s32[64]{0:T(128)} %param.21) | copy-start | bytes 772
  18.1 24.6 %all-to-all-start = ((bf16[16,4,9,1024]{3,1,2,0:T(4,128)(2,1)}), bf16[16,4,9,1024]{3,1,2,0:T(4,128)(2,1)S(1)}, u32[]{:S(2)}, u32[]{:S(2)}) async-start(bf16[16,4,9,1024]{3,1,2,0:T(4,128)(2,1)} %copy.158), calls=%async_computation | async-start | bytes 2359296 | tf_op jit(solution)/shard_map/all_to_all | solution.py:68
  50.0 18.7 %all-to-all-start.1 = ((bf16[64,8,1024]{2,1,0:T(8,128)(2,1)}), bf16[64,8,1024]{2,1,0:T(8,128)(2,1)S(1)}, u32[]{:S(2)}, u32[]{:S(2)}) async-start(bf16[64,8,1024]{2,1,0:T(8,128)(2,1)} %broadcast_select_fusion), calls=%async_computation.1 | async-start | bytes 2097152 | tf_op jit(solution)/shard_map/all_to_all | solution.py:75
  54.1 84.3 %all-gather.2.cloned.1.call-start = ((), (), s32[]{:S(2)}) async-start(), calls=%async_computation.5 | async-start | bytes 7798784 | tf_op jit(solution)/shard_map/all_gather | solution.py:86
  138.5 46.3 %collective-permute-start = (bf16[3584,1024]{1,0:T(8,128)(2,1)}, bf16[3584,1024]{1,0:T(8,128)(2,1)}, u32[]{:S(2)}, u32[]{:S(2)}) collective-permute-start(bf16[3584,1024]{1,0:T(8,128)(2,1)} %all-gather.2.cloned.1.call-done), channel_id=1, source_target_pairs={{0,1},{1,0},{2,3},{3,2},{4,5},{5,4},{6,7},{7,6},{8,9},{9,8},{10,11... | collective-permute-start | bytes 22020104 | tf_op jit(solution)/shard_map/ppermute | solution.py:88
  139.3 38.2 %all-to-all-start.2 = ((bf16[16,600,128]{2,1,0:T(8,128)(2,1)}), bf16[16,600,128]{2,1,0:T(8,128)(2,1)S(1)}, u32[]{:S(2)}, u32[]{:S(2)}) async-start(bf16[16,600,128]{2,1,0:T(8,128)(2,1)} %bitcast.94), calls=%async_computation.2 | async-start | bytes 4915200 | tf_op jit(solution)/shard_map/all_to_all | solution.py:54
  205.3 13.4 %all-to-all-start.3 = ((f32[16,4,4,128]{3,1,2,0:T(4,128)}), f32[16,4,4,128]{3,1,2,0:T(4,128)S(1)}, u32[]{:S(2)}, u32[]{:S(2)}) async-start(f32[16,4,4,128]{3,1,2,0:T(4,128)} %bitcast.24), calls=%async_computation.3 | async-start | bytes 262144 | tf_op jit(solution)/shard_map/all_to_all | solution.py:144
  219.6 11.9 %all-to-all-start.4 = ((f32[8,4,4,128]{3,2,1,0:T(4,128)}), f32[8,4,4,128]{3,2,1,0:T(4,128)S(1)}, u32[]{:S(2)}, u32[]{:S(2)}) async-start(f32[8,4,4,128]{3,2,1,0:T(4,128)} %broadcast_in_dim.163), calls=%async_computation.4 | async-start | bytes 131072 | tf_op jit(solution)/shard_map/all_to_all | solution.py:34
Sparse Core Ops, SparseCore 0:
  70.8 67.5 all-gather.1

commit v9 on v8

--- a/solution.py
+++ b/solution.py
@@ -4,6 +4,7 @@
 import jax.numpy as jnp
 from jax import lax
 from jax.sharding import PartitionSpec as P
+from jax.experimental import pallas as pl
 
 CAP = 224
 
@@ -32,6 +33,42 @@
 def gather_by_all_to_all(x, axis, n):
     tiles = jnp.broadcast_to(x[None], (n,) + x.shape)
     return lax.all_to_all(tiles, axis, split_axis=0, concat_axis=0, tiled=True)
+
+
+def stats_kernel(ids_ref, mine_ref, other_ref, emb_mine_ref, emb_other_ref, out_ref):
+    dims = (((1,), (1,)), ((), ()))
+    logits = lax.dot_general(emb_mine_ref[...], mine_ref[...], dims, preferred_element_type=jnp.float32)
+    logits = logits + lax.dot_general(
+        emb_other_ref[...], other_ref[...], dims, preferred_element_type=jnp.float32
+    )
+    top = jnp.max(logits, axis=0, keepdims=True)
+    shifted = logits - top
+    weights = jnp.exp(shifted)
+    vocab_ids = lax.broadcasted_iota(jnp.int32, logits.shape, 0)
+    target = jnp.sum(jnp.where(vocab_ids == ids_ref[...], logits, 0.0), axis=0, keepdims=True)
+    out_ref[0:1, :] = top
+    out_ref[1:2, :] = jnp.sum(weights, axis=0, keepdims=True)
+    out_ref[2:3, :] = jnp.sum(weights * shifted, axis=0, keepdims=True)
+    out_ref[3:4, :] = target
+    out_ref[4:8, :] = jnp.zeros((4, top.shape[1]), jnp.float32)
+
+
+def row_stats(ids, rows_mine, rows_other, emb_mine, emb_other, tile=256):
+    n_rows, feat = rows_mine.shape
+    vocab = emb_mine.shape[0]
+    return pl.pallas_call(
+        stats_kernel,
+        grid=(n_rows // tile,),
+        in_specs=[
+            pl.BlockSpec((1, tile), lambda i: (0, i)),
+            pl.BlockSpec((tile, feat), lambda i: (i, 0)),
+            pl.BlockSpec((tile, feat), lambda i: (i, 0)),
+            pl.BlockSpec((vocab, feat), lambda i: (0, 0)),
+            pl.BlockSpec((vocab, feat), lambda i: (0, 0)),
+        ],
+        out_specs=pl.BlockSpec((8, tile), lambda i: (0, i)),
+        out_shape=jax.ShapeDtypeStruct((8, n_rows), jnp.float32),
+    )(ids, rows_mine, rows_other, emb_mine, emb_other)
 
 
 def shards(n_voc, hidden, gain, embedding, targets, span_start, span_len, deal_order):
@@ -89,10 +126,6 @@
 
     emb_mine = lax.dynamic_slice_in_dim(emb_piece, core * half, half, axis=1)
     emb_other = lax.dynamic_slice_in_dim(emb_piece, (1 - core) * half, half, axis=1)
-    dims = (((1,), (1,)), ((), ()))
-    logits = lax.dot_general(rows_mine, emb_mine, dims, preferred_element_type=jnp.float32)
-    logits = logits + lax.dot_general(rows_other, emb_other, dims, preferred_element_type=jnp.float32)
-
     dealt_members = source_of.reshape(n_req, per_dev)
     dealt_lengths = jnp.take(all_lengths, dealt_members)
     dealt_offsets = jnp.cumsum(dealt_lengths, axis=1) - dealt_lengths
@@ -107,16 +140,8 @@
     hit = (source_pos[..., None] == slot_ids) & in_member[..., None]
     target_ids = jnp.sum(jnp.where(hit, member_targets[:, :, None, :], 0), axis=(1, 3)).reshape(-1)
 
-    local_top = jnp.max(logits, axis=1)
-    shifted = logits - local_top[:, None]
-    weights = jnp.exp(shifted)
-    local_mass = jnp.sum(weights, axis=1)
-    local_spread = jnp.sum(weights * shifted, axis=1)
-    local_ids = target_ids - (vhere * voc_local + here * piece)
-    local_target = jnp.sum(
-        jnp.where(jnp.arange(piece, dtype=jnp.int32)[None, :] == local_ids[:, None], logits, 0.0),
-        axis=1,
-    )
+    local_ids = (target_ids - (vhere * voc_local + here * piece)).reshape(1, -1)
+    local_stats = row_stats(local_ids, rows_mine, rows_other, emb_mine, emb_other)[:4]
 
     def merge(stats):
         top_each, mass_each, spread_each, target_each = stats[:, 0], stats[:, 1], stats[:, 2], stats[:, 3]
@@ -129,7 +154,7 @@
 
     offsets = dealt_offsets.reshape(-1)
     pos = jnp.arange(slot_len, dtype=jnp.int32)[None, :]
-    local_stats = jnp.stack([local_top, local_mass, local_spread, local_target]).reshape(4, n_req, CAP)
+    local_stats = local_stats.reshape(4, n_req, CAP)
     request_rows = jnp.take(local_stats, deal_order // per_dev, axis=1)
     at = (jnp.take(offsets, deal_order) - all_starts)[:, None] + pos
     pick = (jnp.arange(CAP, dtype=jnp.int32)[None, :, None] == at[:, None, :]).astype(jnp.float32)

time: 240 us -> 238 us (level)
  Pallas kernels: 0 us -> 18.4 us
  matrix products: 21.2 us -> 4.07 us
  other arithmetic: 24.5 us -> 19.3 us
  local copies, waits for them, and re-layouts: 17.7 us -> 20.7 us
    pallas_call x0 -> x1, Pallas kernels: none -> 18.4 us  [row_stats(): pl.pallas_call(stats_kernel, grid=(n_rows // tile,), in_specs=[pl.BlockSp...]
    dot_general x2 -> x0, matrix products: 17.1 us -> none  [the longest x1 10.2 us: shards(): lax.dot_general(rows_other, emb_other, dims, preferred_element_type=jnp.f...]
    reduce_sum x1 -> x0, other arithmetic: 5.08 us -> none  [shards(): local_mass = jnp.sum(weights, axis=1)]
  transfers between devices with their start and end apart: 7 -> 7, of which waited for: 6 -> 6; matrix products, arithmetic and copies ran while one was open for 9% -> 7% of each run, Pallas kernels for 0% -> 0%
where the time goes in v9:
time: 238 us; the launch traced here: 237 us
  waiting for transfers between devices  129 us (54%)
  starting transfers between devices  31.3 us (13%)
  local copies, waits for them, and re-layouts  20.7 us (9%)
  other arithmetic  19.3 us (8%)
  Pallas kernels  18.4 us (8%)
  between operations  14.5 us (6%)
  matrix products  4.07 us (2%)
    all_gather x1, waiting for transfers between devices, shards(): rows_mine = lax.all_gather(compact_half, 'req', axis=0, tiled=True)  67.8 us
    all_to_all x1, waiting for transfers between devices, shards(): lax.all_to_all(embedding, 'req', split_axis=0, concat_axis=1, tiled=True)  22 us
    pallas_call x1, Pallas kernels, row_stats(): pl.pallas_call(stats_kernel, grid=(n_rows // tile,), in_specs=[pl.BlockSp...  18.4 us
    all_to_all x1, waiting for transfers between devices, shards(): lax.all_to_all(blocks, 'req', split_axis=0, concat_axis=0, tiled=True)  16.1 us
    all_to_all x1, waiting for transfers between devices, shards(): lax.all_to_all(dealt_rows, 'req', split_axis=0, concat_axis=1, tiled=True)  12.9 us
    all_to_all x1, starting transfers between devices, shards(): lax.all_to_all(blocks, 'req', split_axis=0, concat_axis=0, tiled=True)  7.57 us
    all_to_all x1, starting transfers between devices, gather_by_all_to_all(): return lax.all_to_all(tiles, axis, split_axis=0, concat_axis=0, tiled=True)  7.01 us
    all_to_all x1, starting transfers between devices, shards(): lax.all_to_all(to_home, 'req', split_axis=0, concat_axis=0, tiled=True)  6.74 us
  transfers between devices with their start and end apart: 7, of which 6 were waited for; matrix products, arithmetic and copies ran while one was open for 7% of the time, Pallas kernels for 0%

profile of v9, /device:TPU:1, one launch (start us, length us, event | category | flops | bytes accessed | tf_op | source)
XLA Modules:
  0.0 237.5 jit_solution(6155874964446411737)
XLA Ops:
  7.2 2.2 multiply_reduce_fusion
  9.5 2.5 %convert_element_type.31 = f32[4,128,2048]{2,1,0:T(8,128)} convert(bf16[4,128,2048]{2,1,0:T(8,128)(2,1)S(1)} %copy-done) | non-fusion elementwise | flops 1048576 | bytes 6291456 | tf_op jit(solution)/shard_map/convert_element_type | solution.py:28
  11.9 0.6 slice.91
  12.7 0.8 scatter.9
  13.6 1.8 fusion.5
  15.6 0.4 maximum_bitcast_fusion
  16.0 2.1 copy.167
  18.1 7.6 %all-to-all-start = ((bf16[16,4,9,1024]{3,1,2,0:T(4,128)(2,1)}), bf16[16,4,9,1024]{3,1,2,0:T(4,128)(2,1)S(1)}, u32[]{:S(2)}, u32[]{:S(2)}) async-start(bf16[16,4,9,1024]{3,1,2,0:T(4,128)(2,1)} %copy.167), calls=%async_computation | async-start | bytes 2359296 | tf_op jit(solution)/shard_map/all_to_all | solution.py:105
  25.8 0.6 gather_fusion.9
  26.5 16.1 %all-to-all-done = bf16[16,4,9,1024]{3,1,2,0:T(4,128)(2,1)S(1)} async-done(((bf16[16,4,9,1024]{3,1,2,0:T(4,128)(2,1)}), bf16[16,4,9,1024]{3,1,2,0:T(4,128)(2,1)S(1)}, u32[]{:S(2)}, u32[]{:S(2)}) %all-to-all-start) | async-done | bytes 1179680 | tf_op jit(solution)/shard_map/all_to_all | solution.py:105
  42.8 0.5 slice.138
  43.3 0.4 copy.190
  43.7 2.4 %slice_reduce_fusion.1 = (s32[64]{0:T(128)S(1)}, s32[64]{0:T(128)S(1)}) fusion(s32[64,4,128]{2,1,0:T(4,128)S(1)} %reshape.310), kind=kLoop, calls=%fused_computation.36 | loop fusion | bytes 1024 | tf_op jit(solution)/shard_map/slice | solution.py:110
  46.1 0.6 gather_fusion.10
  46.7 0.6 gather_fusion.11
  47.4 0.6 fusion.28
  48.2 0.6 gather_fusion.1
  48.8 1.2 broadcast_select_fusion
  50.0 4.1 %all-to-all-start.1 = ((bf16[64,8,1024]{2,1,0:T(8,128)(2,1)}), bf16[64,8,1024]{2,1,0:T(8,128)(2,1)S(1)}, u32[]{:S(2)}, u32[]{:S(2)}) async-start(bf16[64,8,1024]{2,1,0:T(8,128)(2,1)} %broadcast_select_fusion), calls=%async_computation.1 | async-start | bytes 2097152 | tf_op jit(solution)/shard_map/all_to_all | solution.py:112
  54.4 0.7 compare_select_fusion.1
  55.0 0.7 compare_and_fusion.4
  55.7 12.9 %all-to-all-done.1 = bf16[64,8,1024]{2,1,0:T(8,128)(2,1)S(1)} async-done(((bf16[64,8,1024]{2,1,0:T(8,128)(2,1)}), bf16[64,8,1024]{2,1,0:T(8,128)(2,1)S(1)}, u32[]{:S(2)}, u32[]{:S(2)}) %all-to-all-start.1) | async-done | bytes 1048608 | tf_op jit(solution)/shard_map/all_to_all | solution.py:112
  68.7 1.1 gather_fusion.2
  69.8 0.9 broadcast_select_fusion.1
  70.7 67.8 %all-gather.2.cloned.1.call-done.mine_ref = bf16[3584,1024]{1,0:T(8,128)(2,1)} async-done(((bf16[224,1024]{1,0:T(8,128)(2,1)}), bf16[3584,1024]{1,0:T(8,128)(2,1)}) %all-gather.2.cloned.1.call-update) | async-done | bytes 7340048 | tf_op jit(solution)/shard_map/all_gather | solution.py:123
  138.5 0.8 collective-permute-start
  139.3 5.0 %all-to-all-start.2 = ((bf16[16,600,128]{2,1,0:T(8,128)(2,1)}), bf16[16,600,128]{2,1,0:T(8,128)(2,1)S(1)}, u32[]{:S(2)}, u32[]{:S(2)}) async-start(bf16[16,600,128]{2,1,0:T(8,128)(2,1)} %bitcast.92), calls=%async_computation.2 | async-start | bytes 4915200 | tf_op jit(solution)/shard_map/all_to_all | solution.py:91
  144.6 0.8 gather_fusion.7
  145.4 0.8 gather_fusion.8
  146.2 0.6 gather_fusion
  147.6 6.3 %select_reduce_fusion = s32[16,224]{1,0:T(8,128)S(1)} fusion(s32[16,4,128]{2,1,0:T(4,128)S(1)} %broadcast_select_fusion.2, s32[16,4,224]{2,1,0:T(4,128)S(1)} %subtract_add_fusion, pred[16,4,224]{2,1,0:T(4,128)(4,1)S(1)} %fusion.9), kind=kLoop, calls=%fused_computation.13 | loop fusion | flops 7336448 | bytes 118784 | tf_op jit(solution)/shard_map/reduce_sum | solution.py:141
  153.9 0.7 sub.110.ids_ref
  154.6 0.8 gather_fusion.4
  155.5 22.0 %all-to-all-done.2 = bf16[16,600,128]{2,1,0:T(8,128)(2,1)S(1)} async-done(((bf16[16,600,128]{2,1,0:T(8,128)(2,1)}), bf16[16,600,128]{2,1,0:T(8,128)(2,1)S(1)}, u32[]{:S(2)}, u32[]{:S(2)}) %all-to-all-start.2) | async-done | bytes 2457632 | tf_op jit(solution)/shard_map/all_to_all | solution.py:91
  177.5 0.3 copy_bitcast_fusion
  177.8 1.7 constant_dynamic-slice_fusion
  179.5 18.4 %shard_map.86 = f32[8,3584]{1,0:T(8,128)} custom-call(s32[1,3584]{1,0:T(1,128)} %sub.110.ids_ref, bf16[3584,1024]{1,0:T(8,128)(2,1)} %all-gather.2.cloned.1.call-done.mine_ref, bf16[3584,1024]{1,0:T(8,128)(2,1)} %collective-permute-done.other_ref, bf16[600,1024]{1,0:T(8,128)(2,1)} %get-tuple-element.41.emb_mine_ref, ...), custom_call_target="tpu_custom_call" | custom-call | tf_op jit(solution)/shard_map/pallas_call | solution.py:59
  197.9 0.9 slice.139
  199.0 0.7 gather_fusion.3
  199.7 4.1 %fusion.1 = f32[64,4,128]{2,1,0:T(4,128)} fusion(s32[64,128]{1,0:T(8,128)S(1)} %iota_add_fusion, f32[64,4,224]{2,1,0:T(4,128)S(1)} %gather_fusion.3, pred[64]{0:T(512)(128)(4,1)S(1)} %get-tuple-element.34), kind=kOutput, calls=%fused_computation.16 | convolution fusion | flops 89972736 | bytes 393280 | tf_op jit(solution)/shard_map/dot_general | solution.py:161
  203.8 6.7 %all-to-all-start.3 = ((f32[16,4,4,128]{3,1,2,0:T(4,128)}), f32[16,4,4,128]{3,1,2,0:T(4,128)S(1)}, u32[]{:S(2)}, u32[]{:S(2)}) async-start(f32[16,4,4,128]{3,1,2,0:T(4,128)} %bitcast.24), calls=%async_computation.3 | async-start | bytes 262144 | tf_op jit(solution)/shard_map/all_to_all | solution.py:169
  210.5 0.6 gather_fusion.6
  211.2 0.6 gather_fusion.5
  211.8 5.4 %all-to-all-done.3 = f32[16,4,4,128]{3,1,2,0:T(4,128)S(1)} async-done(((f32[16,4,4,128]{3,1,2,0:T(4,128)}), f32[16,4,4,128]{3,1,2,0:T(4,128)S(1)}, u32[]{:S(2)}, u32[]{:S(2)}) %all-to-all-start.3) | async-done | bytes 131104 | tf_op jit(solution)/shard_map/all_to_all | solution.py:169
  217.4 0.6 broadcast_in_dim.155
  218.0 7.0 %all-to-all-start.4 = ((f32[8,4,4,128]{3,2,1,0:T(4,128)}), f32[8,4,4,128]{3,2,1,0:T(4,128)S(1)}, u32[]{:S(2)}, u32[]{:S(2)}) async-start(f32[8,4,4,128]{3,2,1,0:T(4,128)} %broadcast_in_dim.155), calls=%async_computation.4 | async-start | bytes 131072 | tf_op jit(solution)/shard_map/all_to_all | solution.py:35
  225.1 4.8 %all-to-all-done.4 = f32[8,4,4,128]{3,2,1,0:T(4,128)S(1)} async-done(((f32[8,4,4,128]{3,2,1,0:T(4,128)}), f32[8,4,4,128]{3,2,1,0:T(4,128)S(1)}, u32[]{:S(2)}, u32[]{:S(2)}) %all-to-all-start.4) | async-done | bytes 65568 | tf_op jit(solution)/shard_map/all_to_all | solution.py:35
  230.0 0.7 subtract_select_fusion
  (81 shorter events, 2.8 us)
Async XLA Ops:
  7.2 2.2 copy-start
  9.4 3.1 %copy-start.3 = (s32[4]{0:T(128)S(1)}, s32[4]{0:T(128)}, u32[]{:S(2)}) copy-start(s32[4]{0:T(128)} %param.19) | copy-start | bytes 52
  9.4 3.2 %copy-start.4 = (s32[4]{0:T(128)S(1)}, s32[4]{0:T(128)}, u32[]{:S(2)}) copy-start(s32[4]{0:T(128)} %param.20) | copy-start | bytes 52
  9.4 4.0 %copy-start.2 = (s32[4,128]{1,0:T(4,128)S(1)}, s32[4,128]{1,0:T(4,128)}, u32[]{:S(2)}) copy-start(s32[4,128]{1,0:T(4,128)} %param.18) | copy-start | bytes 6148
  9.4 4.2 %copy-start.1 = (f32[2048]{0:T(1024)S(1)}, f32[2048]{0:T(1024)}, u32[]{:S(2)}) copy-start(f32[2048]{0:T(1024)} %param.16) | copy-start | bytes 24580
  16.0 9.7 %copy-start.5 = (s32[64]{0:T(128)S(1)}, s32[64]{0:T(128)}, u32[]{:S(2)}) copy-start(s32[64]{0:T(128)} %param.21) | copy-start | bytes 772
  18.1 24.6 %all-to-all-start = ((bf16[16,4,9,1024]{3,1,2,0:T(4,128)(2,1)}), bf16[16,4,9,1024]{3,1,2,0:T(4,128)(2,1)S(1)}, u32[]{:S(2)}, u32[]{:S(2)}) async-start(bf16[16,4,9,1024]{3,1,2,0:T(4,128)(2,1)} %copy.167), calls=%async_computation | async-start | bytes 2359296 | tf_op jit(solution)/shard_map/all_to_all | solution.py:105
  50.0 18.7 %all-to-all-start.1 = ((bf16[64,8,1024]{2,1,0:T(8,128)(2,1)}), bf16[64,8,1024]{2,1,0:T(8,128)(2,1)S(1)}, u32[]{:S(2)}, u32[]{:S(2)}) async-start(bf16[64,8,1024]{2,1,0:T(8,128)(2,1)} %broadcast_select_fusion), calls=%async_computation.1 | async-start | bytes 2097152 | tf_op jit(solution)/shard_map/all_to_all | solution.py:112
  54.1 84.3 %all-gather.2.cloned.1.call-start = ((), (), s32[]{:S(2)}) async-start(), calls=%async_computation.5 | async-start | bytes 7798784 | tf_op jit(solution)/shard_map/all_gather | solution.py:123
  138.5 41.0 %collective-permute-start = (bf16[3584,1024]{1,0:T(8,128)(2,1)}, bf16[3584,1024]{1,0:T(8,128)(2,1)}, u32[]{:S(2)}, u32[]{:S(2)}) collective-permute-start(bf16[3584,1024]{1,0:T(8,128)(2,1)} %all-gather.2.cloned.1.call-done.mine_ref), channel_id=1, source_target_pairs={{0,1},{1,0},{2,3},{3,2},{4,5},{5,4},{6,7},{7,6},{8,9},{9,8},{10,11... | collective-permute-start | bytes 22020104 | tf_op jit(solution)/shard_map/ppermute | solution.py:125
  139.3 38.2 %all-to-all-start.2 = ((bf16[16,600,128]{2,1,0:T(8,128)(2,1)}), bf16[16,600,128]{2,1,0:T(8,128)(2,1)S(1)}, u32[]{:S(2)}, u32[]{:S(2)}) async-start(bf16[16,600,128]{2,1,0:T(8,128)(2,1)} %bitcast.92), calls=%async_computation.2 | async-start | bytes 4915200 | tf_op jit(solution)/shard_map/all_to_all | solution.py:91
  203.8 13.4 %all-to-all-start.3 = ((f32[16,4,4,128]{3,1,2,0:T(4,128)}), f32[16,4,4,128]{3,1,2,0:T(4,128)S(1)}, u32[]{:S(2)}, u32[]{:S(2)}) async-start(f32[16,4,4,128]{3,1,2,0:T(4,128)} %bitcast.24), calls=%async_computation.3 | async-start | bytes 262144 | tf_op jit(solution)/shard_map/all_to_all | solution.py:169
  218.0 11.9 %all-to-all-start.4 = ((f32[8,4,4,128]{3,2,1,0:T(4,128)}), f32[8,4,4,128]{3,2,1,0:T(4,128)S(1)}, u32[]{:S(2)}, u32[]{:S(2)}) async-start(f32[8,4,4,128]{3,2,1,0:T(4,128)} %broadcast_in_dim.155), calls=%async_computation.4 | async-start | bytes 131072 | tf_op jit(solution)/shard_map/all_to_all | solution.py:35
Sparse Core Ops, SparseCore 0:
  70.8 67.5 all-gather.1

commit v10 on v9

--- a/solution.py
+++ b/solution.py
@@ -36,38 +36,40 @@
 
 
 def stats_kernel(ids_ref, mine_ref, other_ref, emb_mine_ref, emb_other_ref, out_ref):
-    dims = (((1,), (1,)), ((), ()))
-    logits = lax.dot_general(emb_mine_ref[...], mine_ref[...], dims, preferred_element_type=jnp.float32)
-    logits = logits + lax.dot_general(
-        emb_other_ref[...], other_ref[...], dims, preferred_element_type=jnp.float32
-    )
-    top = jnp.max(logits, axis=0, keepdims=True)
+    logits = jnp.dot(mine_ref[...], emb_mine_ref[...], preferred_element_type=jnp.float32)
+    logits = logits + jnp.dot(other_ref[...], emb_other_ref[...], preferred_element_type=jnp.float32)
+    top = jnp.max(logits, axis=1, keepdims=True)
     shifted = logits - top
     weights = jnp.exp(shifted)
-    vocab_ids = lax.broadcasted_iota(jnp.int32, logits.shape, 0)
-    target = jnp.sum(jnp.where(vocab_ids == ids_ref[...], logits, 0.0), axis=0, keepdims=True)
-    out_ref[0:1, :] = top
-    out_ref[1:2, :] = jnp.sum(weights, axis=0, keepdims=True)
-    out_ref[2:3, :] = jnp.sum(weights * shifted, axis=0, keepdims=True)
-    out_ref[3:4, :] = target
-    out_ref[4:8, :] = jnp.zeros((4, top.shape[1]), jnp.float32)
+    vocab_ids = lax.broadcasted_iota(jnp.int32, logits.shape, 1)
+    target = jnp.sum(jnp.where(vocab_ids == ids_ref[...], logits, 0.0), axis=1, keepdims=True)
+    out_ref[...] = jnp.concatenate(
+        [
+            top,
+            jnp.sum(weights, axis=1, keepdims=True),
+            jnp.sum(weights * shifted, axis=1, keepdims=True),
+            target,
+            jnp.zeros((top.shape[0], 4), jnp.float32),
+        ],
+        axis=1,
+    )
 
 
-def row_stats(ids, rows_mine, rows_other, emb_mine, emb_other, tile=256):
+def row_stats(ids, rows_mine, rows_other, emb_mine, emb_other, tile=512):
     n_rows, feat = rows_mine.shape
-    vocab = emb_mine.shape[0]
+    vocab = emb_mine.shape[1]
     return pl.pallas_call(
         stats_kernel,
         grid=(n_rows // tile,),
         in_specs=[
-            pl.BlockSpec((1, tile), lambda i: (0, i)),
+            pl.BlockSpec((tile, 1), lambda i: (i, 0)),
             pl.BlockSpec((tile, feat), lambda i: (i, 0)),
             pl.BlockSpec((tile, feat), lambda i: (i, 0)),
-            pl.BlockSpec((vocab, feat), lambda i: (0, 0)),
-            pl.BlockSpec((vocab, feat), lambda i: (0, 0)),
+            pl.BlockSpec((feat, vocab), lambda i: (0, 0)),
+            pl.BlockSpec((feat, vocab), lambda i: (0, 0)),
         ],
-        out_specs=pl.BlockSpec((8, tile), lambda i: (0, i)),
-        out_shape=jax.ShapeDtypeStruct((8, n_rows), jnp.float32),
+        out_specs=pl.BlockSpec((tile, 8), lambda i: (i, 0)),
+        out_shape=jax.ShapeDtypeStruct((n_rows, 8), jnp.float32),
     )(ids, rows_mine, rows_other, emb_mine, emb_other)
 
 
@@ -140,8 +142,8 @@
     hit = (source_pos[..., None] == slot_ids) & in_member[..., None]
     target_ids = jnp.sum(jnp.where(hit, member_targets[:, :, None, :], 0), axis=(1, 3)).reshape(-1)
 
-    local_ids = (target_ids - (vhere * voc_local + here * piece)).reshape(1, -1)
-    local_stats = row_stats(local_ids, rows_mine, rows_other, emb_mine, emb_other)[:4]
+    local_ids = (target_ids - (vhere * voc_local + here * piece)).reshape(-1, 1)
+    local_stats = row_stats(local_ids, rows_mine, rows_other, emb_mine.T, emb_other.T)[:, :4].T
 
     def merge(stats):
         top_each, mass_each, spread_each, target_each = stats[:, 0], stats[:, 1], stats[:, 2], stats[:, 3]

time: 238 us -> 244 us (1.025)
  local copies, waits for them, and re-layouts: 20.7 us -> 28.2 us
    all_to_all x1, local copies, waits for them, and re-layouts: 0.32 us -> 3.1 us  [shards(): lax.all_to_all(embedding, 'req', split_axis=0, concat_axis=1, tiled=True)]
  transfers between devices with their start and end apart: 7 -> 7, of which waited for: 6 -> 6; matrix products, arithmetic and copies ran while one was open for 7% -> 9% of each run, Pallas kernels for 0% -> 0%
where the time goes in v10:
time: 244 us; the launch traced here: 243 us
  waiting for transfers between devices  127 us (52%)
  starting transfers between devices  31.3 us (13%)
  local copies, waits for them, and re-layouts  28.2 us (12%)
  other arithmetic  19.3 us (8%)
  Pallas kernels  19.1 us (8%)
  between operations  14.5 us (6%)
  matrix products  4.07 us (2%)
    all_gather x1, waiting for transfers between devices, shards(): rows_mine = lax.all_gather(compact_half, 'req', axis=0, tiled=True)  67.8 us
    all_to_all x1, waiting for transfers between devices, shards(): lax.all_to_all(embedding, 'req', split_axis=0, concat_axis=1, tiled=True)  19.8 us
    pallas_call x1, Pallas kernels, row_stats(): pl.pallas_call(stats_kernel, grid=(n_rows // tile,), in_specs=[pl.BlockSp...  19.1 us
    all_to_all x1, waiting for transfers between devices, shards(): lax.all_to_all(blocks, 'req', split_axis=0, concat_axis=0, tiled=True)  16.1 us
    all_to_all x1, waiting for transfers between devices, shards(): lax.all_to_all(dealt_rows, 'req', split_axis=0, concat_axis=1, tiled=True)  12.9 us
    all_to_all x1, starting transfers between devices, shards(): lax.all_to_all(blocks, 'req', split_axis=0, concat_axis=0, tiled=True)  7.57 us
    all_to_all x1, starting transfers between devices, gather_by_all_to_all(): return lax.all_to_all(tiles, axis, split_axis=0, concat_axis=0, tiled=True)  7.01 us
    all_to_all x1, starting transfers between devices, shards(): lax.all_to_all(to_home, 'req', split_axis=0, concat_axis=0, tiled=True)  6.74 us
  transfers between devices with their start and end apart: 7, of which 6 were waited for; matrix products, arithmetic and copies ran while one was open for 9% of the time, Pallas kernels for 0%

profile of v10, /device:TPU:1, one launch (start us, length us, event | category | flops | bytes accessed | tf_op | source)
XLA Modules:
  0.0 243.4 jit_solution(9580928779474380770)
XLA Ops:
  7.2 2.2 multiply_reduce_fusion
  9.5 2.5 %convert_element_type.31 = f32[4,128,2048]{2,1,0:T(8,128)} convert(bf16[4,128,2048]{2,1,0:T(8,128)(2,1)S(1)} %copy-done.1) | non-fusion elementwise | flops 1048576 | bytes 6291456 | tf_op jit(solution)/shard_map/convert_element_type | solution.py:28
  11.9 0.6 slice.91
  12.7 0.8 scatter.9
  13.6 1.8 fusion.5
  15.6 0.4 maximum_bitcast_fusion
  16.0 2.1 copy.175
  18.1 7.6 %all-to-all-start = ((bf16[16,4,9,1024]{3,1,2,0:T(4,128)(2,1)}), bf16[16,4,9,1024]{3,1,2,0:T(4,128)(2,1)S(1)}, u32[]{:S(2)}, u32[]{:S(2)}) async-start(bf16[16,4,9,1024]{3,1,2,0:T(4,128)(2,1)} %copy.175), calls=%async_computation | async-start | bytes 2359296 | tf_op jit(solution)/shard_map/all_to_all | solution.py:107
  25.8 0.6 gather_fusion.9
  26.5 16.1 %all-to-all-done = bf16[16,4,9,1024]{3,1,2,0:T(4,128)(2,1)S(1)} async-done(((bf16[16,4,9,1024]{3,1,2,0:T(4,128)(2,1)}), bf16[16,4,9,1024]{3,1,2,0:T(4,128)(2,1)S(1)}, u32[]{:S(2)}, u32[]{:S(2)}) %all-to-all-start) | async-done | bytes 1179680 | tf_op jit(solution)/shard_map/all_to_all | solution.py:107
  42.8 0.5 slice.138
  43.7 2.4 %slice_reduce_fusion.1 = (s32[64]{0:T(128)S(1)}, s32[64]{0:T(128)S(1)}) fusion(s32[64,4,128]{2,1,0:T(4,128)S(1)} %reshape.310), kind=kLoop, calls=%fused_computation.37 | loop fusion | bytes 1024 | tf_op jit(solution)/shard_map/slice | solution.py:112
  46.1 0.6 gather_fusion.10
  46.7 0.6 gather_fusion.11
  47.4 0.6 fusion.28
  48.2 0.6 gather_fusion.1
  48.8 1.2 broadcast_select_fusion
  50.0 4.1 %all-to-all-start.1 = ((bf16[64,8,1024]{2,1,0:T(8,128)(2,1)}), bf16[64,8,1024]{2,1,0:T(8,128)(2,1)S(1)}, u32[]{:S(2)}, u32[]{:S(2)}) async-start(bf16[64,8,1024]{2,1,0:T(8,128)(2,1)} %broadcast_select_fusion), calls=%async_computation.1 | async-start | bytes 2097152 | tf_op jit(solution)/shard_map/all_to_all | solution.py:114
  54.4 0.7 compare_select_fusion.1
  55.0 0.7 compare_and_fusion.4
  55.7 12.9 %all-to-all-done.1 = bf16[64,8,1024]{2,1,0:T(8,128)(2,1)S(1)} async-done(((bf16[64,8,1024]{2,1,0:T(8,128)(2,1)}), bf16[64,8,1024]{2,1,0:T(8,128)(2,1)S(1)}, u32[]{:S(2)}, u32[]{:S(2)}) %all-to-all-start.1) | async-done | bytes 1048608 | tf_op jit(solution)/shard_map/all_to_all | solution.py:114
  68.7 1.1 gather_fusion.2
  69.8 0.9 broadcast_select_fusion.1
  70.7 67.8 %all-gather.2.cloned.1.call-done.mine_ref = bf16[3584,1024]{1,0:T(8,128)(2,1)} async-done(((bf16[224,1024]{1,0:T(8,128)(2,1)}), bf16[3584,1024]{1,0:T(8,128)(2,1)}) %all-gather.2.cloned.1.call-update) | async-done | bytes 7340048 | tf_op jit(solution)/shard_map/all_gather | solution.py:125
  138.5 0.8 collective-permute-start
  139.3 5.0 %all-to-all-start.2 = ((bf16[16,600,128]{2,1,0:T(8,128)(2,1)}), bf16[16,600,128]{2,1,0:T(8,128)(2,1)S(1)}, u32[]{:S(2)}, u32[]{:S(2)}) async-start(bf16[16,600,128]{2,1,0:T(8,128)(2,1)} %bitcast.99), calls=%async_computation.2 | async-start | bytes 4915200 | tf_op jit(solution)/shard_map/all_to_all | solution.py:93
  144.6 0.8 gather_fusion.7
  145.4 0.8 gather_fusion.8
  146.2 0.6 gather_fusion
  147.6 6.3 %select_reduce_fusion = s32[16,224]{1,0:T(8,128)S(1)} fusion(s32[16,4,128]{2,1,0:T(4,128)S(1)} %broadcast_select_fusion.2, s32[16,4,224]{2,1,0:T(4,128)S(1)} %subtract_add_fusion, pred[16,4,224]{2,1,0:T(4,128)(4,1)S(1)} %fusion.9), kind=kLoop, calls=%fused_computation.13 | loop fusion | flops 7336448 | bytes 118784 | tf_op jit(solution)/shard_map/reduce_sum | solution.py:143
  153.9 2.9 %sub.123.ids_ref = s32[3584,1]{1,0:T(8,128)} reshape(s32[16,224]{1,0:T(8,128)S(1)} %broadcast_subtract_fusion) | data formatting | bytes 28672 | tf_op jit(solution)/shard_map/sub | solution.py:145
  156.9 0.8 gather_fusion.4
  157.7 19.8 %all-to-all-done.2 = bf16[16,600,128]{2,1,0:T(8,128)(2,1)S(1)} async-done(((bf16[16,600,128]{2,1,0:T(8,128)(2,1)}), bf16[16,600,128]{2,1,0:T(8,128)(2,1)S(1)}, u32[]{:S(2)}, u32[]{:S(2)}) %all-to-all-start.2) | async-done | bytes 2457632 | tf_op jit(solution)/shard_map/all_to_all | solution.py:93
  177.5 1.4 copy-done
  178.9 3.1 %copy.181 = bf16[600,16,128]{0,2,1:T(8,128)(2,1)S(1)} copy(bf16[600,16,128]{2,0,1:T(8,128)(2,1)} %bitcast.95) | data formatting | bytes 4915200 | tf_op jit(solution)/shard_map/all_to_all | solution.py:93
  182.0 1.7 dynamic-slice_bitcast_fusion
  183.7 19.1 %shard_map.86 = f32[3584,8]{1,0:T(8,128)} custom-call(s32[3584,1]{1,0:T(8,128)} %sub.123.ids_ref, bf16[3584,1024]{1,0:T(8,128)(2,1)} %all-gather.2.cloned.1.call-done.mine_ref, bf16[3584,1024]{1,0:T(8,128)(2,1)} %collective-permute-done.other_ref, bf16[1024,600]{1,0:T(8,128)(2,1)} %get-tuple-element.41.emb_mine_ref, ...), custom_call_target="tpu_custom_call" | custom-call | tf_op jit(solution)/shard_map/pallas_call | solution.py:61
  202.8 2.1 copy.183
  205.0 0.7 gather_fusion.3
  205.7 4.1 %fusion.1 = f32[64,4,128]{2,1,0:T(4,128)} fusion(s32[64,128]{1,0:T(8,128)S(1)} %iota_add_fusion, f32[64,4,224]{2,1,0:T(4,128)S(1)} %gather_fusion.3, pred[64]{0:T(512)(128)(4,1)S(1)} %get-tuple-element.34), kind=kOutput, calls=%fused_computation.16 | convolution fusion | flops 89972736 | bytes 393280 | tf_op jit(solution)/shard_map/dot_general | solution.py:163
  209.8 6.7 %all-to-all-start.3 = ((f32[16,4,4,128]{3,1,2,0:T(4,128)}), f32[16,4,4,128]{3,1,2,0:T(4,128)S(1)}, u32[]{:S(2)}, u32[]{:S(2)}) async-start(f32[16,4,4,128]{3,1,2,0:T(4,128)} %bitcast.29), calls=%async_computation.3 | async-start | bytes 262144 | tf_op jit(solution)/shard_map/all_to_all | solution.py:171
  216.5 0.6 gather_fusion.6
  217.1 0.6 gather_fusion.5
  217.8 5.4 %all-to-all-done.3 = f32[16,4,4,128]{3,1,2,0:T(4,128)S(1)} async-done(((f32[16,4,4,128]{3,1,2,0:T(4,128)}), f32[16,4,4,128]{3,1,2,0:T(4,128)S(1)}, u32[]{:S(2)}, u32[]{:S(2)}) %all-to-all-start.3) | async-done | bytes 131104 | tf_op jit(solution)/shard_map/all_to_all | solution.py:171
  223.4 0.6 broadcast_in_dim.155
  224.0 7.0 %all-to-all-start.4 = ((f32[8,4,4,128]{3,2,1,0:T(4,128)}), f32[8,4,4,128]{3,2,1,0:T(4,128)S(1)}, u32[]{:S(2)}, u32[]{:S(2)}) async-start(f32[8,4,4,128]{3,2,1,0:T(4,128)} %broadcast_in_dim.155), calls=%async_computation.4 | async-start | bytes 131072 | tf_op jit(solution)/shard_map/all_to_all | solution.py:35
  231.0 4.8 %all-to-all-done.4 = f32[8,4,4,128]{3,2,1,0:T(4,128)S(1)} async-done(((f32[8,4,4,128]{3,2,1,0:T(4,128)}), f32[8,4,4,128]{3,2,1,0:T(4,128)S(1)}, u32[]{:S(2)}, u32[]{:S(2)}) %all-to-all-start.4) | async-done | bytes 65568 | tf_op jit(solution)/shard_map/all_to_all | solution.py:35
  235.9 0.7 subtract_select_fusion
  (81 shorter events, 3.0 us)
Async XLA Ops:
  7.2 2.2 copy-start.1
  9.4 3.1 %copy-start.4 = (s32[4]{0:T(128)S(1)}, s32[4]{0:T(128)}, u32[]{:S(2)}) copy-start(s32[4]{0:T(128)} %param.19) | copy-start | bytes 52
  9.4 3.2 %copy-start.5 = (s32[4]{0:T(128)S(1)}, s32[4]{0:T(128)}, u32[]{:S(2)}) copy-start(s32[4]{0:T(128)} %param.20) | copy-start | bytes 52
  9.4 4.0 %copy-start.3 = (s32[4,128]{1,0:T(4,128)S(1)}, s32[4,128]{1,0:T(4,128)}, u32[]{:S(2)}) copy-start(s32[4,128]{1,0:T(4,128)} %param.18) | copy-start | bytes 6148
  9.4 4.2 %copy-start.2 = (f32[2048]{0:T(1024)S(1)}, f32[2048]{0:T(1024)}, u32[]{:S(2)}) copy-start(f32[2048]{0:T(1024)} %param.16) | copy-start | bytes 24580
  16.0 9.7 %copy-start.6 = (s32[64]{0:T(128)S(1)}, s32[64]{0:T(128)}, u32[]{:S(2)}) copy-start(s32[64]{0:T(128)} %param.21) | copy-start | bytes 772
  18.1 24.6 %all-to-all-start = ((bf16[16,4,9,1024]{3,1,2,0:T(4,128)(2,1)}), bf16[16,4,9,1024]{3,1,2,0:T(4,128)(2,1)S(1)}, u32[]{:S(2)}, u32[]{:S(2)}) async-start(bf16[16,4,9,1024]{3,1,2,0:T(4,128)(2,1)} %copy.175), calls=%async_computation | async-start | bytes 2359296 | tf_op jit(solution)/shard_map/all_to_all | solution.py:107
  50.0 18.7 %all-to-all-start.1 = ((bf16[64,8,1024]{2,1,0:T(8,128)(2,1)}), bf16[64,8,1024]{2,1,0:T(8,128)(2,1)S(1)}, u32[]{:S(2)}, u32[]{:S(2)}) async-start(bf16[64,8,1024]{2,1,0:T(8,128)(2,1)} %broadcast_select_fusion), calls=%async_computation.1 | async-start | bytes 2097152 | tf_op jit(solution)/shard_map/all_to_all | solution.py:114
  54.1 84.3 %all-gather.2.cloned.1.call-start = ((), (), s32[]{:S(2)}) async-start(), calls=%async_computation.5 | async-start | bytes 7798784 | tf_op jit(solution)/shard_map/all_gather | solution.py:125
  138.5 45.3 %collective-permute-start = (bf16[3584,1024]{1,0:T(8,128)(2,1)}, bf16[3584,1024]{1,0:T(8,128)(2,1)}, u32[]{:S(2)}, u32[]{:S(2)}) collective-permute-start(bf16[3584,1024]{1,0:T(8,128)(2,1)} %all-gather.2.cloned.1.call-done.mine_ref), channel_id=1, source_target_pairs={{0,1},{1,0},{2,3},{3,2},{4,5},{5,4},{6,7},{7,6},{8,9},{9,8},{10,11... | collective-permute-start | bytes 22020104 | tf_op jit(solution)/shard_map/ppermute | solution.py:127
  139.3 38.2 %all-to-all-start.2 = ((bf16[16,600,128]{2,1,0:T(8,128)(2,1)}), bf16[16,600,128]{2,1,0:T(8,128)(2,1)S(1)}, u32[]{:S(2)}, u32[]{:S(2)}) async-start(bf16[16,600,128]{2,1,0:T(8,128)(2,1)} %bitcast.99), calls=%async_computation.2 | async-start | bytes 4915200 | tf_op jit(solution)/shard_map/all_to_all | solution.py:93
  177.5 1.4 copy-start
  209.8 13.4 %all-to-all-start.3 = ((f32[16,4,4,128]{3,1,2,0:T(4,128)}), f32[16,4,4,128]{3,1,2,0:T(4,128)S(1)}, u32[]{:S(2)}, u32[]{:S(2)}) async-start(f32[16,4,4,128]{3,1,2,0:T(4,128)} %bitcast.29), calls=%async_computation.3 | async-start | bytes 262144 | tf_op jit(solution)/shard_map/all_to_all | solution.py:171
  224.0 11.9 %all-to-all-start.4 = ((f32[8,4,4,128]{3,2,1,0:T(4,128)}), f32[8,4,4,128]{3,2,1,0:T(4,128)S(1)}, u32[]{:S(2)}, u32[]{:S(2)}) async-start(f32[8,4,4,128]{3,2,1,0:T(4,128)} %broadcast_in_dim.155), calls=%async_computation.4 | async-start | bytes 131072 | tf_op jit(solution)/shard_map/all_to_all | solution.py:35
Sparse Core Ops, SparseCore 0:
  70.8 67.5 all-gather.1

commit v11 on v9

--- a/solution.py
+++ b/solution.py
@@ -53,7 +53,7 @@
     out_ref[4:8, :] = jnp.zeros((4, top.shape[1]), jnp.float32)
 
 
-def row_stats(ids, rows_mine, rows_other, emb_mine, emb_other, tile=256):
+def row_stats(ids, rows_mine, rows_other, emb_mine, emb_other, tile=512):
     n_rows, feat = rows_mine.shape
     vocab = emb_mine.shape[0]
     return pl.pallas_call(

time: 238 us -> 236 us (level)
  no operation moved by 1% of the time
where the time goes in v11:
time: 236 us; the launch traced here: 235 us
  waiting for transfers between devices  129 us (55%)
  starting transfers between devices  31.3 us (13%)
  local copies, waits for them, and re-layouts  20.7 us (9%)
  other arithmetic  19.3 us (8%)
  Pallas kernels  16.1 us (7%)
  between operations  14.5 us (6%)
  matrix products  4.07 us (2%)
    all_gather x1, waiting for transfers between devices, shards(): rows_mine = lax.all_gather(compact_half, 'req', axis=0, tiled=True)  67.8 us
    all_to_all x1, waiting for transfers between devices, shards(): lax.all_to_all(embedding, 'req', split_axis=0, concat_axis=1, tiled=True)  22 us
    all_to_all x1, waiting for transfers between devices, shards(): lax.all_to_all(blocks, 'req', split_axis=0, concat_axis=0, tiled=True)  16.1 us
    pallas_call x1, Pallas kernels, row_stats(): pl.pallas_call(stats_kernel, grid=(n_rows // tile,), in_specs=[pl.BlockSp...  16.1 us
    all_to_all x1, waiting for transfers between devices, shards(): lax.all_to_all(dealt_rows, 'req', split_axis=0, concat_axis=1, tiled=True)  12.9 us
    all_to_all x1, starting transfers between devices, shards(): lax.all_to_all(blocks, 'req', split_axis=0, concat_axis=0, tiled=True)  7.57 us
    all_to_all x1, starting transfers between devices, gather_by_all_to_all(): return lax.all_to_all(tiles, axis, split_axis=0, concat_axis=0, tiled=True)  7.01 us
    all_to_all x1, starting transfers between devices, shards(): lax.all_to_all(to_home, 'req', split_axis=0, concat_axis=0, tiled=True)  6.74 us
  transfers between devices with their start and end apart: 7, of which 6 were waited for; matrix products, arithmetic and copies ran while one was open for 7% of the time, Pallas kernels for 0%

profile of v11, /device:TPU:1, one launch (start us, length us, event | category | flops | bytes accessed | tf_op | source)
XLA Modules:
  0.0 235.1 jit_solution(12860729520632913742)
XLA Ops:
  7.2 2.2 multiply_reduce_fusion
  9.5 2.5 %convert_element_type.31 = f32[4,128,2048]{2,1,0:T(8,128)} convert(bf16[4,128,2048]{2,1,0:T(8,128)(2,1)S(1)} %copy-done) | non-fusion elementwise | flops 1048576 | bytes 6291456 | tf_op jit(solution)/shard_map/convert_element_type | solution.py:28
  11.9 0.6 slice.91
  12.7 0.8 scatter.9
  13.6 1.8 fusion.5
  15.6 0.4 maximum_bitcast_fusion
  16.0 2.1 copy.167
  18.1 7.6 %all-to-all-start = ((bf16[16,4,9,1024]{3,1,2,0:T(4,128)(2,1)}), bf16[16,4,9,1024]{3,1,2,0:T(4,128)(2,1)S(1)}, u32[]{:S(2)}, u32[]{:S(2)}) async-start(bf16[16,4,9,1024]{3,1,2,0:T(4,128)(2,1)} %copy.167), calls=%async_computation | async-start | bytes 2359296 | tf_op jit(solution)/shard_map/all_to_all | solution.py:105
  25.8 0.6 gather_fusion.9
  26.5 16.1 %all-to-all-done = bf16[16,4,9,1024]{3,1,2,0:T(4,128)(2,1)S(1)} async-done(((bf16[16,4,9,1024]{3,1,2,0:T(4,128)(2,1)}), bf16[16,4,9,1024]{3,1,2,0:T(4,128)(2,1)S(1)}, u32[]{:S(2)}, u32[]{:S(2)}) %all-to-all-start) | async-done | bytes 1179680 | tf_op jit(solution)/shard_map/all_to_all | solution.py:105
  42.8 0.5 slice.138
  43.3 0.4 copy.190
  43.7 2.4 %slice_reduce_fusion.1 = (s32[64]{0:T(128)S(1)}, s32[64]{0:T(128)S(1)}) fusion(s32[64,4,128]{2,1,0:T(4,128)S(1)} %reshape.310), kind=kLoop, calls=%fused_computation.36 | loop fusion | bytes 1024 | tf_op jit(solution)/shard_map/slice | solution.py:110
  46.1 0.6 gather_fusion.10
  46.7 0.6 gather_fusion.11
  47.4 0.6 fusion.28
  48.2 0.6 gather_fusion.1
  48.8 1.2 broadcast_select_fusion
  50.0 4.1 %all-to-all-start.1 = ((bf16[64,8,1024]{2,1,0:T(8,128)(2,1)}), bf16[64,8,1024]{2,1,0:T(8,128)(2,1)S(1)}, u32[]{:S(2)}, u32[]{:S(2)}) async-start(bf16[64,8,1024]{2,1,0:T(8,128)(2,1)} %broadcast_select_fusion), calls=%async_computation.1 | async-start | bytes 2097152 | tf_op jit(solution)/shard_map/all_to_all | solution.py:112
  54.4 0.7 compare_select_fusion.1
  55.0 0.7 compare_and_fusion.4
  55.7 12.9 %all-to-all-done.1 = bf16[64,8,1024]{2,1,0:T(8,128)(2,1)S(1)} async-done(((bf16[64,8,1024]{2,1,0:T(8,128)(2,1)}), bf16[64,8,1024]{2,1,0:T(8,128)(2,1)S(1)}, u32[]{:S(2)}, u32[]{:S(2)}) %all-to-all-start.1) | async-done | bytes 1048608 | tf_op jit(solution)/shard_map/all_to_all | solution.py:112
  68.7 1.1 gather_fusion.2
  69.8 0.9 broadcast_select_fusion.1
  70.7 67.8 %all-gather.2.cloned.1.call-done.mine_ref = bf16[3584,1024]{1,0:T(8,128)(2,1)} async-done(((bf16[224,1024]{1,0:T(8,128)(2,1)}), bf16[3584,1024]{1,0:T(8,128)(2,1)}) %all-gather.2.cloned.1.call-update) | async-done | bytes 7340048 | tf_op jit(solution)/shard_map/all_gather | solution.py:123
  138.5 0.8 collective-permute-start
  139.3 5.0 %all-to-all-start.2 = ((bf16[16,600,128]{2,1,0:T(8,128)(2,1)}), bf16[16,600,128]{2,1,0:T(8,128)(2,1)S(1)}, u32[]{:S(2)}, u32[]{:S(2)}) async-start(bf16[16,600,128]{2,1,0:T(8,128)(2,1)} %bitcast.92), calls=%async_computation.2 | async-start | bytes 4915200 | tf_op jit(solution)/shard_map/all_to_all | solution.py:91
  144.6 0.8 gather_fusion.7
  145.4 0.8 gather_fusion.8
  146.2 0.6 gather_fusion
  147.6 6.3 %select_reduce_fusion = s32[16,224]{1,0:T(8,128)S(1)} fusion(s32[16,4,128]{2,1,0:T(4,128)S(1)} %broadcast_select_fusion.2, s32[16,4,224]{2,1,0:T(4,128)S(1)} %subtract_add_fusion, pred[16,4,224]{2,1,0:T(4,128)(4,1)S(1)} %fusion.9), kind=kLoop, calls=%fused_computation.13 | loop fusion | flops 7336448 | bytes 118784 | tf_op jit(solution)/shard_map/reduce_sum | solution.py:141
  153.9 0.7 sub.110.ids_ref
  154.6 0.8 gather_fusion.4
  155.5 22.0 %all-to-all-done.2 = bf16[16,600,128]{2,1,0:T(8,128)(2,1)S(1)} async-done(((bf16[16,600,128]{2,1,0:T(8,128)(2,1)}), bf16[16,600,128]{2,1,0:T(8,128)(2,1)S(1)}, u32[]{:S(2)}, u32[]{:S(2)}) %all-to-all-start.2) | async-done | bytes 2457632 | tf_op jit(solution)/shard_map/all_to_all | solution.py:91
  177.5 0.3 copy_bitcast_fusion
  177.8 1.7 constant_dynamic-slice_fusion
  179.5 16.1 %shard_map.86 = f32[8,3584]{1,0:T(8,128)} custom-call(s32[1,3584]{1,0:T(1,128)} %sub.110.ids_ref, bf16[3584,1024]{1,0:T(8,128)(2,1)} %all-gather.2.cloned.1.call-done.mine_ref, bf16[3584,1024]{1,0:T(8,128)(2,1)} %collective-permute-done.other_ref, bf16[600,1024]{1,0:T(8,128)(2,1)} %get-tuple-element.41.emb_mine_ref, ...), custom_call_target="tpu_custom_call" | custom-call | tf_op jit(solution)/shard_map/pallas_call | solution.py:59
  195.6 0.9 slice.139
  196.7 0.7 gather_fusion.3
  197.4 4.1 %fusion.1 = f32[64,4,128]{2,1,0:T(4,128)} fusion(s32[64,128]{1,0:T(8,128)S(1)} %iota_add_fusion, f32[64,4,224]{2,1,0:T(4,128)S(1)} %gather_fusion.3, pred[64]{0:T(512)(128)(4,1)S(1)} %get-tuple-element.34), kind=kOutput, calls=%fused_computation.16 | convolution fusion | flops 89972736 | bytes 393280 | tf_op jit(solution)/shard_map/dot_general | solution.py:161
  201.4 6.7 %all-to-all-start.3 = ((f32[16,4,4,128]{3,1,2,0:T(4,128)}), f32[16,4,4,128]{3,1,2,0:T(4,128)S(1)}, u32[]{:S(2)}, u32[]{:S(2)}) async-start(f32[16,4,4,128]{3,1,2,0:T(4,128)} %bitcast.24), calls=%async_computation.3 | async-start | bytes 262144 | tf_op jit(solution)/shard_map/all_to_all | solution.py:169
  208.2 0.6 gather_fusion.6
  208.8 0.6 gather_fusion.5
  209.5 5.4 %all-to-all-done.3 = f32[16,4,4,128]{3,1,2,0:T(4,128)S(1)} async-done(((f32[16,4,4,128]{3,1,2,0:T(4,128)}), f32[16,4,4,128]{3,1,2,0:T(4,128)S(1)}, u32[]{:S(2)}, u32[]{:S(2)}) %all-to-all-start.3) | async-done | bytes 131104 | tf_op jit(solution)/shard_map/all_to_all | solution.py:169
  215.1 0.6 broadcast_in_dim.155
  215.7 7.0 %all-to-all-start.4 = ((f32[8,4,4,128]{3,2,1,0:T(4,128)}), f32[8,4,4,128]{3,2,1,0:T(4,128)S(1)}, u32[]{:S(2)}, u32[]{:S(2)}) async-start(f32[8,4,4,128]{3,2,1,0:T(4,128)} %broadcast_in_dim.155), calls=%async_computation.4 | async-start | bytes 131072 | tf_op jit(solution)/shard_map/all_to_all | solution.py:35
  222.7 4.8 %all-to-all-done.4 = f32[8,4,4,128]{3,2,1,0:T(4,128)S(1)} async-done(((f32[8,4,4,128]{3,2,1,0:T(4,128)}), f32[8,4,4,128]{3,2,1,0:T(4,128)S(1)}, u32[]{:S(2)}, u32[]{:S(2)}) %all-to-all-start.4) | async-done | bytes 65568 | tf_op jit(solution)/shard_map/all_to_all | solution.py:35
  227.6 0.7 subtract_select_fusion
  (81 shorter events, 2.8 us)
Async XLA Ops:
  7.2 2.2 copy-start
  9.4 3.1 %copy-start.3 = (s32[4]{0:T(128)S(1)}, s32[4]{0:T(128)}, u32[]{:S(2)}) copy-start(s32[4]{0:T(128)} %param.19) | copy-start | bytes 52
  9.4 3.2 %copy-start.4 = (s32[4]{0:T(128)S(1)}, s32[4]{0:T(128)}, u32[]{:S(2)}) copy-start(s32[4]{0:T(128)} %param.20) | copy-start | bytes 52
  9.4 4.0 %copy-start.2 = (s32[4,128]{1,0:T(4,128)S(1)}, s32[4,128]{1,0:T(4,128)}, u32[]{:S(2)}) copy-start(s32[4,128]{1,0:T(4,128)} %param.18) | copy-start | bytes 6148
  9.4 4.2 %copy-start.1 = (f32[2048]{0:T(1024)S(1)}, f32[2048]{0:T(1024)}, u32[]{:S(2)}) copy-start(f32[2048]{0:T(1024)} %param.16) | copy-start | bytes 24580
  16.0 9.7 %copy-start.5 = (s32[64]{0:T(128)S(1)}, s32[64]{0:T(128)}, u32[]{:S(2)}) copy-start(s32[64]{0:T(128)} %param.21) | copy-start | bytes 772
  18.1 24.6 %all-to-all-start = ((bf16[16,4,9,1024]{3,1,2,0:T(4,128)(2,1)}), bf16[16,4,9,1024]{3,1,2,0:T(4,128)(2,1)S(1)}, u32[]{:S(2)}, u32[]{:S(2)}) async-start(bf16[16,4,9,1024]{3,1,2,0:T(4,128)(2,1)} %copy.167), calls=%async_computation | async-start | bytes 2359296 | tf_op jit(solution)/shard_map/all_to_all | solution.py:105
  50.0 18.7 %all-to-all-start.1 = ((bf16[64,8,1024]{2,1,0:T(8,128)(2,1)}), bf16[64,8,1024]{2,1,0:T(8,128)(2,1)S(1)}, u32[]{:S(2)}, u32[]{:S(2)}) async-start(bf16[64,8,1024]{2,1,0:T(8,128)(2,1)} %broadcast_select_fusion), calls=%async_computation.1 | async-start | bytes 2097152 | tf_op jit(solution)/shard_map/all_to_all | solution.py:112
  54.1 84.3 %all-gather.2.cloned.1.call-start = ((), (), s32[]{:S(2)}) async-start(), calls=%async_computation.5 | async-start | bytes 7798784 | tf_op jit(solution)/shard_map/all_gather | solution.py:123
  138.5 41.0 %collective-permute-start = (bf16[3584,1024]{1,0:T(8,128)(2,1)}, bf16[3584,1024]{1,0:T(8,128)(2,1)}, u32[]{:S(2)}, u32[]{:S(2)}) collective-permute-start(bf16[3584,1024]{1,0:T(8,128)(2,1)} %all-gather.2.cloned.1.call-done.mine_ref), channel_id=1, source_target_pairs={{0,1},{1,0},{2,3},{3,2},{4,5},{5,4},{6,7},{7,6},{8,9},{9,8},{10,11... | collective-permute-start | bytes 22020104 | tf_op jit(solution)/shard_map/ppermute | solution.py:125
  139.3 38.2 %all-to-all-start.2 = ((bf16[16,600,128]{2,1,0:T(8,128)(2,1)}), bf16[16,600,128]{2,1,0:T(8,128)(2,1)S(1)}, u32[]{:S(2)}, u32[]{:S(2)}) async-start(bf16[16,600,128]{2,1,0:T(8,128)(2,1)} %bitcast.92), calls=%async_computation.2 | async-start | bytes 4915200 | tf_op jit(solution)/shard_map/all_to_all | solution.py:91
  201.4 13.4 %all-to-all-start.3 = ((f32[16,4,4,128]{3,1,2,0:T(4,128)}), f32[16,4,4,128]{3,1,2,0:T(4,128)S(1)}, u32[]{:S(2)}, u32[]{:S(2)}) async-start(f32[16,4,4,128]{3,1,2,0:T(4,128)} %bitcast.24), calls=%async_computation.3 | async-start | bytes 262144 | tf_op jit(solution)/shard_map/all_to_all | solution.py:169
  215.7 11.9 %all-to-all-start.4 = ((f32[8,4,4,128]{3,2,1,0:T(4,128)}), f32[8,4,4,128]{3,2,1,0:T(4,128)S(1)}, u32[]{:S(2)}, u32[]{:S(2)}) async-start(f32[8,4,4,128]{3,2,1,0:T(4,128)} %broadcast_in_dim.155), calls=%async_computation.4 | async-start | bytes 131072 | tf_op jit(solution)/shard_map/all_to_all | solution.py:35
Sparse Core Ops, SparseCore 0:
  70.8 67.5 all-gather.1

commit v12 on v11

--- a/solution.py
+++ b/solution.py
@@ -53,7 +53,7 @@
     out_ref[4:8, :] = jnp.zeros((4, top.shape[1]), jnp.float32)
 
 
-def row_stats(ids, rows_mine, rows_other, emb_mine, emb_other, tile=512):
+def row_stats(ids, rows_mine, rows_other, emb_mine, emb_other, tile=896):
     n_rows, feat = rows_mine.shape
     vocab = emb_mine.shape[0]
     return pl.pallas_call(

time: 236 us -> 237 us (level)
  no operation moved by 1% of the time
where the time goes in v12:
time: 237 us; the launch traced here: 236 us
  waiting for transfers between devices  129 us (54%)
  starting transfers between devices  31.3 us (13%)
  local copies, waits for them, and re-layouts  20.7 us (9%)
  other arithmetic  19.3 us (8%)
  Pallas kernels  17.1 us (7%)
  between operations  14.5 us (6%)
  matrix products  4.07 us (2%)
    all_gather x1, waiting for transfers between devices, shards(): rows_mine = lax.all_gather(compact_half, 'req', axis=0, tiled=True)  67.8 us
    all_to_all x1, waiting for transfers between devices, shards(): lax.all_to_all(embedding, 'req', split_axis=0, concat_axis=1, tiled=True)  22 us
    pallas_call x1, Pallas kernels, row_stats(): pl.pallas_call(stats_kernel, grid=(n_rows // tile,), in_specs=[pl.BlockSp...  17.1 us
    all_to_all x1, waiting for transfers between devices, shards(): lax.all_to_all(blocks, 'req', split_axis=0, concat_axis=0, tiled=True)  16.1 us
    all_to_all x1, waiting for transfers between devices, shards(): lax.all_to_all(dealt_rows, 'req', split_axis=0, concat_axis=1, tiled=True)  12.9 us
    all_to_all x1, starting transfers between devices, shards(): lax.all_to_all(blocks, 'req', split_axis=0, concat_axis=0, tiled=True)  7.57 us
    all_to_all x1, starting transfers between devices, gather_by_all_to_all(): return lax.all_to_all(tiles, axis, split_axis=0, concat_axis=0, tiled=True)  7.01 us
    all_to_all x1, starting transfers between devices, shards(): lax.all_to_all(to_home, 'req', split_axis=0, concat_axis=0, tiled=True)  6.74 us
  transfers between devices with their start and end apart: 7, of which 6 were waited for; matrix products, arithmetic and copies ran while one was open for 7% of the time, Pallas kernels for 0%

profile of v12, /device:TPU:1, one launch (start us, length us, event | category | flops | bytes accessed | tf_op | source)
XLA Modules:
  0.0 236.2 jit_solution(5318597339532107966)
XLA Ops:
  7.2 2.2 multiply_reduce_fusion
  9.5 2.5 %convert_element_type.31 = f32[4,128,2048]{2,1,0:T(8,128)} convert(bf16[4,128,2048]{2,1,0:T(8,128)(2,1)S(1)} %copy-done) | non-fusion elementwise | flops 1048576 | bytes 6291456 | tf_op jit(solution)/shard_map/convert_element_type | solution.py:28
  11.9 0.6 slice.91
  12.7 0.8 scatter.9
  13.6 1.8 fusion.5
  15.6 0.4 maximum_bitcast_fusion
  16.0 2.1 copy.167
  18.1 7.6 %all-to-all-start = ((bf16[16,4,9,1024]{3,1,2,0:T(4,128)(2,1)}), bf16[16,4,9,1024]{3,1,2,0:T(4,128)(2,1)S(1)}, u32[]{:S(2)}, u32[]{:S(2)}) async-start(bf16[16,4,9,1024]{3,1,2,0:T(4,128)(2,1)} %copy.167), calls=%async_computation | async-start | bytes 2359296 | tf_op jit(solution)/shard_map/all_to_all | solution.py:105
  25.8 0.6 gather_fusion.9
  26.5 16.1 %all-to-all-done = bf16[16,4,9,1024]{3,1,2,0:T(4,128)(2,1)S(1)} async-done(((bf16[16,4,9,1024]{3,1,2,0:T(4,128)(2,1)}), bf16[16,4,9,1024]{3,1,2,0:T(4,128)(2,1)S(1)}, u32[]{:S(2)}, u32[]{:S(2)}) %all-to-all-start) | async-done | bytes 1179680 | tf_op jit(solution)/shard_map/all_to_all | solution.py:105
  42.8 0.5 slice.138
  43.3 0.4 copy.190
  43.7 2.4 %slice_reduce_fusion.1 = (s32[64]{0:T(128)S(1)}, s32[64]{0:T(128)S(1)}) fusion(s32[64,4,128]{2,1,0:T(4,128)S(1)} %reshape.310), kind=kLoop, calls=%fused_computation.36 | loop fusion | bytes 1024 | tf_op jit(solution)/shard_map/slice | solution.py:110
  46.1 0.6 gather_fusion.10
  46.7 0.6 gather_fusion.11
  47.4 0.6 fusion.28
  48.2 0.6 gather_fusion.1
  48.8 1.2 broadcast_select_fusion
  50.0 4.1 %all-to-all-start.1 = ((bf16[64,8,1024]{2,1,0:T(8,128)(2,1)}), bf16[64,8,1024]{2,1,0:T(8,128)(2,1)S(1)}, u32[]{:S(2)}, u32[]{:S(2)}) async-start(bf16[64,8,1024]{2,1,0:T(8,128)(2,1)} %broadcast_select_fusion), calls=%async_computation.1 | async-start | bytes 2097152 | tf_op jit(solution)/shard_map/all_to_all | solution.py:112
  54.4 0.7 compare_select_fusion.1
  55.0 0.7 compare_and_fusion.4
  55.7 12.9 %all-to-all-done.1 = bf16[64,8,1024]{2,1,0:T(8,128)(2,1)S(1)} async-done(((bf16[64,8,1024]{2,1,0:T(8,128)(2,1)}), bf16[64,8,1024]{2,1,0:T(8,128)(2,1)S(1)}, u32[]{:S(2)}, u32[]{:S(2)}) %all-to-all-start.1) | async-done | bytes 1048608 | tf_op jit(solution)/shard_map/all_to_all | solution.py:112
  68.7 1.1 gather_fusion.2
  69.8 0.9 broadcast_select_fusion.1
  70.7 67.8 %all-gather.2.cloned.1.call-done.mine_ref = bf16[3584,1024]{1,0:T(8,128)(2,1)} async-done(((bf16[224,1024]{1,0:T(8,128)(2,1)}), bf16[3584,1024]{1,0:T(8,128)(2,1)}) %all-gather.2.cloned.1.call-update) | async-done | bytes 7340048 | tf_op jit(solution)/shard_map/all_gather | solution.py:123
  138.5 0.8 collective-permute-start
  139.3 5.0 %all-to-all-start.2 = ((bf16[16,600,128]{2,1,0:T(8,128)(2,1)}), bf16[16,600,128]{2,1,0:T(8,128)(2,1)S(1)}, u32[]{:S(2)}, u32[]{:S(2)}) async-start(bf16[16,600,128]{2,1,0:T(8,128)(2,1)} %bitcast.92), calls=%async_computation.2 | async-start | bytes 4915200 | tf_op jit(solution)/shard_map/all_to_all | solution.py:91
  144.6 0.8 gather_fusion.7
  145.4 0.8 gather_fusion.8
  146.2 0.6 gather_fusion
  147.6 6.3 %select_reduce_fusion = s32[16,224]{1,0:T(8,128)S(1)} fusion(s32[16,4,128]{2,1,0:T(4,128)S(1)} %broadcast_select_fusion.2, s32[16,4,224]{2,1,0:T(4,128)S(1)} %subtract_add_fusion, pred[16,4,224]{2,1,0:T(4,128)(4,1)S(1)} %fusion.9), kind=kLoop, calls=%fused_computation.13 | loop fusion | flops 7336448 | bytes 118784 | tf_op jit(solution)/shard_map/reduce_sum | solution.py:141
  153.9 0.7 sub.110.ids_ref
  154.6 0.8 gather_fusion.4
  155.5 22.0 %all-to-all-done.2 = bf16[16,600,128]{2,1,0:T(8,128)(2,1)S(1)} async-done(((bf16[16,600,128]{2,1,0:T(8,128)(2,1)}), bf16[16,600,128]{2,1,0:T(8,128)(2,1)S(1)}, u32[]{:S(2)}, u32[]{:S(2)}) %all-to-all-start.2) | async-done | bytes 2457632 | tf_op jit(solution)/shard_map/all_to_all | solution.py:91
  177.5 0.3 copy_bitcast_fusion
  177.8 1.7 constant_dynamic-slice_fusion
  179.5 17.1 %shard_map.86 = f32[8,3584]{1,0:T(8,128)} custom-call(s32[1,3584]{1,0:T(1,128)} %sub.110.ids_ref, bf16[3584,1024]{1,0:T(8,128)(2,1)} %all-gather.2.cloned.1.call-done.mine_ref, bf16[3584,1024]{1,0:T(8,128)(2,1)} %collective-permute-done.other_ref, bf16[600,1024]{1,0:T(8,128)(2,1)} %get-tuple-element.41.emb_mine_ref, ...), custom_call_target="tpu_custom_call" | custom-call | tf_op jit(solution)/shard_map/pallas_call | solution.py:59
  196.6 0.9 slice.139
  197.7 0.7 gather_fusion.3
  198.4 4.1 %fusion.1 = f32[64,4,128]{2,1,0:T(4,128)} fusion(s32[64,128]{1,0:T(8,128)S(1)} %iota_add_fusion, f32[64,4,224]{2,1,0:T(4,128)S(1)} %gather_fusion.3, pred[64]{0:T(512)(128)(4,1)S(1)} %get-tuple-element.34), kind=kOutput, calls=%fused_computation.16 | convolution fusion | flops 89972736 | bytes 393280 | tf_op jit(solution)/shard_map/dot_general | solution.py:161
  202.5 6.7 %all-to-all-start.3 = ((f32[16,4,4,128]{3,1,2,0:T(4,128)}), f32[16,4,4,128]{3,1,2,0:T(4,128)S(1)}, u32[]{:S(2)}, u32[]{:S(2)}) async-start(f32[16,4,4,128]{3,1,2,0:T(4,128)} %bitcast.24), calls=%async_computation.3 | async-start | bytes 262144 | tf_op jit(solution)/shard_map/all_to_all | solution.py:169
  209.2 0.6 gather_fusion.6
  209.9 0.6 gather_fusion.5
  210.5 5.4 %all-to-all-done.3 = f32[16,4,4,128]{3,1,2,0:T(4,128)S(1)} async-done(((f32[16,4,4,128]{3,1,2,0:T(4,128)}), f32[16,4,4,128]{3,1,2,0:T(4,128)S(1)}, u32[]{:S(2)}, u32[]{:S(2)}) %all-to-all-start.3) | async-done | bytes 131104 | tf_op jit(solution)/shard_map/all_to_all | solution.py:169
  216.1 0.6 broadcast_in_dim.155
  216.7 7.0 %all-to-all-start.4 = ((f32[8,4,4,128]{3,2,1,0:T(4,128)}), f32[8,4,4,128]{3,2,1,0:T(4,128)S(1)}, u32[]{:S(2)}, u32[]{:S(2)}) async-start(f32[8,4,4,128]{3,2,1,0:T(4,128)} %broadcast_in_dim.155), calls=%async_computation.4 | async-start | bytes 131072 | tf_op jit(solution)/shard_map/all_to_all | solution.py:35
  223.8 4.8 %all-to-all-done.4 = f32[8,4,4,128]{3,2,1,0:T(4,128)S(1)} async-done(((f32[8,4,4,128]{3,2,1,0:T(4,128)}), f32[8,4,4,128]{3,2,1,0:T(4,128)S(1)}, u32[]{:S(2)}, u32[]{:S(2)}) %all-to-all-start.4) | async-done | bytes 65568 | tf_op jit(solution)/shard_map/all_to_all | solution.py:35
  228.7 0.7 subtract_select_fusion
  (81 shorter events, 2.8 us)
Async XLA Ops:
  7.2 2.2 copy-start
  9.4 3.1 %copy-start.3 = (s32[4]{0:T(128)S(1)}, s32[4]{0:T(128)}, u32[]{:S(2)}) copy-start(s32[4]{0:T(128)} %param.19) | copy-start | bytes 52
  9.4 3.2 %copy-start.4 = (s32[4]{0:T(128)S(1)}, s32[4]{0:T(128)}, u32[]{:S(2)}) copy-start(s32[4]{0:T(128)} %param.20) | copy-start | bytes 52
  9.4 4.0 %copy-start.2 = (s32[4,128]{1,0:T(4,128)S(1)}, s32[4,128]{1,0:T(4,128)}, u32[]{:S(2)}) copy-start(s32[4,128]{1,0:T(4,128)} %param.18) | copy-start | bytes 6148
  9.4 4.2 %copy-start.1 = (f32[2048]{0:T(1024)S(1)}, f32[2048]{0:T(1024)}, u32[]{:S(2)}) copy-start(f32[2048]{0:T(1024)} %param.16) | copy-start | bytes 24580
  16.0 9.7 %copy-start.5 = (s32[64]{0:T(128)S(1)}, s32[64]{0:T(128)}, u32[]{:S(2)}) copy-start(s32[64]{0:T(128)} %param.21) | copy-start | bytes 772
  18.1 24.6 %all-to-all-start = ((bf16[16,4,9,1024]{3,1,2,0:T(4,128)(2,1)}), bf16[16,4,9,1024]{3,1,2,0:T(4,128)(2,1)S(1)}, u32[]{:S(2)}, u32[]{:S(2)}) async-start(bf16[16,4,9,1024]{3,1,2,0:T(4,128)(2,1)} %copy.167), calls=%async_computation | async-start | bytes 2359296 | tf_op jit(solution)/shard_map/all_to_all | solution.py:105
  50.0 18.7 %all-to-all-start.1 = ((bf16[64,8,1024]{2,1,0:T(8,128)(2,1)}), bf16[64,8,1024]{2,1,0:T(8,128)(2,1)S(1)}, u32[]{:S(2)}, u32[]{:S(2)}) async-start(bf16[64,8,1024]{2,1,0:T(8,128)(2,1)} %broadcast_select_fusion), calls=%async_computation.1 | async-start | bytes 2097152 | tf_op jit(solution)/shard_map/all_to_all | solution.py:112
  54.1 84.3 %all-gather.2.cloned.1.call-start = ((), (), s32[]{:S(2)}) async-start(), calls=%async_computation.5 | async-start | bytes 7798784 | tf_op jit(solution)/shard_map/all_gather | solution.py:123
  138.5 41.0 %collective-permute-start = (bf16[3584,1024]{1,0:T(8,128)(2,1)}, bf16[3584,1024]{1,0:T(8,128)(2,1)}, u32[]{:S(2)}, u32[]{:S(2)}) collective-permute-start(bf16[3584,1024]{1,0:T(8,128)(2,1)} %all-gather.2.cloned.1.call-done.mine_ref), channel_id=1, source_target_pairs={{0,1},{1,0},{2,3},{3,2},{4,5},{5,4},{6,7},{7,6},{8,9},{9,8},{10,11... | collective-permute-start | bytes 22020104 | tf_op jit(solution)/shard_map/ppermute | solution.py:125
  139.3 38.2 %all-to-all-start.2 = ((bf16[16,600,128]{2,1,0:T(8,128)(2,1)}), bf16[16,600,128]{2,1,0:T(8,128)(2,1)S(1)}, u32[]{:S(2)}, u32[]{:S(2)}) async-start(bf16[16,600,128]{2,1,0:T(8,128)(2,1)} %bitcast.92), calls=%async_computation.2 | async-start | bytes 4915200 | tf_op jit(solution)/shard_map/all_to_all | solution.py:91
  202.5 13.4 %all-to-all-start.3 = ((f32[16,4,4,128]{3,1,2,0:T(4,128)}), f32[16,4,4,128]{3,1,2,0:T(4,128)S(1)}, u32[]{:S(2)}, u32[]{:S(2)}) async-start(f32[16,4,4,128]{3,1,2,0:T(4,128)} %bitcast.24), calls=%async_computation.3 | async-start | bytes 262144 | tf_op jit(solution)/shard_map/all_to_all | solution.py:169
  216.7 11.9 %all-to-all-start.4 = ((f32[8,4,4,128]{3,2,1,0:T(4,128)}), f32[8,4,4,128]{3,2,1,0:T(4,128)S(1)}, u32[]{:S(2)}, u32[]{:S(2)}) async-start(f32[8,4,4,128]{3,2,1,0:T(4,128)} %broadcast_in_dim.155), calls=%async_computation.4 | async-start | bytes 131072 | tf_op jit(solution)/shard_map/all_to_all | solution.py:35
Sparse Core Ops, SparseCore 0:
  70.8 67.5 all-gather.1

commit v13 on v11

--- a/solution.py
+++ b/solution.py
@@ -90,8 +90,11 @@
 
     emb_piece = lax.all_to_all(embedding, "req", split_axis=0, concat_axis=1, tiled=True)
 
-    normed_home = normalize(hidden, gain)
-    my_half = lax.dynamic_slice_in_dim(normed_home, core * half, half, axis=2)
+    wide = hidden.astype(jnp.float32)
+    scale = lax.rsqrt(jnp.mean(wide * wide, axis=-1, keepdims=True) + eps)
+    half_rows = lax.dynamic_slice_in_dim(hidden, core * half, half, axis=2).astype(jnp.float32)
+    half_gain = lax.dynamic_slice_in_dim(gain, core * half, half)
+    my_half = (half_rows * scale * half_gain).astype(jnp.bfloat16)
     block = slot_len // n_req
     digits = jnp.stack([targets // 16384, (targets // 128) % 128, targets % 128], axis=1)
     bounds = jnp.zeros((per_dev, 1, slot_len), jnp.int32)

time: 236 us -> 233 us (0.987)
  other arithmetic: 19.3 us -> 15.2 us
    convert_element_type x1 -> x0, other arithmetic: 2.45 us -> none  [normalize(): wide_rows = rows.astype(jnp.float32)]
where the time goes in v13:
time: 233 us; the launch traced here: 232 us
  waiting for transfers between devices  129 us (55%)
  starting transfers between devices  31.3 us (13%)
  local copies, waits for them, and re-layouts  22 us (9%)
  Pallas kernels  16.1 us (7%)
  other arithmetic  15.2 us (7%)
  between operations  14.5 us (6%)
  matrix products  4.07 us (2%)
    all_gather x1, waiting for transfers between devices, shards(): rows_mine = lax.all_gather(compact_half, 'req', axis=0, tiled=True)  67.8 us
    all_to_all x1, waiting for transfers between devices, shards(): lax.all_to_all(embedding, 'req', split_axis=0, concat_axis=1, tiled=True)  22 us
    all_to_all x1, waiting for transfers between devices, shards(): lax.all_to_all(blocks, 'req', split_axis=0, concat_axis=0, tiled=True)  16.1 us
    pallas_call x1, Pallas kernels, row_stats(): pl.pallas_call(stats_kernel, grid=(n_rows // tile,), in_specs=[pl.BlockSp...  16.1 us
    all_to_all x1, waiting for transfers between devices, shards(): lax.all_to_all(dealt_rows, 'req', split_axis=0, concat_axis=1, tiled=True)  12.9 us
    all_to_all x1, starting transfers between devices, shards(): lax.all_to_all(blocks, 'req', split_axis=0, concat_axis=0, tiled=True)  7.57 us
    all_to_all x1, starting transfers between devices, gather_by_all_to_all(): return lax.all_to_all(tiles, axis, split_axis=0, concat_axis=0, tiled=True)  7.01 us
    all_to_all x1, starting transfers between devices, shards(): lax.all_to_all(to_home, 'req', split_axis=0, concat_axis=0, tiled=True)  6.74 us
  transfers between devices with their start and end apart: 7, of which 6 were waited for; matrix products, arithmetic and copies ran while one was open for 7% of the time, Pallas kernels for 0%

profile of v13, /device:TPU:1, one launch (start us, length us, event | category | flops | bytes accessed | tf_op | source)
XLA Modules:
  0.0 232.3 jit_solution(5928021717101605384)
XLA Ops:
  7.2 0.6 slice.91
  7.8 0.8 copy.161
  8.6 0.7 copy.162
  9.3 0.8 scatter.9
  10.1 2.1 multiply_reduce_fusion
  12.8 0.4 maximum_bitcast_fusion
  13.2 2.1 copy.167
  15.3 7.6 %all-to-all-start = ((bf16[16,4,9,1024]{3,1,2,0:T(4,128)(2,1)}), bf16[16,4,9,1024]{3,1,2,0:T(4,128)(2,1)S(1)}, u32[]{:S(2)}, u32[]{:S(2)}) async-start(bf16[16,4,9,1024]{3,1,2,0:T(4,128)(2,1)} %copy.167), calls=%async_computation | async-start | bytes 2359296 | tf_op jit(solution)/shard_map/all_to_all | solution.py:108
  23.0 0.6 gather_fusion.9
  23.7 16.1 %all-to-all-done = bf16[16,4,9,1024]{3,1,2,0:T(4,128)(2,1)S(1)} async-done(((bf16[16,4,9,1024]{3,1,2,0:T(4,128)(2,1)}), bf16[16,4,9,1024]{3,1,2,0:T(4,128)(2,1)S(1)}, u32[]{:S(2)}, u32[]{:S(2)}) %all-to-all-start) | async-done | bytes 1179680 | tf_op jit(solution)/shard_map/all_to_all | solution.py:108
  40.0 0.5 slice.138
  40.5 0.4 copy.190
  40.8 2.4 %slice_reduce_fusion.1 = (s32[64]{0:T(128)S(1)}, s32[64]{0:T(128)S(1)}) fusion(s32[64,4,128]{2,1,0:T(4,128)S(1)} %reshape.310), kind=kLoop, calls=%fused_computation.34 | loop fusion | bytes 1024 | tf_op jit(solution)/shard_map/slice | solution.py:113
  43.3 0.6 gather_fusion.10
  43.9 0.6 gather_fusion.11
  44.6 0.6 fusion.26
  45.4 0.6 gather_fusion.1
  46.0 1.2 broadcast_select_fusion
  47.2 4.1 %all-to-all-start.1 = ((bf16[64,8,1024]{2,1,0:T(8,128)(2,1)}), bf16[64,8,1024]{2,1,0:T(8,128)(2,1)S(1)}, u32[]{:S(2)}, u32[]{:S(2)}) async-start(bf16[64,8,1024]{2,1,0:T(8,128)(2,1)} %broadcast_select_fusion), calls=%async_computation.1 | async-start | bytes 2097152 | tf_op jit(solution)/shard_map/all_to_all | solution.py:115
  51.6 0.7 compare_select_fusion.1
  52.2 0.7 compare_and_fusion.4
  52.9 12.9 %all-to-all-done.1 = bf16[64,8,1024]{2,1,0:T(8,128)(2,1)S(1)} async-done(((bf16[64,8,1024]{2,1,0:T(8,128)(2,1)}), bf16[64,8,1024]{2,1,0:T(8,128)(2,1)S(1)}, u32[]{:S(2)}, u32[]{:S(2)}) %all-to-all-start.1) | async-done | bytes 1048608 | tf_op jit(solution)/shard_map/all_to_all | solution.py:115
  65.9 1.1 gather_fusion.2
  67.0 0.9 broadcast_select_fusion.1
  67.9 67.8 %all-gather.2.cloned.1.call-done.mine_ref = bf16[3584,1024]{1,0:T(8,128)(2,1)} async-done(((bf16[224,1024]{1,0:T(8,128)(2,1)}), bf16[3584,1024]{1,0:T(8,128)(2,1)}) %all-gather.2.cloned.1.call-update) | async-done | bytes 7340048 | tf_op jit(solution)/shard_map/all_gather | solution.py:126
  135.7 0.8 collective-permute-start
  136.5 5.0 %all-to-all-start.2 = ((bf16[16,600,128]{2,1,0:T(8,128)(2,1)}), bf16[16,600,128]{2,1,0:T(8,128)(2,1)S(1)}, u32[]{:S(2)}, u32[]{:S(2)}) async-start(bf16[16,600,128]{2,1,0:T(8,128)(2,1)} %bitcast.92), calls=%async_computation.2 | async-start | bytes 4915200 | tf_op jit(solution)/shard_map/all_to_all | solution.py:91
  141.8 0.8 gather_fusion.7
  142.5 0.8 gather_fusion.8
  143.4 0.6 gather_fusion
  144.8 6.3 %select_reduce_fusion = s32[16,224]{1,0:T(8,128)S(1)} fusion(s32[16,4,128]{2,1,0:T(4,128)S(1)} %broadcast_select_fusion.2, s32[16,4,224]{2,1,0:T(4,128)S(1)} %subtract_add_fusion, pred[16,4,224]{2,1,0:T(4,128)(4,1)S(1)} %fusion.7), kind=kLoop, calls=%fused_computation.13 | loop fusion | flops 7336448 | bytes 118784 | tf_op jit(solution)/shard_map/reduce_sum | solution.py:144
  151.1 0.7 sub.110.ids_ref
  151.8 0.8 gather_fusion.4
  152.7 22.0 %all-to-all-done.2 = bf16[16,600,128]{2,1,0:T(8,128)(2,1)S(1)} async-done(((bf16[16,600,128]{2,1,0:T(8,128)(2,1)}), bf16[16,600,128]{2,1,0:T(8,128)(2,1)S(1)}, u32[]{:S(2)}, u32[]{:S(2)}) %all-to-all-start.2) | async-done | bytes 2457632 | tf_op jit(solution)/shard_map/all_to_all | solution.py:91
  174.7 0.3 copy_bitcast_fusion
  175.0 1.7 constant_dynamic-slice_fusion
  176.7 16.1 %shard_map.86 = f32[8,3584]{1,0:T(8,128)} custom-call(s32[1,3584]{1,0:T(1,128)} %sub.110.ids_ref, bf16[3584,1024]{1,0:T(8,128)(2,1)} %all-gather.2.cloned.1.call-done.mine_ref, bf16[3584,1024]{1,0:T(8,128)(2,1)} %collective-permute-done.other_ref, bf16[600,1024]{1,0:T(8,128)(2,1)} %get-tuple-element.41.emb_mine_ref, ...), custom_call_target="tpu_custom_call" | custom-call | tf_op jit(solution)/shard_map/pallas_call | solution.py:59
  192.8 0.9 slice.139
  193.8 0.7 gather_fusion.3
  194.6 4.1 %fusion.1 = f32[64,4,128]{2,1,0:T(4,128)} fusion(s32[64,128]{1,0:T(8,128)S(1)} %iota_add_fusion, f32[64,4,224]{2,1,0:T(4,128)S(1)} %gather_fusion.3, pred[64]{0:T(512)(128)(4,1)S(1)} %get-tuple-element.34), kind=kOutput, calls=%fused_computation.16 | convolution fusion | flops 89972736 | bytes 393280 | tf_op jit(solution)/shard_map/dot_general | solution.py:164
  198.6 6.7 %all-to-all-start.3 = ((f32[16,4,4,128]{3,1,2,0:T(4,128)}), f32[16,4,4,128]{3,1,2,0:T(4,128)S(1)}, u32[]{:S(2)}, u32[]{:S(2)}) async-start(f32[16,4,4,128]{3,1,2,0:T(4,128)} %bitcast.24), calls=%async_computation.3 | async-start | bytes 262144 | tf_op jit(solution)/shard_map/all_to_all | solution.py:172
  205.4 0.6 gather_fusion.6
  206.0 0.6 gather_fusion.5
  206.7 5.4 %all-to-all-done.3 = f32[16,4,4,128]{3,1,2,0:T(4,128)S(1)} async-done(((f32[16,4,4,128]{3,1,2,0:T(4,128)}), f32[16,4,4,128]{3,1,2,0:T(4,128)S(1)}, u32[]{:S(2)}, u32[]{:S(2)}) %all-to-all-start.3) | async-done | bytes 131104 | tf_op jit(solution)/shard_map/all_to_all | solution.py:172
  212.3 0.6 broadcast_in_dim.155
  212.9 7.0 %all-to-all-start.4 = ((f32[8,4,4,128]{3,2,1,0:T(4,128)}), f32[8,4,4,128]{3,2,1,0:T(4,128)S(1)}, u32[]{:S(2)}, u32[]{:S(2)}) async-start(f32[8,4,4,128]{3,2,1,0:T(4,128)} %broadcast_in_dim.155), calls=%async_computation.4 | async-start | bytes 131072 | tf_op jit(solution)/shard_map/all_to_all | solution.py:35
  219.9 4.8 %all-to-all-done.4 = f32[8,4,4,128]{3,2,1,0:T(4,128)S(1)} async-done(((f32[8,4,4,128]{3,2,1,0:T(4,128)}), f32[8,4,4,128]{3,2,1,0:T(4,128)S(1)}, u32[]{:S(2)}, u32[]{:S(2)}) %all-to-all-start.4) | async-done | bytes 65568 | tf_op jit(solution)/shard_map/all_to_all | solution.py:35
  224.8 0.7 subtract_select_fusion
  (76 shorter events, 2.9 us)
Async XLA Ops:
  7.2 5.2 %copy-start = (bf16[4,128,2048]{2,1,0:T(8,128)(2,1)S(1)}, bf16[4,128,2048]{2,1,0:T(8,128)(2,1)}, u32[]{:S(2)}) copy-start(bf16[4,128,2048]{2,1,0:T(8,128)(2,1)} %param.15) | copy-start | bytes 6291460
  7.2 5.0 %copy-start.2 = (s32[4,128]{1,0:T(4,128)S(1)}, s32[4,128]{1,0:T(4,128)}, u32[]{:S(2)}) copy-start(s32[4,128]{1,0:T(4,128)} %param.18) | copy-start | bytes 6148
  7.2 5.1 %copy-start.1 = (f32[2048]{0:T(1024)S(1)}, f32[2048]{0:T(1024)}, u32[]{:S(2)}) copy-start(f32[2048]{0:T(1024)} %param.16) | copy-start | bytes 24580
  13.2 9.7 %copy-start.3 = (s32[64]{0:T(128)S(1)}, s32[64]{0:T(128)}, u32[]{:S(2)}) copy-start(s32[64]{0:T(128)} %param.21) | copy-start | bytes 772
  15.3 24.6 %all-to-all-start = ((bf16[16,4,9,1024]{3,1,2,0:T(4,128)(2,1)}), bf16[16,4,9,1024]{3,1,2,0:T(4,128)(2,1)S(1)}, u32[]{:S(2)}, u32[]{:S(2)}) async-start(bf16[16,4,9,1024]{3,1,2,0:T(4,128)(2,1)} %copy.167), calls=%async_computation | async-start | bytes 2359296 | tf_op jit(solution)/shard_map/all_to_all | solution.py:108
  47.2 18.7 %all-to-all-start.1 = ((bf16[64,8,1024]{2,1,0:T(8,128)(2,1)}), bf16[64,8,1024]{2,1,0:T(8,128)(2,1)S(1)}, u32[]{:S(2)}, u32[]{:S(2)}) async-start(bf16[64,8,1024]{2,1,0:T(8,128)(2,1)} %broadcast_select_fusion), calls=%async_computation.1 | async-start | bytes 2097152 | tf_op jit(solution)/shard_map/all_to_all | solution.py:115
  51.3 84.3 %all-gather.2.cloned.1.call-start = ((), (), s32[]{:S(2)}) async-start(), calls=%async_computation.5 | async-start | bytes 7798784 | tf_op jit(solution)/shard_map/all_gather | solution.py:126
  135.7 41.0 %collective-permute-start = (bf16[3584,1024]{1,0:T(8,128)(2,1)}, bf16[3584,1024]{1,0:T(8,128)(2,1)}, u32[]{:S(2)}, u32[]{:S(2)}) collective-permute-start(bf16[3584,1024]{1,0:T(8,128)(2,1)} %all-gather.2.cloned.1.call-done.mine_ref), channel_id=1, source_target_pairs={{0,1},{1,0},{2,3},{3,2},{4,5},{5,4},{6,7},{7,6},{8,9},{9,8},{10,11... | collective-permute-start | bytes 22020104 | tf_op jit(solution)/shard_map/ppermute | solution.py:128
  136.5 38.2 %all-to-all-start.2 = ((bf16[16,600,128]{2,1,0:T(8,128)(2,1)}), bf16[16,600,128]{2,1,0:T(8,128)(2,1)S(1)}, u32[]{:S(2)}, u32[]{:S(2)}) async-start(bf16[16,600,128]{2,1,0:T(8,128)(2,1)} %bitcast.92), calls=%async_computation.2 | async-start | bytes 4915200 | tf_op jit(solution)/shard_map/all_to_all | solution.py:91
  198.6 13.4 %all-to-all-start.3 = ((f32[16,4,4,128]{3,1,2,0:T(4,128)}), f32[16,4,4,128]{3,1,2,0:T(4,128)S(1)}, u32[]{:S(2)}, u32[]{:S(2)}) async-start(f32[16,4,4,128]{3,1,2,0:T(4,128)} %bitcast.24), calls=%async_computation.3 | async-start | bytes 262144 | tf_op jit(solution)/shard_map/all_to_all | solution.py:172
  212.9 11.9 %all-to-all-start.4 = ((f32[8,4,4,128]{3,2,1,0:T(4,128)}), f32[8,4,4,128]{3,2,1,0:T(4,128)S(1)}, u32[]{:S(2)}, u32[]{:S(2)}) async-start(f32[8,4,4,128]{3,2,1,0:T(4,128)} %broadcast_in_dim.155), calls=%async_computation.4 | async-start | bytes 131072 | tf_op jit(solution)/shard_map/all_to_all | solution.py:35
Sparse Core Ops, SparseCore 0:
  68.0 67.5 all-gather.1

commit v14 on v13

--- a/solution.py
+++ b/solution.py
@@ -169,8 +169,10 @@
         preferred_element_type=jnp.float32,
     )
     to_home = picked.reshape(n_req, per_dev, 4, slot_len).transpose(0, 2, 1, 3)
-    by_req = merge(lax.all_to_all(to_home, "req", split_axis=0, concat_axis=0, tiled=True))
-    row_top, row_mass, row_spread, row_target = merge(gather_by_all_to_all(by_req, "vocab", n_voc))
+    to_all = jnp.broadcast_to(to_home[:, None], (n_req, n_voc) + to_home.shape[1:])
+    to_all = to_all.reshape((n_req * n_voc,) + to_home.shape[1:])
+    from_all = lax.all_to_all(to_all, ("req", "vocab"), split_axis=0, concat_axis=0, tiled=True)
+    row_top, row_mass, row_spread, row_target = merge(from_all)
     log_mass = jnp.log(row_mass)
 
     my_reqs = here * per_dev + jnp.arange(per_dev, dtype=jnp.int32)

time: 233 us -> 237 us (1.017)
  waiting for transfers between devices: 129 us -> 137 us
  starting transfers between devices: 31.3 us -> 27.8 us
    all_to_all x2 -> x1, waiting for transfers between devices: 10.3 us -> 17.9 us  [shards(): lax.all_to_all(to_all, ('req', 'vocab'), split_axis=0, concat_axis=0, til...]
    all_to_all x2 -> x1, starting transfers between devices: 13.8 us -> 10.3 us  [shards(): lax.all_to_all(to_all, ('req', 'vocab'), split_axis=0, concat_axis=0, til...]
  transfers between devices with their start and end apart: 7 -> 6, of which waited for: 6 -> 5; matrix products, arithmetic and copies ran while one was open for 7% -> 7% of each run, Pallas kernels for 0% -> 0%
where the time goes in v14:
time: 237 us
  waiting for transfers between devices  137 us (58%)
  starting transfers between devices  27.8 us (12%)
  local copies, waits for them, and re-layouts  22.5 us (9%)
  Pallas kernels  16.1 us (7%)
  other arithmetic  15.5 us (7%)
  between operations  14.5 us (6%)
  matrix products  3.42 us (1%)
    all_gather x1, waiting for transfers between devices, shards(): rows_mine = lax.all_gather(compact_half, 'req', axis=0, tiled=True)  67.8 us
    all_to_all x1, waiting for transfers between devices, shards(): lax.all_to_all(embedding, 'req', split_axis=0, concat_axis=1, tiled=True)  22 us
    all_to_all x1, waiting for transfers between devices, shards(): lax.all_to_all(to_all, ('req', 'vocab'), split_axis=0, concat_axis=0, til...  17.9 us
    all_to_all x1, waiting for transfers between devices, shards(): lax.all_to_all(blocks, 'req', split_axis=0, concat_axis=0, tiled=True)  16.1 us
    pallas_call x1, Pallas kernels, row_stats(): pl.pallas_call(stats_kernel, grid=(n_rows // tile,), in_specs=[pl.BlockSp...  16.1 us
    all_to_all x1, waiting for transfers between devices, shards(): lax.all_to_all(dealt_rows, 'req', split_axis=0, concat_axis=1, tiled=True)  12.9 us
    all_to_all x1, starting transfers between devices, shards(): lax.all_to_all(to_all, ('req', 'vocab'), split_axis=0, concat_axis=0, til...  10.3 us
    all_to_all x1, starting transfers between devices, shards(): lax.all_to_all(blocks, 'req', split_axis=0, concat_axis=0, tiled=True)  7.57 us
  transfers between devices with their start and end apart: 6, of which 5 were waited for; matrix products, arithmetic and copies ran while one was open for 7% of the time, Pallas kernels for 0%

profile of v14, /device:TPU:1, one launch (start us, length us, event | category | flops | bytes accessed | tf_op | source)
XLA Modules:
  0.0 236.6 jit_solution(12530930010085387845)
XLA Ops:
  7.2 0.6 slice.79
  7.8 0.8 copy.152
  8.6 0.7 copy.153
  9.3 0.8 scatter.9
  10.1 2.1 multiply_reduce_fusion
  12.3 0.3 fusion.3
  12.8 0.4 maximum_bitcast_fusion
  13.2 2.1 copy.158
  15.3 7.6 %all-to-all-start = ((bf16[16,4,9,1024]{3,1,2,0:T(4,128)(2,1)}), bf16[16,4,9,1024]{3,1,2,0:T(4,128)(2,1)S(1)}, u32[]{:S(2)}, u32[]{:S(2)}) async-start(bf16[16,4,9,1024]{3,1,2,0:T(4,128)(2,1)} %copy.158), calls=%async_computation | async-start | bytes 2359296 | tf_op jit(solution)/shard_map/all_to_all | solution.py:108
  23.0 0.6 gather_fusion.9
  23.7 16.1 %all-to-all-done = bf16[16,4,9,1024]{3,1,2,0:T(4,128)(2,1)S(1)} async-done(((bf16[16,4,9,1024]{3,1,2,0:T(4,128)(2,1)}), bf16[16,4,9,1024]{3,1,2,0:T(4,128)(2,1)S(1)}, u32[]{:S(2)}, u32[]{:S(2)}) %all-to-all-start) | async-done | bytes 1179680 | tf_op jit(solution)/shard_map/all_to_all | solution.py:108
  40.0 0.5 slice.122
  40.5 0.4 copy.180
  40.8 2.4 %slice_reduce_fusion.1 = (s32[64]{0:T(128)S(1)}, s32[64]{0:T(128)S(1)}) fusion(s32[64,4,128]{2,1,0:T(4,128)S(1)} %reshape.313), kind=kLoop, calls=%fused_computation.43 | loop fusion | bytes 1024 | tf_op jit(solution)/shard_map/slice | solution.py:113
  43.3 0.6 gather_fusion.10
  43.9 0.6 gather_fusion.11
  44.6 0.6 fusion.26
  45.4 0.6 gather_fusion.1
  46.0 1.2 broadcast_select_fusion
  47.2 4.1 %all-to-all-start.1 = ((bf16[64,8,1024]{2,1,0:T(8,128)(2,1)}), bf16[64,8,1024]{2,1,0:T(8,128)(2,1)S(1)}, u32[]{:S(2)}, u32[]{:S(2)}) async-start(bf16[64,8,1024]{2,1,0:T(8,128)(2,1)} %broadcast_select_fusion), calls=%async_computation.1 | async-start | bytes 2097152 | tf_op jit(solution)/shard_map/all_to_all | solution.py:115
  51.6 0.7 compare_select_fusion.1
  52.2 0.7 compare_and_fusion.4
  52.9 12.9 %all-to-all-done.1 = bf16[64,8,1024]{2,1,0:T(8,128)(2,1)S(1)} async-done(((bf16[64,8,1024]{2,1,0:T(8,128)(2,1)}), bf16[64,8,1024]{2,1,0:T(8,128)(2,1)S(1)}, u32[]{:S(2)}, u32[]{:S(2)}) %all-to-all-start.1) | async-done | bytes 1048608 | tf_op jit(solution)/shard_map/all_to_all | solution.py:115
  65.9 1.1 gather_fusion.2
  67.0 0.9 broadcast_select_fusion.1
  67.9 67.8 %all-gather.2.cloned.1.call-done.mine_ref = bf16[3584,1024]{1,0:T(8,128)(2,1)} async-done(((bf16[224,1024]{1,0:T(8,128)(2,1)}), bf16[3584,1024]{1,0:T(8,128)(2,1)}) %all-gather.2.cloned.1.call-update) | async-done | bytes 7340048 | tf_op jit(solution)/shard_map/all_gather | solution.py:126
  135.7 0.8 collective-permute-start
  136.5 5.0 %all-to-all-start.2 = ((bf16[16,600,128]{2,1,0:T(8,128)(2,1)}), bf16[16,600,128]{2,1,0:T(8,128)(2,1)S(1)}, u32[]{:S(2)}, u32[]{:S(2)}) async-start(bf16[16,600,128]{2,1,0:T(8,128)(2,1)} %bitcast.82), calls=%async_computation.2 | async-start | bytes 4915200 | tf_op jit(solution)/shard_map/all_to_all | solution.py:91
  141.8 0.8 gather_fusion.7
  142.5 0.8 gather_fusion.8
  143.4 0.6 gather_fusion
  144.8 6.3 %select_reduce_fusion = s32[16,224]{1,0:T(8,128)S(1)} fusion(s32[16,4,128]{2,1,0:T(4,128)S(1)} %broadcast_select_fusion.2, s32[16,4,224]{2,1,0:T(4,128)S(1)} %subtract_add_fusion, pred[16,4,224]{2,1,0:T(4,128)(4,1)S(1)} %fusion.11), kind=kLoop, calls=%fused_computation.13 | loop fusion | flops 7336448 | bytes 118784 | tf_op jit(solution)/shard_map/reduce_sum | solution.py:144
  151.1 0.7 sub.102.ids_ref
  151.8 0.8 gather_fusion.4
  152.7 22.0 %all-to-all-done.2 = bf16[16,600,128]{2,1,0:T(8,128)(2,1)S(1)} async-done(((bf16[16,600,128]{2,1,0:T(8,128)(2,1)}), bf16[16,600,128]{2,1,0:T(8,128)(2,1)S(1)}, u32[]{:S(2)}, u32[]{:S(2)}) %all-to-all-start.2) | async-done | bytes 2457632 | tf_op jit(solution)/shard_map/all_to_all | solution.py:91
  174.7 0.3 copy_bitcast_fusion
  175.0 1.7 constant_dynamic-slice_fusion
  176.7 16.1 %shard_map.86 = f32[8,3584]{1,0:T(8,128)} custom-call(s32[1,3584]{1,0:T(1,128)} %sub.102.ids_ref, bf16[3584,1024]{1,0:T(8,128)(2,1)} %all-gather.2.cloned.1.call-done.mine_ref, bf16[3584,1024]{1,0:T(8,128)(2,1)} %collective-permute-done.other_ref, bf16[600,1024]{1,0:T(8,128)(2,1)} %get-tuple-element.39.emb_mine_ref, ...), custom_call_target="tpu_custom_call" | custom-call | tf_op jit(solution)/shard_map/pallas_call | solution.py:59
  192.8 0.9 slice.123
  193.8 0.7 gather_fusion.3
  194.6 3.4 %fusion.1 = f32[64,4,128]{2,1,0:T(4,128)S(1)} fusion(s32[64,128]{1,0:T(8,128)S(1)} %iota_add_fusion, f32[64,4,224]{2,1,0:T(4,128)S(1)} %gather_fusion.3, pred[64]{0:T(512)(128)(4,1)S(1)} %get-tuple-element.32), kind=kOutput, calls=%fused_computation.16 | convolution fusion | flops 89972736 | bytes 393280 | tf_op jit(solution)/shard_map/dot_general | solution.py:164
  198.0 1.2 broadcast_in_dim.154
  199.2 10.3 %all-to-all-start.3 = ((f32[128,4,4,128]{3,2,1,0:T(4,128)}), f32[128,4,4,128]{3,2,1,0:T(4,128)S(1)}, u32[]{:S(2)}, u32[]{:S(2)}) async-start(f32[128,4,4,128]{3,2,1,0:T(4,128)} %bitcast.25), calls=%async_computation.3 | async-start | bytes 2097152 | tf_op jit(solution)/shard_map/all_to_all | solution.py:174
  209.4 0.6 gather_fusion.6
  210.1 0.6 gather_fusion.5
  210.7 17.9 %all-to-all-done.3 = f32[128,4,4,128]{3,2,1,0:T(4,128)S(1)} async-done(((f32[128,4,4,128]{3,2,1,0:T(4,128)}), f32[128,4,4,128]{3,2,1,0:T(4,128)S(1)}, u32[]{:S(2)}, u32[]{:S(2)}) %all-to-all-start.3) | async-done | bytes 1048608 | tf_op jit(solution)/shard_map/all_to_all | solution.py:174
  228.9 0.2 fusion.6
  229.1 0.7 subtract_select_fusion
  (71 shorter events, 2.6 us)
Async XLA Ops:
  7.2 5.2 %copy-start = (bf16[4,128,2048]{2,1,0:T(8,128)(2,1)S(1)}, bf16[4,128,2048]{2,1,0:T(8,128)(2,1)}, u32[]{:S(2)}) copy-start(bf16[4,128,2048]{2,1,0:T(8,128)(2,1)} %param.15) | copy-start | bytes 6291460
  7.2 5.0 %copy-start.2 = (s32[4,128]{1,0:T(4,128)S(1)}, s32[4,128]{1,0:T(4,128)}, u32[]{:S(2)}) copy-start(s32[4,128]{1,0:T(4,128)} %param.18) | copy-start | bytes 6148
  7.2 5.1 %copy-start.1 = (f32[2048]{0:T(1024)S(1)}, f32[2048]{0:T(1024)}, u32[]{:S(2)}) copy-start(f32[2048]{0:T(1024)} %param.16) | copy-start | bytes 24580
  13.2 9.7 %copy-start.3 = (s32[64]{0:T(128)S(1)}, s32[64]{0:T(128)}, u32[]{:S(2)}) copy-start(s32[64]{0:T(128)} %param.21) | copy-start | bytes 772
  15.3 24.6 %all-to-all-start = ((bf16[16,4,9,1024]{3,1,2,0:T(4,128)(2,1)}), bf16[16,4,9,1024]{3,1,2,0:T(4,128)(2,1)S(1)}, u32[]{:S(2)}, u32[]{:S(2)}) async-start(bf16[16,4,9,1024]{3,1,2,0:T(4,128)(2,1)} %copy.158), calls=%async_computation | async-start | bytes 2359296 | tf_op jit(solution)/shard_map/all_to_all | solution.py:108
  47.2 18.7 %all-to-all-start.1 = ((bf16[64,8,1024]{2,1,0:T(8,128)(2,1)}), bf16[64,8,1024]{2,1,0:T(8,128)(2,1)S(1)}, u32[]{:S(2)}, u32[]{:S(2)}) async-start(bf16[64,8,1024]{2,1,0:T(8,128)(2,1)} %broadcast_select_fusion), calls=%async_computation.1 | async-start | bytes 2097152 | tf_op jit(solution)/shard_map/all_to_all | solution.py:115
  51.3 84.3 %all-gather.2.cloned.1.call-start = ((), (), s32[]{:S(2)}) async-start(), calls=%async_computation.4 | async-start | bytes 7798784 | tf_op jit(solution)/shard_map/all_gather | solution.py:126
  135.7 41.0 %collective-permute-start = (bf16[3584,1024]{1,0:T(8,128)(2,1)}, bf16[3584,1024]{1,0:T(8,128)(2,1)}, u32[]{:S(2)}, u32[]{:S(2)}) collective-permute-start(bf16[3584,1024]{1,0:T(8,128)(2,1)} %all-gather.2.cloned.1.call-done.mine_ref), channel_id=1, source_target_pairs={{0,1},{1,0},{2,3},{3,2},{4,5},{5,4},{6,7},{7,6},{8,9},{9,8},{10,11... | collective-permute-start | bytes 22020104 | tf_op jit(solution)/shard_map/ppermute | solution.py:128
  136.5 38.2 %all-to-all-start.2 = ((bf16[16,600,128]{2,1,0:T(8,128)(2,1)}), bf16[16,600,128]{2,1,0:T(8,128)(2,1)S(1)}, u32[]{:S(2)}, u32[]{:S(2)}) async-start(bf16[16,600,128]{2,1,0:T(8,128)(2,1)} %bitcast.82), calls=%async_computation.2 | async-start | bytes 4915200 | tf_op jit(solution)/shard_map/all_to_all | solution.py:91
  199.2 29.4 %all-to-all-start.3 = ((f32[128,4,4,128]{3,2,1,0:T(4,128)}), f32[128,4,4,128]{3,2,1,0:T(4,128)S(1)}, u32[]{:S(2)}, u32[]{:S(2)}) async-start(f32[128,4,4,128]{3,2,1,0:T(4,128)} %bitcast.25), calls=%async_computation.3 | async-start | bytes 2097152 | tf_op jit(solution)/shard_map/all_to_all | solution.py:174
Sparse Core Ops, SparseCore 0:
  68.0 67.5 all-gather.1

commit v15 on v13

--- a/solution.py
+++ b/solution.py
@@ -97,8 +97,9 @@
     my_half = (half_rows * scale * half_gain).astype(jnp.bfloat16)
     block = slot_len // n_req
     digits = jnp.stack([targets // 16384, (targets // 128) % 128, targets % 128], axis=1)
-    bounds = jnp.zeros((per_dev, 1, slot_len), jnp.int32)
-    bounds = bounds.at[:, 0, 0].set(span_start).at[:, 0, 1].set(span_len)
+    bounds = jnp.concatenate(
+        [span_start[:, None], span_len[:, None], jnp.zeros((per_dev, slot_len - 2), jnp.int32)], axis=1
+    )[:, None, :]
     meta = jnp.concatenate([digits, bounds], axis=1).astype(jnp.bfloat16).reshape(per_dev, 1, 1, -1)
     meta = jnp.pad(meta, ((0, 0), (0, 0), (0, 0), (0, half - meta.shape[3])))
     blocks = jnp.concatenate(

time: 233 us -> 232 us (level)
  local copies, waits for them, and re-layouts: 22 us -> 19.4 us
where the time goes in v15:
time: 232 us; the launch traced here: 231 us
  waiting for transfers between devices  129 us (56%)
  starting transfers between devices  31.3 us (13%)
  local copies, waits for them, and re-layouts  19.4 us (8%)
  other arithmetic  16.7 us (7%)
  Pallas kernels  16.1 us (7%)
  between operations  14.5 us (6%)
  matrix products  4.07 us (2%)
    all_gather x1, waiting for transfers between devices, shards(): rows_mine = lax.all_gather(compact_half, 'req', axis=0, tiled=True)  67.8 us
    all_to_all x1, waiting for transfers between devices, shards(): lax.all_to_all(embedding, 'req', split_axis=0, concat_axis=1, tiled=True)  22 us
    all_to_all x1, waiting for transfers between devices, shards(): lax.all_to_all(blocks, 'req', split_axis=0, concat_axis=0, tiled=True)  16.1 us
    pallas_call x1, Pallas kernels, row_stats(): pl.pallas_call(stats_kernel, grid=(n_rows // tile,), in_specs=[pl.BlockSp...  16.1 us
    all_to_all x1, waiting for transfers between devices, shards(): lax.all_to_all(dealt_rows, 'req', split_axis=0, concat_axis=1, tiled=True)  12.9 us
    all_to_all x1, starting transfers between devices, shards(): lax.all_to_all(blocks, 'req', split_axis=0, concat_axis=0, tiled=True)  7.57 us
    all_to_all x1, starting transfers between devices, gather_by_all_to_all(): return lax.all_to_all(tiles, axis, split_axis=0, concat_axis=0, tiled=True)  7.01 us
    all_to_all x1, starting transfers between devices, shards(): lax.all_to_all(to_home, 'req', split_axis=0, concat_axis=0, tiled=True)  6.74 us
  transfers between devices with their start and end apart: 7, of which 6 were waited for; matrix products, arithmetic and copies ran while one was open for 7% of the time, Pallas kernels for 0%

profile of v15, /device:TPU:1, one launch (start us, length us, event | category | flops | bytes accessed | tf_op | source)
XLA Modules:
  0.0 231.2 jit_solution(2708783817357732143)
XLA Ops:
  7.2 0.8 convert_bitcast_fusion.1
  8.1 0.7 convert_bitcast_fusion
  8.9 2.1 multiply_reduce_fusion
  11.2 0.3 fusion.3
  11.7 0.4 maximum_bitcast_fusion
  12.1 2.1 copy.70
  14.2 7.6 %all-to-all-start = ((bf16[16,4,9,1024]{3,1,2,0:T(4,128)(2,1)}), bf16[16,4,9,1024]{3,1,2,0:T(4,128)(2,1)S(1)}, u32[]{:S(2)}, u32[]{:S(2)}) async-start(bf16[16,4,9,1024]{3,1,2,0:T(4,128)(2,1)} %copy.70), calls=%async_computation | async-start | bytes 2359296 | tf_op jit(solution)/shard_map/all_to_all | solution.py:109
  21.9 0.6 gather_fusion.9
  22.6 16.1 %all-to-all-done = bf16[16,4,9,1024]{3,1,2,0:T(4,128)(2,1)S(1)} async-done(((bf16[16,4,9,1024]{3,1,2,0:T(4,128)(2,1)}), bf16[16,4,9,1024]{3,1,2,0:T(4,128)(2,1)S(1)}, u32[]{:S(2)}, u32[]{:S(2)}) %all-to-all-start) | async-done | bytes 1179680 | tf_op jit(solution)/shard_map/all_to_all | solution.py:109
  38.9 0.5 slice.94
  39.4 0.4 copy.93
  39.7 2.4 %slice_reduce_fusion.1 = (s32[64]{0:T(128)S(1)}, s32[64]{0:T(128)S(1)}) fusion(s32[64,4,128]{2,1,0:T(4,128)S(1)} %reshape.244), kind=kLoop, calls=%fused_computation.34 | loop fusion | bytes 1024 | tf_op jit(solution)/shard_map/slice | solution.py:114
  42.2 0.6 gather_fusion.10
  42.8 0.6 gather_fusion.11
  43.5 0.6 fusion.26
  44.1 0.2 reduce-window.9
  44.3 0.6 gather_fusion.1
  44.9 1.2 broadcast_select_fusion
  46.1 4.1 %all-to-all-start.1 = ((bf16[64,8,1024]{2,1,0:T(8,128)(2,1)}), bf16[64,8,1024]{2,1,0:T(8,128)(2,1)S(1)}, u32[]{:S(2)}, u32[]{:S(2)}) async-start(bf16[64,8,1024]{2,1,0:T(8,128)(2,1)} %broadcast_select_fusion), calls=%async_computation.1 | async-start | bytes 2097152 | tf_op jit(solution)/shard_map/all_to_all | solution.py:116
  50.5 0.7 compare_select_fusion.1
  51.1 0.7 compare_and_fusion.4
  51.8 12.9 %all-to-all-done.1 = bf16[64,8,1024]{2,1,0:T(8,128)(2,1)S(1)} async-done(((bf16[64,8,1024]{2,1,0:T(8,128)(2,1)}), bf16[64,8,1024]{2,1,0:T(8,128)(2,1)S(1)}, u32[]{:S(2)}, u32[]{:S(2)}) %all-to-all-start.1) | async-done | bytes 1048608 | tf_op jit(solution)/shard_map/all_to_all | solution.py:116
  64.8 1.1 gather_fusion.2
  65.9 0.9 broadcast_select_fusion.1
  66.8 67.8 %all-gather.2.cloned.1.call-done.mine_ref = bf16[3584,1024]{1,0:T(8,128)(2,1)} async-done(((bf16[224,1024]{1,0:T(8,128)(2,1)}), bf16[3584,1024]{1,0:T(8,128)(2,1)}) %all-gather.2.cloned.1.call-update) | async-done | bytes 7340048 | tf_op jit(solution)/shard_map/all_gather | solution.py:127
  134.5 0.8 collective-permute-start
  135.4 5.0 %all-to-all-start.2 = ((bf16[16,600,128]{2,1,0:T(8,128)(2,1)}), bf16[16,600,128]{2,1,0:T(8,128)(2,1)S(1)}, u32[]{:S(2)}, u32[]{:S(2)}) async-start(bf16[16,600,128]{2,1,0:T(8,128)(2,1)} %bitcast.97), calls=%async_computation.2 | async-start | bytes 4915200 | tf_op jit(solution)/shard_map/all_to_all | solution.py:91
  140.7 0.8 gather_fusion.7
  141.4 0.8 gather_fusion.8
  142.3 0.6 gather_fusion
  143.7 6.3 %select_reduce_fusion = s32[16,224]{1,0:T(8,128)S(1)} fusion(s32[16,4,128]{2,1,0:T(4,128)S(1)} %broadcast_select_fusion.2, s32[16,4,224]{2,1,0:T(4,128)S(1)} %subtract_add_fusion, pred[16,4,224]{2,1,0:T(4,128)(4,1)S(1)} %fusion.7), kind=kLoop, calls=%fused_computation.13 | loop fusion | flops 7336448 | bytes 118784 | tf_op jit(solution)/shard_map/reduce_sum | solution.py:145
  150.0 0.7 sub.110.ids_ref
  150.7 0.8 gather_fusion.4
  151.6 22.0 %all-to-all-done.2 = bf16[16,600,128]{2,1,0:T(8,128)(2,1)S(1)} async-done(((bf16[16,600,128]{2,1,0:T(8,128)(2,1)}), bf16[16,600,128]{2,1,0:T(8,128)(2,1)S(1)}, u32[]{:S(2)}, u32[]{:S(2)}) %all-to-all-start.2) | async-done | bytes 2457632 | tf_op jit(solution)/shard_map/all_to_all | solution.py:91
  173.6 0.3 copy_bitcast_fusion
  173.9 1.7 constant_dynamic-slice_fusion
  175.6 16.1 %shard_map.86 = f32[8,3584]{1,0:T(8,128)} custom-call(s32[1,3584]{1,0:T(1,128)} %sub.110.ids_ref, bf16[3584,1024]{1,0:T(8,128)(2,1)} %all-gather.2.cloned.1.call-done.mine_ref, bf16[3584,1024]{1,0:T(8,128)(2,1)} %collective-permute-done.other_ref, bf16[600,1024]{1,0:T(8,128)(2,1)} %get-tuple-element.17.emb_mine_ref, ...), custom_call_target="tpu_custom_call" | custom-call | tf_op jit(solution)/shard_map/pallas_call | solution.py:59
  191.7 0.9 slice.95
  192.7 0.7 gather_fusion.3
  193.5 4.1 %fusion.1 = f32[64,4,128]{2,1,0:T(4,128)} fusion(s32[64,128]{1,0:T(8,128)S(1)} %iota_add_fusion, f32[64,4,224]{2,1,0:T(4,128)S(1)} %gather_fusion.3, pred[64]{0:T(512)(128)(4,1)S(1)} %get-tuple-element.10), kind=kOutput, calls=%fused_computation.16 | convolution fusion | flops 89972736 | bytes 393280 | tf_op jit(solution)/shard_map/dot_general | solution.py:165
  197.5 6.7 %all-to-all-start.3 = ((f32[16,4,4,128]{3,1,2,0:T(4,128)}), f32[16,4,4,128]{3,1,2,0:T(4,128)S(1)}, u32[]{:S(2)}, u32[]{:S(2)}) async-start(f32[16,4,4,128]{3,1,2,0:T(4,128)} %bitcast.25), calls=%async_computation.3 | async-start | bytes 262144 | tf_op jit(solution)/shard_map/all_to_all | solution.py:173
  204.3 0.6 gather_fusion.6
  204.9 0.6 gather_fusion.5
  205.6 5.4 %all-to-all-done.3 = f32[16,4,4,128]{3,1,2,0:T(4,128)S(1)} async-done(((f32[16,4,4,128]{3,1,2,0:T(4,128)}), f32[16,4,4,128]{3,1,2,0:T(4,128)S(1)}, u32[]{:S(2)}, u32[]{:S(2)}) %all-to-all-start.3) | async-done | bytes 131104 | tf_op jit(solution)/shard_map/all_to_all | solution.py:173
  211.2 0.6 broadcast_in_dim.173
  211.8 7.0 %all-to-all-start.4 = ((f32[8,4,4,128]{3,2,1,0:T(4,128)}), f32[8,4,4,128]{3,2,1,0:T(4,128)S(1)}, u32[]{:S(2)}, u32[]{:S(2)}) async-start(f32[8,4,4,128]{3,2,1,0:T(4,128)} %broadcast_in_dim.173), calls=%async_computation.4 | async-start | bytes 131072 | tf_op jit(solution)/shard_map/all_to_all | solution.py:35
  218.8 4.8 %all-to-all-done.4 = f32[8,4,4,128]{3,2,1,0:T(4,128)S(1)} async-done(((f32[8,4,4,128]{3,2,1,0:T(4,128)}), f32[8,4,4,128]{3,2,1,0:T(4,128)S(1)}, u32[]{:S(2)}, u32[]{:S(2)}) %all-to-all-start.4) | async-done | bytes 65568 | tf_op jit(solution)/shard_map/all_to_all | solution.py:35
  223.7 0.7 subtract_select_fusion
  (71 shorter events, 2.7 us)
Async XLA Ops:
  7.2 4.1 %copy-start = (bf16[4,128,2048]{2,1,0:T(8,128)(2,1)S(1)}, bf16[4,128,2048]{2,1,0:T(8,128)(2,1)}, u32[]{:S(2)}) copy-start(bf16[4,128,2048]{2,1,0:T(8,128)(2,1)} %param.11) | copy-start | bytes 6291460
  7.2 3.8 %copy-start.2 = (s32[4,128]{1,0:T(4,128)S(1)}, s32[4,128]{1,0:T(4,128)}, u32[]{:S(2)}) copy-start(s32[4,128]{1,0:T(4,128)} %param.14) | copy-start | bytes 6148
  7.2 4.0 %copy-start.1 = (f32[2048]{0:T(1024)S(1)}, f32[2048]{0:T(1024)}, u32[]{:S(2)}) copy-start(f32[2048]{0:T(1024)} %param.12) | copy-start | bytes 24580
  12.1 9.7 %copy-start.3 = (s32[64]{0:T(128)S(1)}, s32[64]{0:T(128)}, u32[]{:S(2)}) copy-start(s32[64]{0:T(128)} %param.17) | copy-start | bytes 772
  14.2 24.6 %all-to-all-start = ((bf16[16,4,9,1024]{3,1,2,0:T(4,128)(2,1)}), bf16[16,4,9,1024]{3,1,2,0:T(4,128)(2,1)S(1)}, u32[]{:S(2)}, u32[]{:S(2)}) async-start(bf16[16,4,9,1024]{3,1,2,0:T(4,128)(2,1)} %copy.70), calls=%async_computation | async-start | bytes 2359296 | tf_op jit(solution)/shard_map/all_to_all | solution.py:109
  46.1 18.7 %all-to-all-start.1 = ((bf16[64,8,1024]{2,1,0:T(8,128)(2,1)}), bf16[64,8,1024]{2,1,0:T(8,128)(2,1)S(1)}, u32[]{:S(2)}, u32[]{:S(2)}) async-start(bf16[64,8,1024]{2,1,0:T(8,128)(2,1)} %broadcast_select_fusion), calls=%async_computation.1 | async-start | bytes 2097152 | tf_op jit(solution)/shard_map/all_to_all | solution.py:116
  50.2 84.3 %all-gather.2.cloned.1.call-start = ((), (), s32[]{:S(2)}) async-start(), calls=%async_computation.5 | async-start | bytes 7798784 | tf_op jit(solution)/shard_map/all_gather | solution.py:127
  134.5 41.0 %collective-permute-start = (bf16[3584,1024]{1,0:T(8,128)(2,1)}, bf16[3584,1024]{1,0:T(8,128)(2,1)}, u32[]{:S(2)}, u32[]{:S(2)}) collective-permute-start(bf16[3584,1024]{1,0:T(8,128)(2,1)} %all-gather.2.cloned.1.call-done.mine_ref), channel_id=1, source_target_pairs={{0,1},{1,0},{2,3},{3,2},{4,5},{5,4},{6,7},{7,6},{8,9},{9,8},{10,11... | collective-permute-start | bytes 22020104 | tf_op jit(solution)/shard_map/ppermute | solution.py:129
  135.4 38.2 %all-to-all-start.2 = ((bf16[16,600,128]{2,1,0:T(8,128)(2,1)}), bf16[16,600,128]{2,1,0:T(8,128)(2,1)S(1)}, u32[]{:S(2)}, u32[]{:S(2)}) async-start(bf16[16,600,128]{2,1,0:T(8,128)(2,1)} %bitcast.97), calls=%async_computation.2 | async-start | bytes 4915200 | tf_op jit(solution)/shard_map/all_to_all | solution.py:91
  197.5 13.4 %all-to-all-start.3 = ((f32[16,4,4,128]{3,1,2,0:T(4,128)}), f32[16,4,4,128]{3,1,2,0:T(4,128)S(1)}, u32[]{:S(2)}, u32[]{:S(2)}) async-start(f32[16,4,4,128]{3,1,2,0:T(4,128)} %bitcast.25), calls=%async_computation.3 | async-start | bytes 262144 | tf_op jit(solution)/shard_map/all_to_all | solution.py:173
  211.8 11.9 %all-to-all-start.4 = ((f32[8,4,4,128]{3,2,1,0:T(4,128)}), f32[8,4,4,128]{3,2,1,0:T(4,128)S(1)}, u32[]{:S(2)}, u32[]{:S(2)}) async-start(f32[8,4,4,128]{3,2,1,0:T(4,128)} %broadcast_in_dim.173), calls=%async_computation.4 | async-start | bytes 131072 | tf_op jit(solution)/shard_map/all_to_all | solution.py:35
Sparse Core Ops, SparseCore 0:
  66.9 67.5 all-gather.1

commit v16 on v13

--- a/solution.py
+++ b/solution.py
@@ -50,7 +50,6 @@
     out_ref[1:2, :] = jnp.sum(weights, axis=0, keepdims=True)
     out_ref[2:3, :] = jnp.sum(weights * shifted, axis=0, keepdims=True)
     out_ref[3:4, :] = target
-    out_ref[4:8, :] = jnp.zeros((4, top.shape[1]), jnp.float32)
 
 
 def row_stats(ids, rows_mine, rows_other, emb_mine, emb_other, tile=512):
@@ -66,8 +65,8 @@
             pl.BlockSpec((vocab, feat), lambda i: (0, 0)),
             pl.BlockSpec((vocab, feat), lambda i: (0, 0)),
         ],
-        out_specs=pl.BlockSpec((8, tile), lambda i: (0, i)),
-        out_shape=jax.ShapeDtypeStruct((8, n_rows), jnp.float32),
+        out_specs=pl.BlockSpec((4, tile), lambda i: (0, i)),
+        out_shape=jax.ShapeDtypeStruct((4, n_rows), jnp.float32),
     )(ids, rows_mine, rows_other, emb_mine, emb_other)
 
 
@@ -144,7 +143,7 @@
     target_ids = jnp.sum(jnp.where(hit, member_targets[:, :, None, :], 0), axis=(1, 3)).reshape(-1)
 
     local_ids = (target_ids - (vhere * voc_local + here * piece)).reshape(1, -1)
-    local_stats = row_stats(local_ids, rows_mine, rows_other, emb_mine, emb_other)[:4]
+    local_stats = row_stats(local_ids, rows_mine, rows_other, emb_mine, emb_other)
 
     def merge(stats):
         top_each, mass_each, spread_each, target_each = stats[:, 0], stats[:, 1], stats[:, 2], stats[:, 3]

time: 233 us -> 233 us (level)
  no operation moved by 1% of the time
where the time goes in v16:
time: 233 us; the launch traced here: 232 us
  waiting for transfers between devices  129 us (55%)
  starting transfers between devices  31.3 us (13%)
  local copies, waits for them, and re-layouts  21.9 us (9%)
  Pallas kernels  16.1 us (7%)
  other arithmetic  15.2 us (7%)
  between operations  14.5 us (6%)
  matrix products  4.07 us (2%)
    all_gather x1, waiting for transfers between devices, shards(): rows_mine = lax.all_gather(compact_half, 'req', axis=0, tiled=True)  67.8 us
    all_to_all x1, waiting for transfers between devices, shards(): lax.all_to_all(embedding, 'req', split_axis=0, concat_axis=1, tiled=True)  22 us
    all_to_all x1, waiting for transfers between devices, shards(): lax.all_to_all(blocks, 'req', split_axis=0, concat_axis=0, tiled=True)  16.1 us
    pallas_call x1, Pallas kernels, row_stats(): pl.pallas_call(stats_kernel, grid=(n_rows // tile,), in_specs=[pl.BlockSp...  16.1 us
    all_to_all x1, waiting for transfers between devices, shards(): lax.all_to_all(dealt_rows, 'req', split_axis=0, concat_axis=1, tiled=True)  12.9 us
    all_to_all x1, starting transfers between devices, shards(): lax.all_to_all(blocks, 'req', split_axis=0, concat_axis=0, tiled=True)  7.57 us
    all_to_all x1, starting transfers between devices, gather_by_all_to_all(): return lax.all_to_all(tiles, axis, split_axis=0, concat_axis=0, tiled=True)  7.01 us
    all_to_all x1, starting transfers between devices, shards(): lax.all_to_all(to_home, 'req', split_axis=0, concat_axis=0, tiled=True)  6.74 us
  transfers between devices with their start and end apart: 7, of which 6 were waited for; matrix products, arithmetic and copies ran while one was open for 7% of the time, Pallas kernels for 0%

profile of v16, /device:TPU:1, one launch (start us, length us, event | category | flops | bytes accessed | tf_op | source)
XLA Modules:
  0.0 232.2 jit_solution(15289084776653671284)
XLA Ops:
  7.2 0.6 slice.88
  7.8 0.8 copy.161
  8.6 0.7 copy.162
  9.3 0.8 scatter.9
  10.1 2.1 multiply_reduce_fusion
  12.8 0.4 maximum_bitcast_fusion
  13.2 2.1 copy.167
  15.3 7.6 %all-to-all-start = ((bf16[16,4,9,1024]{3,1,2,0:T(4,128)(2,1)}), bf16[16,4,9,1024]{3,1,2,0:T(4,128)(2,1)S(1)}, u32[]{:S(2)}, u32[]{:S(2)}) async-start(bf16[16,4,9,1024]{3,1,2,0:T(4,128)(2,1)} %copy.167), calls=%async_computation | async-start | bytes 2359296 | tf_op jit(solution)/shard_map/all_to_all | solution.py:107
  23.0 0.6 gather_fusion.9
  23.7 16.1 %all-to-all-done = bf16[16,4,9,1024]{3,1,2,0:T(4,128)(2,1)S(1)} async-done(((bf16[16,4,9,1024]{3,1,2,0:T(4,128)(2,1)}), bf16[16,4,9,1024]{3,1,2,0:T(4,128)(2,1)S(1)}, u32[]{:S(2)}, u32[]{:S(2)}) %all-to-all-start) | async-done | bytes 1179680 | tf_op jit(solution)/shard_map/all_to_all | solution.py:107
  40.0 0.5 slice.134
  40.5 0.4 copy.190
  40.8 2.4 %slice_reduce_fusion.1 = (s32[64]{0:T(128)S(1)}, s32[64]{0:T(128)S(1)}) fusion(s32[64,4,128]{2,1,0:T(4,128)S(1)} %reshape.310), kind=kLoop, calls=%fused_computation.34 | loop fusion | bytes 1024 | tf_op jit(solution)/shard_map/slice | solution.py:112
  43.3 0.6 gather_fusion.10
  43.9 0.6 gather_fusion.11
  44.6 0.6 fusion.26
  45.4 0.6 gather_fusion.1
  46.0 1.2 broadcast_select_fusion
  47.2 4.1 %all-to-all-start.1 = ((bf16[64,8,1024]{2,1,0:T(8,128)(2,1)}), bf16[64,8,1024]{2,1,0:T(8,128)(2,1)S(1)}, u32[]{:S(2)}, u32[]{:S(2)}) async-start(bf16[64,8,1024]{2,1,0:T(8,128)(2,1)} %broadcast_select_fusion), calls=%async_computation.1 | async-start | bytes 2097152 | tf_op jit(solution)/shard_map/all_to_all | solution.py:114
  51.6 0.7 compare_select_fusion.1
  52.2 0.7 compare_and_fusion.4
  52.9 12.9 %all-to-all-done.1 = bf16[64,8,1024]{2,1,0:T(8,128)(2,1)S(1)} async-done(((bf16[64,8,1024]{2,1,0:T(8,128)(2,1)}), bf16[64,8,1024]{2,1,0:T(8,128)(2,1)S(1)}, u32[]{:S(2)}, u32[]{:S(2)}) %all-to-all-start.1) | async-done | bytes 1048608 | tf_op jit(solution)/shard_map/all_to_all | solution.py:114
  65.9 1.1 gather_fusion.2
  67.0 0.9 broadcast_select_fusion.1
  67.9 67.8 %all-gather.2.cloned.1.call-done.mine_ref = bf16[3584,1024]{1,0:T(8,128)(2,1)} async-done(((bf16[224,1024]{1,0:T(8,128)(2,1)}), bf16[3584,1024]{1,0:T(8,128)(2,1)}) %all-gather.2.cloned.1.call-update) | async-done | bytes 7340048 | tf_op jit(solution)/shard_map/all_gather | solution.py:125
  135.7 0.8 collective-permute-start
  136.5 5.0 %all-to-all-start.2 = ((bf16[16,600,128]{2,1,0:T(8,128)(2,1)}), bf16[16,600,128]{2,1,0:T(8,128)(2,1)S(1)}, u32[]{:S(2)}, u32[]{:S(2)}) async-start(bf16[16,600,128]{2,1,0:T(8,128)(2,1)} %bitcast.92), calls=%async_computation.2 | async-start | bytes 4915200 | tf_op jit(solution)/shard_map/all_to_all | solution.py:90
  141.8 0.8 gather_fusion.7
  142.5 0.8 gather_fusion.8
  143.4 0.6 gather_fusion
  144.8 6.3 %select_reduce_fusion = s32[16,224]{1,0:T(8,128)S(1)} fusion(s32[16,4,128]{2,1,0:T(4,128)S(1)} %broadcast_select_fusion.2, s32[16,4,224]{2,1,0:T(4,128)S(1)} %subtract_add_fusion, pred[16,4,224]{2,1,0:T(4,128)(4,1)S(1)} %fusion.7), kind=kLoop, calls=%fused_computation.13 | loop fusion | flops 7336448 | bytes 118784 | tf_op jit(solution)/shard_map/reduce_sum | solution.py:143
  151.1 0.7 sub.110.ids_ref
  151.8 0.8 gather_fusion.4
  152.7 22.0 %all-to-all-done.2 = bf16[16,600,128]{2,1,0:T(8,128)(2,1)S(1)} async-done(((bf16[16,600,128]{2,1,0:T(8,128)(2,1)}), bf16[16,600,128]{2,1,0:T(8,128)(2,1)S(1)}, u32[]{:S(2)}, u32[]{:S(2)}) %all-to-all-start.2) | async-done | bytes 2457632 | tf_op jit(solution)/shard_map/all_to_all | solution.py:90
  174.7 0.3 copy_bitcast_fusion
  175.0 1.7 constant_dynamic-slice_fusion
  176.7 16.1 %shard_map.86 = f32[4,3584]{1,0:T(4,128)} custom-call(s32[1,3584]{1,0:T(1,128)} %sub.110.ids_ref, bf16[3584,1024]{1,0:T(8,128)(2,1)} %all-gather.2.cloned.1.call-done.mine_ref, bf16[3584,1024]{1,0:T(8,128)(2,1)} %collective-permute-done.other_ref, bf16[600,1024]{1,0:T(8,128)(2,1)} %get-tuple-element.41.emb_mine_ref, ...), custom_call_target="tpu_custom_call" | custom-call | tf_op jit(solution)/shard_map/pallas_call | solution.py:58
  192.8 0.9 reshape.307
  193.8 0.7 gather_fusion.3
  194.5 4.1 %fusion.1 = f32[64,4,128]{2,1,0:T(4,128)} fusion(s32[64,128]{1,0:T(8,128)S(1)} %iota_add_fusion, f32[64,4,224]{2,1,0:T(4,128)S(1)} %gather_fusion.3, pred[64]{0:T(512)(128)(4,1)S(1)} %get-tuple-element.34), kind=kOutput, calls=%fused_computation.16 | convolution fusion | flops 89972736 | bytes 393280 | tf_op jit(solution)/shard_map/dot_general | solution.py:163
  198.5 6.7 %all-to-all-start.3 = ((f32[16,4,4,128]{3,1,2,0:T(4,128)}), f32[16,4,4,128]{3,1,2,0:T(4,128)S(1)}, u32[]{:S(2)}, u32[]{:S(2)}) async-start(f32[16,4,4,128]{3,1,2,0:T(4,128)} %bitcast.24), calls=%async_computation.3 | async-start | bytes 262144 | tf_op jit(solution)/shard_map/all_to_all | solution.py:171
  205.3 0.6 gather_fusion.6
  205.9 0.6 gather_fusion.5
  206.6 5.4 %all-to-all-done.3 = f32[16,4,4,128]{3,1,2,0:T(4,128)S(1)} async-done(((f32[16,4,4,128]{3,1,2,0:T(4,128)}), f32[16,4,4,128]{3,1,2,0:T(4,128)S(1)}, u32[]{:S(2)}, u32[]{:S(2)}) %all-to-all-start.3) | async-done | bytes 131104 | tf_op jit(solution)/shard_map/all_to_all | solution.py:171
  212.2 0.6 broadcast_in_dim.155
  212.8 7.0 %all-to-all-start.4 = ((f32[8,4,4,128]{3,2,1,0:T(4,128)}), f32[8,4,4,128]{3,2,1,0:T(4,128)S(1)}, u32[]{:S(2)}, u32[]{:S(2)}) async-start(f32[8,4,4,128]{3,2,1,0:T(4,128)} %broadcast_in_dim.155), calls=%async_computation.4 | async-start | bytes 131072 | tf_op jit(solution)/shard_map/all_to_all | solution.py:35
  219.8 4.8 %all-to-all-done.4 = f32[8,4,4,128]{3,2,1,0:T(4,128)S(1)} async-done(((f32[8,4,4,128]{3,2,1,0:T(4,128)}), f32[8,4,4,128]{3,2,1,0:T(4,128)S(1)}, u32[]{:S(2)}, u32[]{:S(2)}) %all-to-all-start.4) | async-done | bytes 65568 | tf_op jit(solution)/shard_map/all_to_all | solution.py:35
  224.7 0.7 subtract_select_fusion
  (75 shorter events, 2.8 us)
Async XLA Ops:
  7.2 5.2 %copy-start = (bf16[4,128,2048]{2,1,0:T(8,128)(2,1)S(1)}, bf16[4,128,2048]{2,1,0:T(8,128)(2,1)}, u32[]{:S(2)}) copy-start(bf16[4,128,2048]{2,1,0:T(8,128)(2,1)} %param.15) | copy-start | bytes 6291460
  7.2 5.0 %copy-start.2 = (s32[4,128]{1,0:T(4,128)S(1)}, s32[4,128]{1,0:T(4,128)}, u32[]{:S(2)}) copy-start(s32[4,128]{1,0:T(4,128)} %param.18) | copy-start | bytes 6148
  7.2 5.1 %copy-start.1 = (f32[2048]{0:T(1024)S(1)}, f32[2048]{0:T(1024)}, u32[]{:S(2)}) copy-start(f32[2048]{0:T(1024)} %param.16) | copy-start | bytes 24580
  13.2 9.7 %copy-start.3 = (s32[64]{0:T(128)S(1)}, s32[64]{0:T(128)}, u32[]{:S(2)}) copy-start(s32[64]{0:T(128)} %param.21) | copy-start | bytes 772
  15.3 24.6 %all-to-all-start = ((bf16[16,4,9,1024]{3,1,2,0:T(4,128)(2,1)}), bf16[16,4,9,1024]{3,1,2,0:T(4,128)(2,1)S(1)}, u32[]{:S(2)}, u32[]{:S(2)}) async-start(bf16[16,4,9,1024]{3,1,2,0:T(4,128)(2,1)} %copy.167), calls=%async_computation | async-start | bytes 2359296 | tf_op jit(solution)/shard_map/all_to_all | solution.py:107
  47.2 18.7 %all-to-all-start.1 = ((bf16[64,8,1024]{2,1,0:T(8,128)(2,1)}), bf16[64,8,1024]{2,1,0:T(8,128)(2,1)S(1)}, u32[]{:S(2)}, u32[]{:S(2)}) async-start(bf16[64,8,1024]{2,1,0:T(8,128)(2,1)} %broadcast_select_fusion), calls=%async_computation.1 | async-start | bytes 2097152 | tf_op jit(solution)/shard_map/all_to_all | solution.py:114
  51.3 84.3 %all-gather.2.cloned.1.call-start = ((), (), s32[]{:S(2)}) async-start(), calls=%async_computation.5 | async-start | bytes 7798784 | tf_op jit(solution)/shard_map/all_gather | solution.py:125
  135.7 41.0 %collective-permute-start = (bf16[3584,1024]{1,0:T(8,128)(2,1)}, bf16[3584,1024]{1,0:T(8,128)(2,1)}, u32[]{:S(2)}, u32[]{:S(2)}) collective-permute-start(bf16[3584,1024]{1,0:T(8,128)(2,1)} %all-gather.2.cloned.1.call-done.mine_ref), channel_id=1, source_target_pairs={{0,1},{1,0},{2,3},{3,2},{4,5},{5,4},{6,7},{7,6},{8,9},{9,8},{10,11... | collective-permute-start | bytes 22020104 | tf_op jit(solution)/shard_map/ppermute | solution.py:127
  136.5 38.2 %all-to-all-start.2 = ((bf16[16,600,128]{2,1,0:T(8,128)(2,1)}), bf16[16,600,128]{2,1,0:T(8,128)(2,1)S(1)}, u32[]{:S(2)}, u32[]{:S(2)}) async-start(bf16[16,600,128]{2,1,0:T(8,128)(2,1)} %bitcast.92), calls=%async_computation.2 | async-start | bytes 4915200 | tf_op jit(solution)/shard_map/all_to_all | solution.py:90
  198.5 13.4 %all-to-all-start.3 = ((f32[16,4,4,128]{3,1,2,0:T(4,128)}), f32[16,4,4,128]{3,1,2,0:T(4,128)S(1)}, u32[]{:S(2)}, u32[]{:S(2)}) async-start(f32[16,4,4,128]{3,1,2,0:T(4,128)} %bitcast.24), calls=%async_computation.3 | async-start | bytes 262144 | tf_op jit(solution)/shard_map/all_to_all | solution.py:171
  212.8 11.9 %all-to-all-start.4 = ((f32[8,4,4,128]{3,2,1,0:T(4,128)}), f32[8,4,4,128]{3,2,1,0:T(4,128)S(1)}, u32[]{:S(2)}, u32[]{:S(2)}) async-start(f32[8,4,4,128]{3,2,1,0:T(4,128)} %broadcast_in_dim.155), calls=%async_computation.4 | async-start | bytes 131072 | tf_op jit(solution)/shard_map/all_to_all | solution.py:35
Sparse Core Ops, SparseCore 0:
  68.0 67.5 all-gather.1
